TPU v7x, 256 devices: a whole 4x4x8 slice. The times are simulated.
256 devices in a mesh: space: 128 (over z_lo, y, x, core), op: 2 (over z_hi).
Axes of the slice: x: 4, y: 4, z: 8 (z_hi: 2, z_lo: 4; z = z_hi * 4 + z_lo), core: 2. Of those that a mesh axis runs over, the one named last changes fastest.
Arguments:
- order_field: float32 [16, 1024, 64, 128], P('op', 'space'), may hold values from 0 to 1
- adjoint_next: float32 [16, 1024, 64, 128], P('op', 'space'), may hold values from -6 to 6
- mobility: float32 [16], P('op'), may hold values from 0.5 to 2
- labels: int32 [1024, 128], P('space'), may hold values from 0 to 15
Outputs:
- order_next: float32 [16, 1024, 64, 128], P('op', 'space')
- adjoint_order: float32 [16, 1024, 64, 128], P('op', 'space')
All inputs are finite; a program needn't handle non-finite values.
Results may differ from a plain program's by a relative error of at most 0.00002.
Values sent between devices are 32-bit elements; how exact they have to be, the bound alone decides.
No kernel may reach another device: no remote copies, remote signals or barrier semaphores. Data moves between devices by JAX's collectives and lax.ppermute only.
A program may use at most 128 MiB of HBM per device.

v0:
```python
import jax
import jax.numpy as jnp
from jax import lax
from jax.sharding import PartitionSpec as P


def extended(cells, sides, width):
    for axis, dim in sides:
        count = lax.axis_size(axis)
        head = lax.slice_in_dim(cells, 0, width, axis=dim)
        tail = lax.slice_in_dim(cells, cells.shape[dim] - width, cells.shape[dim], axis=dim)
        cells = jnp.concatenate(
            [
                lax.ppermute(tail, axis, [(i, (i + 1) % count) for i in range(count)]),
                cells,
                lax.ppermute(head, axis, [((i + 1) % count, i) for i in range(count)]),
            ],
            axis=dim,
        )
    return cells


def laplace(padded):
    centre = padded[:, 1:-1]
    beside = padded[:, 2:] + padded[:, :-2]
    beside = beside + jnp.roll(centre, 1, 3) + jnp.roll(centre, -1, 3)
    upper = jnp.concatenate([centre[:, :, 1:], centre[:, :, -1:]], axis=2)
    lower = jnp.concatenate([centre[:, :, :1], centre[:, :, :-1]], axis=2)
    return beside + upper + lower - 6.0 * centre


def local(order_field, adjoint_next, mobility, labels):
    local_count = order_field.shape[0]
    first = lax.axis_index("op") * local_count
    indices = first + jnp.arange(local_count, dtype=jnp.int32)
    foreign = (labels[None, :, None, :] != indices[:, None, None, None]).astype(jnp.float32)
    rates = mobility[:, None, None, None]
    weighted = 0.1 * rates * adjoint_next
    squares, coupled = lax.psum(
        (jnp.sum(order_field * order_field, axis=0), jnp.sum(order_field * weighted, axis=0)), "op"
    )
    padded_state = extended(order_field, (("space", 1),), 1)
    padded_weight = extended(weighted, (("space", 1),), 1)
    potential = (
        (-1.0 + 2.0 * foreign) * order_field
        - 2.0 * order_field**3
        + 3.0 * order_field * squares
        - 0.5 * laplace(padded_state)
    )
    order_next = order_field - 0.1 * rates * potential
    local_part = (-1.0 + 2.0 * foreign - 6.0 * order_field * order_field + 3.0 * squares) * weighted
    adjoint_order = adjoint_next - (
        local_part + 6.0 * order_field * coupled - 0.5 * laplace(padded_weight)
    )
    return (order_next, adjoint_order)


def solution(mesh):
    placed = (P("op", "space", None, None), P("op", "space", None, None), P("op"), P("space", None))
    return jax.shard_map(
        local,
        mesh=mesh,
        in_specs=placed,
        out_specs=(P("op", "space", None, None), P("op", "space", None, None)),
        check_vma=False,
    )
```

profile of v0, /device:TPU:1, one launch (start us, length us, event | category | flops | bytes accessed | tf_op | source)
XLA Modules:
  0.0 109.8 jit_solution(4687173651691273641)
XLA Ops:
  7.2 0.0 all-reduce.3.cloned.1.call-start
  7.2 0.7 broadcast_multiply_fusion.3
  7.9 0.0 copy-start
  7.9 3.8 %multiply_reduce_fusion.1 = (f32[8,64,128]{2,1,0:T(8,128)}, f32[8,64,128]{2,1,0:T(8,128)}, f32[8,8,64,128]{3,2,1,0:T(8,128)S(1)}) fusion(f32[8,8,64,128]{3,2,1,0:T(8,128)} %param.4, f32[8,8,64,128]{3,2,1,0:T(8,128)} %param.5, f32[8]{0:T(128)S(1)} %broadcast_multiply_fusion.3), kind=kLoop, calls=%fused_computation.33 | loop fusion | flops 2490368 | bytes 6815776 | tf_op jit(solution)/shard_map/reduce_sum | solution.py:40
  11.7 0.0 copy-start.1
  11.7 1.3 %copy-done.1 = f32[8,8,64,128]{3,2,1,0:T(8,128)} copy-done((f32[8,8,64,128]{3,2,1,0:T(8,128)}, f32[8,8,64,128]{3,2,1,0:T(8,128)S(1)}, u32[]{:S(2)}) %copy-start.1) | copy-done | bytes 2097176
  13.0 0.8 fusion.29
  13.7 3.2 %collective-permute-start.2 = (f32[8,1,64,128]{3,2,1,0:T(8,128)}, f32[8,1,64,128]{3,2,1,0:T(8,128)S(1)}, u32[]{:S(2)}, u32[]{:S(2)}) collective-permute-start(f32[8,1,64,128]{3,2,1,0:T(8,128)} %get-tuple-element.15), channel_id=1, source_target_pairs={{2,0},{4,2},{6,4},{8,6},{10,8},{12,10},{14,12},{16,14},{18,16},{20... | collective-permute-start | bytes 786440 | tf_op jit(solution)/shard_map/ppermute | solution.py:16
  17.0 0.0 collective-permute-start.3
  17.0 0.0 copy-done
  17.0 0.9 fusion.34
  17.9 7.0 %collective-permute-start = (f32[8,1,64,128]{3,2,1,0:T(8,128)}, f32[8,1,64,128]{3,2,1,0:T(8,128)S(1)}, u32[]{:S(2)}, u32[]{:S(2)}) collective-permute-start(f32[8,1,64,128]{3,2,1,0:T(8,128)} %get-tuple-element.25), channel_id=1, source_target_pairs={{2,0},{4,2},{6,4},{8,6},{10,8},{12,10},{14,12},{16,14},{18,16},{20... | collective-permute-start | bytes 786440 | tf_op jit(solution)/shard_map/ppermute | solution.py:16
  24.8 0.0 collective-permute-start.1
  24.8 0.0 all-reduce.3.cloned.1.call-update
  24.9 0.0 copy-start.2
  24.9 5.2 %fusion.26 = (f32[8,8,63,128]{3,2,1,0:T(8,128)}, f32[8,8,63,128]{3,2,1,0:T(8,128)}) fusion(f32[8,8,64,128]{3,2,1,0:T(8,128)} %copy-done.1), kind=kLoop, calls=%fused_computation.41 | loop fusion | bytes 8257536 | tf_op jit(solution)/shard_map/slice | solution.py:28
  30.1 0.0 copy-done.2
  30.1 2.8 %fusion.27 = (f32[8,8,64,127]{3,2,1,0:T(8,128)}, f32[8,8,64,127]{3,2,1,0:T(8,128)}) fusion(f32[8,8,64,128]{3,2,1,0:T(8,128)S(1)} %copy-done.2), kind=kLoop, calls=%fused_computation.42 | loop fusion | bytes 8323072 | tf_op jit(solution)/shard_map/jit(_roll_static)/slice | solution.py:26
  32.9 2.8 %fusion.28 = (f32[8,8,64,1]{3,2,1,0:T(8,128)}, f32[8,8,64,1]{3,2,1,0:T(8,128)}) fusion(f32[8,8,64,128]{3,2,1,0:T(8,128)S(1)} %copy-done.2), kind=kLoop, calls=%fused_computation.43 | loop fusion | bytes 65536 | tf_op jit(solution)/shard_map/jit(_roll_static)/slice | solution.py:26
  35.7 2.5 %fusion.31 = (f32[8,8,63,128]{3,2,1,0:T(8,128)}, f32[8,8,63,128]{3,2,1,0:T(8,128)}) fusion(f32[8,8,64,128]{3,2,1,0:T(8,128)S(1)} %copy-done), kind=kLoop, calls=%fused_computation.46 | loop fusion | bytes 8257536 | tf_op jit(solution)/shard_map/slice | solution.py:28
  38.2 2.9 %fusion.32 = (f32[8,8,64,127]{3,2,1,0:T(8,128)}, f32[8,8,64,127]{3,2,1,0:T(8,128)}) fusion(f32[8,8,64,128]{3,2,1,0:T(8,128)S(1)} %copy-done), kind=kLoop, calls=%fused_computation.47 | loop fusion | bytes 8323072 | tf_op jit(solution)/shard_map/jit(_roll_static)/slice | solution.py:26
  41.0 0.0 copy-start.11
  41.0 2.9 %fusion.33 = (f32[8,8,64,1]{3,2,1,0:T(8,128)}, f32[8,8,64,1]{3,2,1,0:T(8,128)}) fusion(f32[8,8,64,128]{3,2,1,0:T(8,128)S(1)} %copy-done), kind=kLoop, calls=%fused_computation.48 | loop fusion | bytes 65536 | tf_op jit(solution)/shard_map/jit(_roll_static)/slice | solution.py:26
  43.9 0.7 fusion.30
  44.6 0.0 copy-done.11
  44.6 0.1 select_add_fusion
  44.7 43.0 %all-reduce.3.cloned.1.call-done = (f32[8,64,128]{2,1,0:T(8,128)}, f32[8,64,128]{2,1,0:T(8,128)}) async-done(((f32[8,64,128]{2,1,0:T(8,128)}, f32[8,64,128]{2,1,0:T(8,128)}), (f32[8,64,128]{2,1,0:T(8,128)}, f32[8,64,128]{2,1,0:T(8,128)})) %all-reduce.3.cloned.1.call-update) | async-done | bytes 524304 | tf_op jit(solution)/shard_map/psum | solution.py:39
  87.6 1.1 broadcast_multiply_fusion.1
  88.7 0.0 collective-permute-done
  88.7 0.0 collective-permute-done.1
  88.7 0.0 copy-start.3
  88.7 0.0 copy-start.4
  88.7 0.0 copy-start.5
  88.7 0.0 copy-start.6
  88.7 0.0 copy-start.7
  88.8 0.0 copy-start.8
  88.8 0.0 copy-start.9
  88.8 0.0 copy-start.10
  88.8 6.9 %fusion.5 = f32[8,8,64,128]{3,2,1,0:T(8,128)} fusion(f32[8,8,64,128]{3,2,1,0:T(8,128)S(1)} %copy-done, f32[8,1,64,128]{3,2,1,0:T(8,128)S(1)} %collective-permute-done.1, f32[8,1,64,128]{3,2,1,0:T(8,128)S(1)} %collective-permute-done, f32[8,8,64,127]{3,2,1,0:T(8,128)} %get-tuple-element.22, f32[8,8,64,1]{3,2,1,0:T(8,128)} %get-tuple-element.24, ...), kind=kLoop, calls=%fused_computation.9 | loop fusion | flops 12582912 | bytes 13402144 | tf_op jit(solution)/shard_map/sub | solution.py:50
  95.7 0.0 collective-permute-done.2
  95.7 0.0 collective-permute-done.3
  95.7 0.0 copy-done.3
  95.7 0.0 copy-done.4
  95.7 0.0 copy-done.5
  95.7 0.9 copy-done.6
  96.6 0.6 copy-done.7
  97.2 0.6 copy-done.8
  97.8 0.6 copy-done.9
  98.4 0.6 copy-done.10
  99.0 4.0 %fusion.12 = f32[8,8,64,128]{3,2,1,0:T(8,128)} fusion(f32[8,8,64,128]{3,2,1,0:T(8,128)S(1)} %copy-done.4, f32[8,8,64,128]{3,2,1,0:T(8,128)S(1)} %copy-done.3, f32[8,8,64,128]{3,2,1,0:T(8,128)S(1)} %copy-done, f32[8,1,64,128]{3,2,1,0:T(8,128)S(1)} %collective-permute-done.3, f32[8,1,64,128]{3,2,1,0:T(8,128)S(1)} %collective-permute-done.2, ...), kind=kLoop, calls=%fused_computation.16 | loop fusion | flops 12058624 | bytes 17858560 | tf_op jit(solution)/shard_map/sub | solution.py:52
  (2 shorter events, 0.1 us)
Async XLA Ops:
  7.2 80.4 %all-reduce.3.cloned.1.call-start = ((), (), s32[]{:S(2)}) async-start(), calls=%async_computation | async-start | bytes 1048576 | tf_op jit(solution)/shard_map/psum | solution.py:39
  7.9 9.1 %copy-start = (f32[8,8,64,128]{3,2,1,0:T(8,128)S(1)}, f32[8,8,64,128]{3,2,1,0:T(8,128)}, u32[]{:S(2)}) copy-start(f32[8,8,64,128]{3,2,1,0:T(8,128)} %param.4) | copy-start | bytes 6291460
  11.7 1.3 %copy-start.1 = (f32[8,8,64,128]{3,2,1,0:T(8,128)}, f32[8,8,64,128]{3,2,1,0:T(8,128)S(1)}, u32[]{:S(2)}) copy-start(f32[8,8,64,128]{3,2,1,0:T(8,128)S(1)} %get-tuple-element.6) | copy-start | bytes 6291460
  13.7 81.9 %collective-permute-start.2 = (f32[8,1,64,128]{3,2,1,0:T(8,128)}, f32[8,1,64,128]{3,2,1,0:T(8,128)S(1)}, u32[]{:S(2)}, u32[]{:S(2)}) collective-permute-start(f32[8,1,64,128]{3,2,1,0:T(8,128)} %get-tuple-element.15), channel_id=1, source_target_pairs={{2,0},{4,2},{6,4},{8,6},{10,8},{12,10},{14,12},{16,14},{18,16},{20... | collective-permute-start | bytes 786440 | tf_op jit(solution)/shard_map/ppermute | solution.py:16
  17.0 78.7 %collective-permute-start.3 = (f32[8,1,64,128]{3,2,1,0:T(8,128)S(1)}, f32[8,1,64,128]{3,2,1,0:T(8,128)S(1)}, u32[]{:S(2)}, u32[]{:S(2)}) collective-permute-start(f32[8,1,64,128]{3,2,1,0:T(8,128)S(1)} %get-tuple-element.16), channel_id=1, source_target_pairs={{0,2},{2,4},{4,6},{6,8},{8,10},{10,12},{12,14},{14,16},{16,18},{18... | collective-permute-start | bytes 786440 | tf_op jit(solution)/shard_map/ppermute | solution.py:14
  17.9 70.8 %collective-permute-start = (f32[8,1,64,128]{3,2,1,0:T(8,128)}, f32[8,1,64,128]{3,2,1,0:T(8,128)S(1)}, u32[]{:S(2)}, u32[]{:S(2)}) collective-permute-start(f32[8,1,64,128]{3,2,1,0:T(8,128)} %get-tuple-element.25), channel_id=1, source_target_pairs={{2,0},{4,2},{6,4},{8,6},{10,8},{12,10},{14,12},{16,14},{18,16},{20... | collective-permute-start | bytes 786440 | tf_op jit(solution)/shard_map/ppermute | solution.py:16
  24.8 63.9 %collective-permute-start.1 = (f32[8,1,64,128]{3,2,1,0:T(8,128)}, f32[8,1,64,128]{3,2,1,0:T(8,128)S(1)}, u32[]{:S(2)}, u32[]{:S(2)}) collective-permute-start(f32[8,1,64,128]{3,2,1,0:T(8,128)} %get-tuple-element.26), channel_id=1, source_target_pairs={{0,2},{2,4},{4,6},{6,8},{8,10},{10,12},{12,14},{14,16},{16,18},{18... | collective-permute-start | bytes 786440 | tf_op jit(solution)/shard_map/ppermute | solution.py:14
  24.9 5.2 %copy-start.2 = (f32[8,8,64,128]{3,2,1,0:T(8,128)S(1)}, f32[8,8,64,128]{3,2,1,0:T(8,128)}, u32[]{:S(2)}) copy-start(f32[8,8,64,128]{3,2,1,0:T(8,128)} %copy-done.1) | copy-start | bytes 6291460
  41.0 3.5 %copy-start.11 = (s32[8,128]{1,0:T(8,128)S(1)}, s32[8,128]{1,0:T(8,128)}, u32[]{:S(2)}) copy-start(s32[8,128]{1,0:T(8,128)} %param.7) | copy-start | bytes 12292
  88.7 7.0 %copy-start.3 = (f32[8,8,64,128]{3,2,1,0:T(8,128)S(1)}, f32[8,8,64,128]{3,2,1,0:T(8,128)}, u32[]{:S(2)}) copy-start(f32[8,8,64,128]{3,2,1,0:T(8,128)} %copy-done.1) | copy-start | bytes 6291460
  88.7 7.0 %copy-start.4 = (f32[8,8,64,128]{3,2,1,0:T(8,128)S(1)}, f32[8,8,64,128]{3,2,1,0:T(8,128)}, u32[]{:S(2)}) copy-start(f32[8,8,64,128]{3,2,1,0:T(8,128)} %param.5) | copy-start | bytes 6291460
  88.7 7.0 %copy-start.5 = (f32[8,8,63,128]{3,2,1,0:T(8,128)S(1)}, f32[8,8,63,128]{3,2,1,0:T(8,128)}, u32[]{:S(2)}) copy-start(f32[8,8,63,128]{3,2,1,0:T(8,128)} %get-tuple-element.9) | copy-start | bytes 6193156
  88.7 7.9 %copy-start.6 = (f32[8,8,63,128]{3,2,1,0:T(8,128)S(1)}, f32[8,8,63,128]{3,2,1,0:T(8,128)}, u32[]{:S(2)}) copy-start(f32[8,8,63,128]{3,2,1,0:T(8,128)} %get-tuple-element.10) | copy-start | bytes 6193156
  88.7 8.5 %copy-start.7 = (f32[8,8,64,127]{3,2,1,0:T(8,128)S(1)}, f32[8,8,64,127]{3,2,1,0:T(8,128)}, u32[]{:S(2)}) copy-start(f32[8,8,64,127]{3,2,1,0:T(8,128)} %get-tuple-element.11) | copy-start | bytes 6242308
  88.8 9.0 %copy-start.8 = (f32[8,8,64,127]{3,2,1,0:T(8,128)S(1)}, f32[8,8,64,127]{3,2,1,0:T(8,128)}, u32[]{:S(2)}) copy-start(f32[8,8,64,127]{3,2,1,0:T(8,128)} %get-tuple-element.12) | copy-start | bytes 6242308
  88.8 9.6 %copy-start.9 = (f32[8,8,64,1]{3,2,1,0:T(8,128)S(1)}, f32[8,8,64,1]{3,2,1,0:T(8,128)}, u32[]{:S(2)}) copy-start(f32[8,8,64,1]{3,2,1,0:T(8,128)} %get-tuple-element.13) | copy-start | bytes 49156
  88.8 10.2 %copy-start.10 = (f32[8,8,64,1]{3,2,1,0:T(8,128)S(1)}, f32[8,8,64,1]{3,2,1,0:T(8,128)}, u32[]{:S(2)}) copy-start(f32[8,8,64,1]{3,2,1,0:T(8,128)} %get-tuple-element.14) | copy-start | bytes 49156
Sparse Core Ops, SparseCore 0:
  25.0 62.5 all-reduce.2
where the time goes:
time: 110 us
  waiting for transfers between devices  43 us (39%)
  local copies, waits for them, and re-layouts  26 us (24%)
  other arithmetic  16.5 us (15%)
  between operations  14.2 us (13%)
  starting transfers between devices  10.3 us (9%)
    psum x1, waiting for transfers between devices, local(): lax.psum((jnp.sum(order_field * order_field, axis=0), jnp.sum(order_field...  43 us
    slice x4, local copies, waits for them, and re-layouts, laplace(): beside = beside + jnp.roll(centre, 1, 3) + jnp.roll(centre, -1, 3)  11.3 us
    ppermute x2, starting transfers between devices, extended(): lax.ppermute(head, axis, [((i + 1) % count, i) for i in range(count)])  10.2 us
    slice x4, local copies, waits for them, and re-layouts, laplace(): lower = jnp.concatenate([centre[:, :, :1], centre[:, :, :-1]], axis=2)  8.41 us
    sub x1, other arithmetic, local(): order_next = order_field - 0.1 * rates * potential  6.88 us
    unnamed x24, local copies, waits for them, and re-layouts  4.67 us
    sub x1, other arithmetic, local(): adjoint_next - (local_part + 6.0 * order_field * coupled - 0.5 * laplace(...  4 us
    reduce_sum x1, other arithmetic, local(): jnp.sum(order_field * weighted, axis=0)  3.78 us
  transfers between devices with their start and end apart: 5, of which 1 were waited for; matrix products, arithmetic and copies ran while one was open for 26% of the time, Pallas kernels for 0%

commit v1 on v0

--- a/solution.py
+++ b/solution.py
@@ -36,9 +36,11 @@
     foreign = (labels[None, :, None, :] != indices[:, None, None, None]).astype(jnp.float32)
     rates = mobility[:, None, None, None]
     weighted = 0.1 * rates * adjoint_next
-    squares, coupled = lax.psum(
-        (jnp.sum(order_field * order_field, axis=0), jnp.sum(order_field * weighted, axis=0)), "op"
-    )
+    partial = jnp.stack([jnp.sum(order_field * order_field, axis=0), jnp.sum(order_field * weighted, axis=0)])
+    count = lax.axis_size("op")
+    other = lax.ppermute(partial, "op", [(i, (i + 1) % count) for i in range(count)])
+    total = partial + other
+    squares, coupled = total[0], total[1]
     padded_state = extended(order_field, (("space", 1),), 1)
     padded_weight = extended(weighted, (("space", 1),), 1)
     potential = (

time: 110 us -> 57.1 us (0.52)
  the two profiles are of different devices: /device:TPU:1 before, /device:TPU:64 now
where the time goes in v1:
time: 57.1 us; the launch traced here: 56.5 us
  local copies, waits for them, and re-layouts  17.9 us (31%)
  starting transfers between devices  16.2 us (28%)
  other arithmetic  14 us (25%)
  waiting for transfers between devices  7.55 us (13%)
  between operations  0.86 us (2%)
    ppermute x2, starting transfers between devices, extended(): lax.ppermute(head, axis, [((i + 1) % count, i) for i in range(count)])  10.8 us
    slice x4, local copies, waits for them, and re-layouts, laplace(): beside = beside + jnp.roll(centre, 1, 3) + jnp.roll(centre, -1, 3)  9.15 us
    ppermute x1, starting transfers between devices, local(): lax.ppermute(partial, 'op', [(i, (i + 1) % count) for i in range(count)])  5.39 us
    sub x1, other arithmetic, local(): adjoint_next - (local_part + 6.0 * order_field * coupled - 0.5 * laplace(...  4.9 us
    ppermute x2, waiting for transfers between devices, extended(): lax.ppermute(tail, axis, [(i, (i + 1) % count) for i in range(count)])  4.84 us
    slice x4, local copies, waits for them, and re-layouts, laplace(): lower = jnp.concatenate([centre[:, :, :1], centre[:, :, :-1]], axis=2)  4.8 us
    sub x1, other arithmetic, local(): order_next = order_field - 0.1 * rates * potential  4.54 us
    reduce_sum x1, other arithmetic, local(): jnp.sum(order_field * order_field, axis=0)  2.85 us
  transfers between devices with their start and end apart: 5, of which 2 were waited for; matrix products, arithmetic and copies ran while one was open for 36% of the time, Pallas kernels for 0%

profile of v1, /device:TPU:64, one launch (start us, length us, event | category | flops | bytes accessed | tf_op | source)
XLA Modules:
  0.0 56.5 jit_solution(2928805811672334180)
XLA Ops:
  0.6 0.7 %broadcast_multiply_fusion.1 = f32[8]{0:T(128)S(1)} fusion(f32[8]{0:T(128)} %param.6), kind=kLoop, calls=%fused_computation.42 | loop fusion | flops 8 | bytes 64 | tf_op jit(solution)/shard_map/mul | solution.py:52
  1.3 2.8 %multiply_reduce_fusion = (f32[8,64,128]{2,1,0:T(8,128)S(1)}, f32[8,64,128]{2,1,0:T(8,128)S(1)}, f32[8,8,64,128]{3,2,1,0:T(8,128)S(1)}) fusion(f32[8,8,64,128]{3,2,1,0:T(8,128)} %param.4, f32[8,8,64,128]{3,2,1,0:T(8,128)} %param.5, f32[8]{0:T(128)S(1)} %broadcast_multiply_fusion.1), kind=kLoop, calls=%fused_computation.2 | loop fusion | flops 2490368 | bytes 6815776 | tf_op jit(solution)/shard_map/reduce_sum | solution.py:39
  4.1 0.0 copy-start.1
  4.2 0.0 copy-start
  4.2 0.8 %pad_maximum_fusion.4 = f32[2,8,64,128]{3,2,1,0:T(8,128)} fusion(f32[1,8,64,128]{3,2,1,0:T(8,128)S(1)} %bitcast.8, f32[1,8,64,128]{3,2,1,0:T(8,128)S(1)} %bitcast.6), kind=kLoop, calls=%fused_computation.35 | loop fusion | flops 131072 | bytes 1048576 | tf_op jit(solution)/shard_map/stack | solution.py:39
  5.0 5.4 %collective-permute-start = (f32[2,8,64,128]{3,2,1,0:T(8,128)}, f32[2,8,64,128]{3,2,1,0:T(8,128)S(1)}, u32[]{:S(2)}, u32[]{:S(2)}) collective-permute-start(f32[2,8,64,128]{3,2,1,0:T(8,128)} %pad_maximum_fusion.4), channel_id=1, source_target_pairs={{0,1},{1,0},{2,3},{3,2},{4,5},{5,4},{6,7},{7,6},{8,9},{9,8},{10,11... | collective-permute-start | bytes 1572872 | tf_op jit(solution)/shard_map/ppermute | solution.py:41
  10.4 0.8 %fusion.32 = (f32[8,1,64,128]{3,2,1,0:T(8,128)}, f32[8,1,64,128]{3,2,1,0:T(8,128)}) fusion(f32[8,8,64,128]{3,2,1,0:T(8,128)S(1)} %get-tuple-element.4), kind=kLoop, calls=%fused_computation.48 | loop fusion | bytes 1048576 | tf_op jit(solution)/shard_map/slice | solution.py:10
  11.2 4.8 %collective-permute-start.3 = (f32[8,1,64,128]{3,2,1,0:T(8,128)}, f32[8,1,64,128]{3,2,1,0:T(8,128)S(1)}, u32[]{:S(2)}, u32[]{:S(2)}) collective-permute-start(f32[8,1,64,128]{3,2,1,0:T(8,128)} %get-tuple-element.13), channel_id=1, source_target_pairs={{2,0},{4,2},{6,4},{8,6},{10,8},{12,10},{14,12},{16,14},{18,16},{20... | collective-permute-start | bytes 786440 | tf_op jit(solution)/shard_map/ppermute | solution.py:16
  16.1 0.0 collective-permute-start.4
  16.1 0.0 copy-done
  16.1 0.8 %fusion.37 = (f32[8,1,64,128]{3,2,1,0:T(8,128)}, f32[8,1,64,128]{3,2,1,0:T(8,128)}) fusion(f32[8,8,64,128]{3,2,1,0:T(8,128)S(1)} %copy-done), kind=kLoop, calls=%fused_computation.53 | loop fusion | bytes 1048576 | tf_op jit(solution)/shard_map/slice | solution.py:10
  16.9 6.0 %collective-permute-start.1 = (f32[8,1,64,128]{3,2,1,0:T(8,128)}, f32[8,1,64,128]{3,2,1,0:T(8,128)}, u32[]{:S(2)}, u32[]{:S(2)}) collective-permute-start(f32[8,1,64,128]{3,2,1,0:T(8,128)} %get-tuple-element.23), channel_id=1, source_target_pairs={{2,0},{4,2},{6,4},{8,6},{10,8},{12,10},{14,12},{16,14},{18,16},{20... | collective-permute-start | bytes 786440 | tf_op jit(solution)/shard_map/ppermute | solution.py:16
  22.9 0.0 collective-permute-start.2
  22.9 2.8 %fusion.30 = (f32[8,8,64,127]{3,2,1,0:T(8,128)}, f32[8,8,64,127]{3,2,1,0:T(8,128)}) fusion(f32[8,8,64,128]{3,2,1,0:T(8,128)S(1)} %get-tuple-element.4), kind=kLoop, calls=%fused_computation.46 | loop fusion | bytes 8323072 | tf_op jit(solution)/shard_map/jit(_roll_static)/slice | solution.py:26
  25.7 2.8 %fusion.31 = (f32[8,8,64,1]{3,2,1,0:T(8,128)}, f32[8,8,64,1]{3,2,1,0:T(8,128)}) fusion(f32[8,8,64,128]{3,2,1,0:T(8,128)S(1)} %get-tuple-element.4), kind=kLoop, calls=%fused_computation.47 | loop fusion | bytes 65536 | tf_op jit(solution)/shard_map/jit(_roll_static)/slice | solution.py:26
  28.4 2.4 %fusion.29 = (f32[8,8,63,128]{3,2,1,0:T(8,128)}, f32[8,8,63,128]{3,2,1,0:T(8,128)}) fusion(f32[8,8,64,128]{3,2,1,0:T(8,128)S(1)} %get-tuple-element.4), kind=kLoop, calls=%fused_computation.45 | loop fusion | bytes 8257536 | tf_op jit(solution)/shard_map/slice | solution.py:28
  30.8 0.0 copy-done.1
  30.9 2.3 %fusion.34 = (f32[8,8,63,128]{3,2,1,0:T(8,128)}, f32[8,8,63,128]{3,2,1,0:T(8,128)}) fusion(f32[8,8,64,128]{3,2,1,0:T(8,128)S(1)} %copy-done), kind=kLoop, calls=%fused_computation.50 | loop fusion | bytes 8257536 | tf_op jit(solution)/shard_map/slice | solution.py:28
  33.2 0.0 copy-start.14
  33.2 2.8 %fusion.35 = (f32[8,8,64,127]{3,2,1,0:T(8,128)}, f32[8,8,64,127]{3,2,1,0:T(8,128)}) fusion(f32[8,8,64,128]{3,2,1,0:T(8,128)S(1)} %copy-done), kind=kLoop, calls=%fused_computation.51 | loop fusion | bytes 8323072 | tf_op jit(solution)/shard_map/jit(_roll_static)/slice | solution.py:26
  36.0 0.0 copy-done.14
  36.0 0.1 select_add_fusion
  36.1 0.0 copy-start.4
  36.1 0.0 copy-start.5
  36.1 0.0 copy-start.6
  36.2 0.8 %fusion.36 = (f32[8,8,64,1]{3,2,1,0:T(8,128)S(1)}, f32[8,8,64,1]{3,2,1,0:T(8,128)S(1)}) fusion(f32[8,8,64,128]{3,2,1,0:T(8,128)S(1)} %copy-done), kind=kLoop, calls=%fused_computation.52 | loop fusion | bytes 65536 | tf_op jit(solution)/shard_map/jit(_roll_static)/slice | solution.py:26
  37.0 0.0 copy-start.3
  37.0 2.7 %collective-permute-done = f32[2,8,64,128]{3,2,1,0:T(8,128)S(1)} collective-permute-done((f32[2,8,64,128]{3,2,1,0:T(8,128)}, f32[2,8,64,128]{3,2,1,0:T(8,128)S(1)}, u32[]{:S(2)}, u32[]{:S(2)}) %collective-permute-start) | collective-permute-done | bytes 524320 | tf_op jit(solution)/shard_map/ppermute | solution.py:41
  39.7 0.1 fusion.27
  39.8 0.0 collective-permute-done.1
  39.8 4.8 %collective-permute-done.2 = f32[8,1,64,128]{3,2,1,0:T(8,128)} collective-permute-done((f32[8,1,64,128]{3,2,1,0:T(8,128)}, f32[8,1,64,128]{3,2,1,0:T(8,128)}, u32[]{:S(2)}, u32[]{:S(2)}) %collective-permute-start.2) | collective-permute-done | bytes 262176 | tf_op jit(solution)/shard_map/ppermute | solution.py:14
  44.7 0.0 copy-done.4
  44.7 0.0 copy-done.5
  44.7 0.0 copy-done.6
  44.7 0.0 copy-done.3
  44.7 0.0 copy-start.2
  44.7 0.0 copy-start.7
  44.7 0.0 copy-start.8
  44.7 0.0 copy-start.9
  44.7 0.0 copy-start.10
  44.7 0.0 copy-start.11
  44.7 0.0 copy-start.12
  44.8 0.0 copy-start.13
  44.8 4.5 %fusion.5 = f32[8,8,64,128]{3,2,1,0:T(8,128)} fusion(f32[8,8,64,128]{3,2,1,0:T(8,128)S(1)} %copy-done, f32[8,1,64,128]{3,2,1,0:T(8,128)} %collective-permute-done.2, f32[8,1,64,128]{3,2,1,0:T(8,128)} %collective-permute-done.1, f32[8,8,64,127]{3,2,1,0:T(8,128)S(1)} %copy-done.6, f32[8,8,64,1]{3,2,1,0:T(8,128)S(1)} %get-tuple-element.22, ...), kind=kLoop, calls=%fused_computation.9 | loop fusion | flops 12582912 | bytes 13402144 | tf_op jit(solution)/shard_map/sub | solution.py:52
  49.3 0.0 collective-permute-done.3
  49.3 0.0 collective-permute-done.4
  49.3 0.0 copy-done.2
  49.3 0.0 copy-done.7
  49.3 0.0 copy-done.8
  49.3 0.0 copy-done.9
  49.4 0.1 copy-done.10
  49.4 0.9 %copy-done.11 = f32[8,8,64,1]{3,2,1,0:T(8,128)S(1)} copy-done((f32[8,8,64,1]{3,2,1,0:T(8,128)S(1)}, f32[8,8,64,1]{3,2,1,0:T(8,128)}, u32[]{:S(2)}) %copy-start.11) | copy-done | bytes 16408
  50.4 0.6 %copy-done.12 = f32[8,8,63,128]{3,2,1,0:T(8,128)S(1)} copy-done((f32[8,8,63,128]{3,2,1,0:T(8,128)S(1)}, f32[8,8,63,128]{3,2,1,0:T(8,128)}, u32[]{:S(2)}) %copy-start.12) | copy-done | bytes 2064408
  51.0 0.6 %copy-done.13 = f32[8,8,63,128]{3,2,1,0:T(8,128)S(1)} copy-done((f32[8,8,63,128]{3,2,1,0:T(8,128)S(1)}, f32[8,8,63,128]{3,2,1,0:T(8,128)}, u32[]{:S(2)}) %copy-start.13) | copy-done | bytes 2064408
  51.6 4.9 %fusion.12 = f32[8,8,64,128]{3,2,1,0:T(8,128)} fusion(f32[8,8,64,128]{3,2,1,0:T(8,128)S(1)} %copy-done.7, f32[8,8,64,128]{3,2,1,0:T(8,128)S(1)} %copy-done.2, f32[8,8,64,128]{3,2,1,0:T(8,128)S(1)} %copy-done, f32[8,1,64,128]{3,2,1,0:T(8,128)} %collective-permute-done.4, f32[8,1,64,128]{3,2,1,0:T(8,128)S(1)} %collective-permute-done.3, ...), kind=kLoop, calls=%fused_computation.16 | loop fusion | flops 12058624 | bytes 17858560 | tf_op jit(solution)/shard_map/sub | solution.py:54
  (4 shorter events, 0.1 us)
Async XLA Ops:
  4.1 26.7 %copy-start.1 = (f32[8,8,64,128]{3,2,1,0:T(8,128)}, f32[8,8,64,128]{3,2,1,0:T(8,128)S(1)}, u32[]{:S(2)}) copy-start(f32[8,8,64,128]{3,2,1,0:T(8,128)S(1)} %get-tuple-element.4) | copy-start | bytes 6291460
  4.2 11.9 %copy-start = (f32[8,8,64,128]{3,2,1,0:T(8,128)S(1)}, f32[8,8,64,128]{3,2,1,0:T(8,128)}, u32[]{:S(2)}) copy-start(f32[8,8,64,128]{3,2,1,0:T(8,128)} %param.4) | copy-start | bytes 6291460
  5.0 34.7 %collective-permute-start = (f32[2,8,64,128]{3,2,1,0:T(8,128)}, f32[2,8,64,128]{3,2,1,0:T(8,128)S(1)}, u32[]{:S(2)}, u32[]{:S(2)}) collective-permute-start(f32[2,8,64,128]{3,2,1,0:T(8,128)} %pad_maximum_fusion.4), channel_id=1, source_target_pairs={{0,1},{1,0},{2,3},{3,2},{4,5},{5,4},{6,7},{7,6},{8,9},{9,8},{10,11... | collective-permute-start | bytes 1572872 | tf_op jit(solution)/shard_map/ppermute | solution.py:41
  11.2 38.1 %collective-permute-start.3 = (f32[8,1,64,128]{3,2,1,0:T(8,128)}, f32[8,1,64,128]{3,2,1,0:T(8,128)S(1)}, u32[]{:S(2)}, u32[]{:S(2)}) collective-permute-start(f32[8,1,64,128]{3,2,1,0:T(8,128)} %get-tuple-element.13), channel_id=1, source_target_pairs={{2,0},{4,2},{6,4},{8,6},{10,8},{12,10},{14,12},{16,14},{18,16},{20... | collective-permute-start | bytes 786440 | tf_op jit(solution)/shard_map/ppermute | solution.py:16
  16.1 33.3 %collective-permute-start.4 = (f32[8,1,64,128]{3,2,1,0:T(8,128)}, f32[8,1,64,128]{3,2,1,0:T(8,128)}, u32[]{:S(2)}, u32[]{:S(2)}) collective-permute-start(f32[8,1,64,128]{3,2,1,0:T(8,128)} %get-tuple-element.14), channel_id=1, source_target_pairs={{0,2},{2,4},{4,6},{6,8},{8,10},{10,12},{12,14},{14,16},{16,18},{18... | collective-permute-start | bytes 786440 | tf_op jit(solution)/shard_map/ppermute | solution.py:14
  16.9 22.9 %collective-permute-start.1 = (f32[8,1,64,128]{3,2,1,0:T(8,128)}, f32[8,1,64,128]{3,2,1,0:T(8,128)}, u32[]{:S(2)}, u32[]{:S(2)}) collective-permute-start(f32[8,1,64,128]{3,2,1,0:T(8,128)} %get-tuple-element.23), channel_id=1, source_target_pairs={{2,0},{4,2},{6,4},{8,6},{10,8},{12,10},{14,12},{16,14},{18,16},{20... | collective-permute-start | bytes 786440 | tf_op jit(solution)/shard_map/ppermute | solution.py:16
  22.9 21.8 %collective-permute-start.2 = (f32[8,1,64,128]{3,2,1,0:T(8,128)}, f32[8,1,64,128]{3,2,1,0:T(8,128)}, u32[]{:S(2)}, u32[]{:S(2)}) collective-permute-start(f32[8,1,64,128]{3,2,1,0:T(8,128)} %get-tuple-element.24), channel_id=1, source_target_pairs={{0,2},{2,4},{4,6},{6,8},{8,10},{10,12},{12,14},{14,16},{16,18},{18... | collective-permute-start | bytes 786440 | tf_op jit(solution)/shard_map/ppermute | solution.py:14
  33.2 2.8 %copy-start.14 = (s32[8,128]{1,0:T(8,128)S(1)}, s32[8,128]{1,0:T(8,128)}, u32[]{:S(2)}) copy-start(s32[8,128]{1,0:T(8,128)} %param.7) | copy-start | bytes 12292
  36.1 8.5 %copy-start.4 = (f32[8,8,63,128]{3,2,1,0:T(8,128)S(1)}, f32[8,8,63,128]{3,2,1,0:T(8,128)}, u32[]{:S(2)}) copy-start(f32[8,8,63,128]{3,2,1,0:T(8,128)} %get-tuple-element.18) | copy-start | bytes 6193156
  36.1 8.5 %copy-start.5 = (f32[8,8,64,127]{3,2,1,0:T(8,128)S(1)}, f32[8,8,64,127]{3,2,1,0:T(8,128)}, u32[]{:S(2)}) copy-start(f32[8,8,64,127]{3,2,1,0:T(8,128)} %get-tuple-element.19) | copy-start | bytes 6242308
  36.1 8.5 %copy-start.6 = (f32[8,8,64,127]{3,2,1,0:T(8,128)S(1)}, f32[8,8,64,127]{3,2,1,0:T(8,128)}, u32[]{:S(2)}) copy-start(f32[8,8,64,127]{3,2,1,0:T(8,128)} %get-tuple-element.20) | copy-start | bytes 6242308
  37.0 7.7 %copy-start.3 = (f32[8,8,63,128]{3,2,1,0:T(8,128)S(1)}, f32[8,8,63,128]{3,2,1,0:T(8,128)}, u32[]{:S(2)}) copy-start(f32[8,8,63,128]{3,2,1,0:T(8,128)} %get-tuple-element.17) | copy-start | bytes 6193156
  44.7 4.6 %copy-start.2 = (f32[8,8,64,128]{3,2,1,0:T(8,128)S(1)}, f32[8,8,64,128]{3,2,1,0:T(8,128)}, u32[]{:S(2)}) copy-start(f32[8,8,64,128]{3,2,1,0:T(8,128)} %copy-done.1) | copy-start | bytes 6291460
  44.7 4.6 %copy-start.7 = (f32[8,8,64,128]{3,2,1,0:T(8,128)S(1)}, f32[8,8,64,128]{3,2,1,0:T(8,128)}, u32[]{:S(2)}) copy-start(f32[8,8,64,128]{3,2,1,0:T(8,128)} %param.5) | copy-start | bytes 6291460
  44.7 4.6 %copy-start.8 = (f32[8,8,64,127]{3,2,1,0:T(8,128)S(1)}, f32[8,8,64,127]{3,2,1,0:T(8,128)}, u32[]{:S(2)}) copy-start(f32[8,8,64,127]{3,2,1,0:T(8,128)} %get-tuple-element.9) | copy-start | bytes 6242308
  44.7 4.6 %copy-start.9 = (f32[8,8,64,127]{3,2,1,0:T(8,128)S(1)}, f32[8,8,64,127]{3,2,1,0:T(8,128)}, u32[]{:S(2)}) copy-start(f32[8,8,64,127]{3,2,1,0:T(8,128)} %get-tuple-element.10) | copy-start | bytes 6242308
  44.7 4.7 %copy-start.10 = (f32[8,8,64,1]{3,2,1,0:T(8,128)S(1)}, f32[8,8,64,1]{3,2,1,0:T(8,128)}, u32[]{:S(2)}) copy-start(f32[8,8,64,1]{3,2,1,0:T(8,128)} %get-tuple-element.11) | copy-start | bytes 49156
  44.7 5.6 %copy-start.11 = (f32[8,8,64,1]{3,2,1,0:T(8,128)S(1)}, f32[8,8,64,1]{3,2,1,0:T(8,128)}, u32[]{:S(2)}) copy-start(f32[8,8,64,1]{3,2,1,0:T(8,128)} %get-tuple-element.12) | copy-start | bytes 49156
  44.7 6.2 %copy-start.12 = (f32[8,8,63,128]{3,2,1,0:T(8,128)S(1)}, f32[8,8,63,128]{3,2,1,0:T(8,128)}, u32[]{:S(2)}) copy-start(f32[8,8,63,128]{3,2,1,0:T(8,128)} %get-tuple-element.7) | copy-start | bytes 6193156
  44.8 6.8 %copy-start.13 = (f32[8,8,63,128]{3,2,1,0:T(8,128)S(1)}, f32[8,8,63,128]{3,2,1,0:T(8,128)}, u32[]{:S(2)}) copy-start(f32[8,8,63,128]{3,2,1,0:T(8,128)} %get-tuple-element.8) | copy-start | bytes 6193156

commit v2 on v0

v2 whole, which is shorter than its diff:
```python
import jax
import jax.numpy as jnp
from jax import lax
from jax.experimental import pallas as pl
from jax.experimental.pallas import tpu as pltpu
from jax.sharding import PartitionSpec as P


def neighbour_rows(cells, axis):
    count = lax.axis_size(axis)
    head = cells[:, :1]
    tail = cells[:, -1:]
    below = lax.ppermute(tail, axis, [(i, (i + 1) % count) for i in range(count)])
    above = lax.ppermute(head, axis, [((i + 1) % count, i) for i in range(count)])
    return jnp.concatenate([below, above], axis=1)


def step_kernel(rate_ref, index_ref, labels_ref, order_ref, adjoint_ref, order_halo_ref, adjoint_halo_ref,
                own_ref, other_ref, order_next_ref, adjoint_order_ref):
    p = pl.program_id(0)
    rate = 0.1 * rate_ref[p]
    index = index_ref[p]
    rows = order_ref.shape[1]
    depth = order_ref.shape[2]
    width = order_ref.shape[3]
    level = lax.broadcasted_iota(jnp.int32, (depth, width), 0)
    top = level == depth - 1
    bottom = level == 0

    def laplace(centre, before, after):
        beside = before + after
        beside = beside + pltpu.roll(centre, 1, 1) + pltpu.roll(centre, width - 1, 1)
        upper = jnp.where(top, centre, pltpu.roll(centre, depth - 1, 0))
        lower = jnp.where(bottom, centre, pltpu.roll(centre, 1, 0))
        return beside + upper + lower - 6.0 * centre

    def order_row(j):
        if j < 0:
            return order_halo_ref[0, 0]
        if j >= rows:
            return order_halo_ref[0, 1]
        return order_ref[0, j]

    def weight_row(j):
        if j < 0:
            return rate * adjoint_halo_ref[0, 0]
        if j >= rows:
            return rate * adjoint_halo_ref[0, 1]
        return rate * adjoint_ref[0, j]

    for j in range(rows):
        o = order_row(j)
        adj = adjoint_ref[0, j]
        w = rate * adj
        squares = own_ref[0, j] + other_ref[0, j]
        coupled = own_ref[1, j] + other_ref[1, j]
        foreign = (labels_ref[j : j + 1, :] != index).astype(jnp.float32)
        sign = -1.0 + 2.0 * foreign
        potential = sign * o - 2.0 * (o * o * o) + 3.0 * o * squares - 0.5 * laplace(o, order_row(j - 1), order_row(j + 1))
        order_next_ref[0, j] = o - rate * potential
        local_part = (sign - 6.0 * o * o + 3.0 * squares) * w
        adjoint_order_ref[0, j] = adj - (local_part + 6.0 * o * coupled - 0.5 * laplace(w, weight_row(j - 1), weight_row(j + 1)))


def local(order_field, adjoint_next, mobility, labels):
    count, rows, depth, width = order_field.shape
    first = lax.axis_index("op") * count
    indices = first + jnp.arange(count, dtype=jnp.int32)
    rates = mobility[:, None, None, None]
    weighted = 0.1 * rates * adjoint_next
    own = jnp.stack([jnp.sum(order_field * order_field, axis=0), jnp.sum(order_field * weighted, axis=0)])
    parts = lax.axis_size("op")
    other = lax.ppermute(own, "op", [(i, (i + 1) % parts) for i in range(parts)])
    order_halo = neighbour_rows(order_field, "space")
    adjoint_halo = neighbour_rows(adjoint_next, "space")
    block = pl.BlockSpec((1, rows, depth, width), lambda p, *_: (p, 0, 0, 0))
    halo = pl.BlockSpec((1, 2, depth, width), lambda p, *_: (p, 0, 0, 0))
    sums = pl.BlockSpec((2, rows, depth, width), lambda p, *_: (0, 0, 0, 0))
    grid_spec = pltpu.PrefetchScalarGridSpec(
        num_scalar_prefetch=2,
        grid=(count,),
        in_specs=[
            pl.BlockSpec((rows, width), lambda p, *_: (0, 0)),
            block,
            block,
            halo,
            halo,
            sums,
            sums,
        ],
        out_specs=[block, block],
    )
    return pl.pallas_call(
        step_kernel,
        grid_spec=grid_spec,
        out_shape=[jax.ShapeDtypeStruct(order_field.shape, jnp.float32)] * 2,
    )(mobility, indices, labels, order_field, adjoint_next, order_halo, adjoint_halo, own, other)


def solution(mesh):
    placed = (P("op", "space", None, None), P("op", "space", None, None), P("op"), P("space", None))
    return jax.shard_map(
        local,
        mesh=mesh,
        in_specs=placed,
        out_specs=(P("op", "space", None, None), P("op", "space", None, None)),
        check_vma=False,
    )
```

time: 110 us -> 55 us (0.50)
  the two profiles are of different devices: /device:TPU:1 before, /device:TPU:64 now
where the time goes in v2:
time: 55 us; the launch traced here: 54.2 us
  waiting for transfers between devices  18.3 us (33%)
  starting transfers between devices  17.5 us (32%)
  Pallas kernels  9 us (16%)
  other arithmetic  5.74 us (10%)
  local copies, waits for them, and re-layouts  2.93 us (5%)
  between operations  0.68 us (1%)
    ppermute x2, waiting for transfers between devices, neighbour_rows(): lax.ppermute(tail, axis, [(i, (i + 1) % count) for i in range(count)])  18.3 us
    ppermute x2, starting transfers between devices, neighbour_rows(): lax.ppermute(head, axis, [((i + 1) % count, i) for i in range(count)])  11.9 us
    pallas_call x1, Pallas kernels, local(): pl.pallas_call(step_kernel, grid_spec=grid_spec, out_shape=[jax.ShapeDtyp...  9 us
    ppermute x1, starting transfers between devices, local(): lax.ppermute(own, 'op', [(i, (i + 1) % parts) for i in range(parts)])  5.48 us
    reduce_sum x1, other arithmetic, local(): jnp.sum(order_field * order_field, axis=0)  2.85 us
    slice x2, local copies, waits for them, and re-layouts, neighbour_rows(): tail = cells[:, -1:]  2.14 us
    concatenate x2, other arithmetic, neighbour_rows(): return jnp.concatenate([below, above], axis=1)  1.67 us
  transfers between devices with their start and end apart: 5, of which 1 were waited for; matrix products, arithmetic and copies ran while one was open for 13% of the time, Pallas kernels for 0%

profile of v2, /device:TPU:64, one launch (start us, length us, event | category | flops | bytes accessed | tf_op | source)
XLA Modules:
  0.0 54.2 jit_solution(13057857872458912)
XLA Ops:
  0.6 1.1 %fusion.1 = (f32[8,1,64,128]{3,2,1,0:T(8,128)S(1)}, f32[8,1,64,128]{3,2,1,0:T(8,128)S(1)}) fusion(f32[8,8,64,128]{3,2,1,0:T(8,128)} %order_ref.1), kind=kLoop, calls=%fused_computation.8 | loop fusion | bytes 1048576 | tf_op jit(solution)/shard_map/slice | solution.py:12
  1.7 0.1 collective-permute-start
  1.8 6.0 %collective-permute-start.1 = (f32[8,1,64,128]{3,2,1,0:T(8,128)S(1)}, f32[8,1,64,128]{3,2,1,0:T(8,128)S(1)}, u32[]{:S(2)}, u32[]{:S(2)}) collective-permute-start(f32[8,1,64,128]{3,2,1,0:T(8,128)S(1)} %get-tuple-element.7), channel_id=1, source_target_pairs={{2,0},{4,2},{6,4},{8,6},{10,8},{12,10},{14,12},{16,14},{18,16},{20... | collective-permute-start | bytes 786440 | tf_op jit(solution)/shard_map/ppermute | solution.py:14
  7.8 0.7 %broadcast_multiply_fusion = f32[8]{0:T(128)S(1)} fusion(f32[8]{0:T(128)} %rate_ref.1), kind=kLoop, calls=%fused_computation.6 | loop fusion | flops 8 | bytes 64 | tf_op jit(solution)/shard_map/mul | solution.py:70
  8.4 2.9 %multiply_reduce_fusion.1 = (f32[8,64,128]{2,1,0:T(8,128)S(1)}, f32[8,64,128]{2,1,0:T(8,128)S(1)}) fusion(f32[8,8,64,128]{3,2,1,0:T(8,128)} %order_ref.1, f32[8,8,64,128]{3,2,1,0:T(8,128)} %adjoint_ref.1, f32[8]{0:T(128)S(1)} %broadcast_multiply_fusion), kind=kLoop, calls=%fused_computation.1 | loop fusion | flops 2490368 | bytes 4718624 | tf_op jit(solution)/shard_map/reduce_sum | solution.py:71
  11.3 0.0 copy-start
  11.3 5.5 %collective-permute-start.4 = (f32[2,8,64,128]{3,2,1,0:T(8,128)S(1)}, f32[2,8,64,128]{3,2,1,0:T(8,128)S(1)}, u32[]{:S(2)}, u32[]{:S(2)}) collective-permute-start(f32[2,8,64,128]{3,2,1,0:T(8,128)S(1)} %pad_maximum_fusion.2.own_ref), channel_id=1, source_target_pairs={{0,1},{1,0},{2,3},{3,2},{4,5},{5,4},{6,7},{7,6},{8,9},{9,8},{10,11... | collective-permute-start | bytes 1572872 | tf_op jit(solution)/shard_map/ppermute | solution.py:73
  16.8 1.1 %fusion = (f32[8,1,64,128]{3,2,1,0:T(8,128)S(1)}, f32[8,1,64,128]{3,2,1,0:T(8,128)S(1)}) fusion(f32[8,8,64,128]{3,2,1,0:T(8,128)} %adjoint_ref.1), kind=kLoop, calls=%fused_computation.7 | loop fusion | bytes 1048576 | tf_op jit(solution)/shard_map/slice | solution.py:12
  17.9 0.1 collective-permute-start.2
  18.0 6.0 %collective-permute-start.3 = (f32[8,1,64,128]{3,2,1,0:T(8,128)S(1)}, f32[8,1,64,128]{3,2,1,0:T(8,128)S(1)}, u32[]{:S(2)}, u32[]{:S(2)}) collective-permute-start(f32[8,1,64,128]{3,2,1,0:T(8,128)S(1)} %get-tuple-element.5), channel_id=1, source_target_pairs={{2,0},{4,2},{6,4},{8,6},{10,8},{12,10},{14,12},{16,14},{18,16},{20... | collective-permute-start | bytes 786440 | tf_op jit(solution)/shard_map/ppermute | solution.py:14
  23.9 0.5 iota_add_fusion.index_ref
  24.4 0.0 collective-permute-done
  24.4 0.0 collective-permute-done.1
  24.4 0.8 %pad_maximum_fusion.order_halo_ref = f32[8,2,64,128]{3,2,1,0:T(8,128)} fusion(f32[8,1,64,128]{3,2,1,0:T(8,128)S(1)} %collective-permute-done.1, f32[8,1,64,128]{3,2,1,0:T(8,128)S(1)} %collective-permute-done), kind=kLoop, calls=%fused_computation.2 | loop fusion | flops 131072 | bytes 1048576 | tf_op jit(solution)/shard_map/concatenate | solution.py:15
  25.3 18.3 %collective-permute-done.2 = f32[8,1,64,128]{3,2,1,0:T(8,128)S(1)} collective-permute-done((f32[8,1,64,128]{3,2,1,0:T(8,128)S(1)}, f32[8,1,64,128]{3,2,1,0:T(8,128)S(1)}, u32[]{:S(2)}, u32[]{:S(2)}) %collective-permute-start.2) | collective-permute-done | bytes 262176 | tf_op jit(solution)/shard_map/ppermute | solution.py:13
  43.5 0.0 collective-permute-done.3
  43.5 0.8 %pad_maximum_fusion.1.adjoint_halo_ref = f32[8,2,64,128]{3,2,1,0:T(8,128)} fusion(f32[8,1,64,128]{3,2,1,0:T(8,128)S(1)} %collective-permute-done.3, f32[8,1,64,128]{3,2,1,0:T(8,128)S(1)} %collective-permute-done.2), kind=kLoop, calls=%fused_computation.3 | loop fusion | flops 131072 | bytes 1048576 | tf_op jit(solution)/shard_map/concatenate | solution.py:15
  44.4 0.0 collective-permute-done.4.other_ref
  44.4 0.0 copy-done
  44.4 0.0 copy-start.1
  44.4 0.8 %copy-done.1 = f32[2,8,64,128]{3,2,1,0:T(8,128)} copy-done((f32[2,8,64,128]{3,2,1,0:T(8,128)}, f32[2,8,64,128]{3,2,1,0:T(8,128)S(1)}, u32[]{:S(2)}) %copy-start.1) | copy-done | bytes 524312
  45.2 9.0 %shard_map.59 = (f32[8,8,64,128]{3,2,1,0:T(8,128)}, f32[8,8,64,128]{3,2,1,0:T(8,128)}) custom-call(f32[8]{0:T(128)} %rate_ref.1, s32[8]{0:T(128)} %iota_add_fusion.index_ref, s32[8,128]{1,0:T(8,128)} %labels_ref.1, f32[8,8,64,128]{3,2,1,0:T(8,128)} %order_ref.1, f32[8,8,64,128]{3,2,1,0:T(8,128)} %adjoint_ref.1, ...), custom_call_target="tpu_custom_call" | custom-call | tf_op jit(solution)/shard_map/pallas_call | solution.py:93
  (1 shorter events, 0.0 us)
Async XLA Ops:
  1.7 22.7 %collective-permute-start = (f32[8,1,64,128]{3,2,1,0:T(8,128)S(1)}, f32[8,1,64,128]{3,2,1,0:T(8,128)S(1)}, u32[]{:S(2)}, u32[]{:S(2)}) collective-permute-start(f32[8,1,64,128]{3,2,1,0:T(8,128)S(1)} %get-tuple-element.6), channel_id=1, source_target_pairs={{0,2},{2,4},{4,6},{6,8},{8,10},{10,12},{12,14},{14,16},{16,18},{18... | collective-permute-start | bytes 786440 | tf_op jit(solution)/shard_map/ppermute | solution.py:13
  1.8 22.6 %collective-permute-start.1 = (f32[8,1,64,128]{3,2,1,0:T(8,128)S(1)}, f32[8,1,64,128]{3,2,1,0:T(8,128)S(1)}, u32[]{:S(2)}, u32[]{:S(2)}) collective-permute-start(f32[8,1,64,128]{3,2,1,0:T(8,128)S(1)} %get-tuple-element.7), channel_id=1, source_target_pairs={{2,0},{4,2},{6,4},{8,6},{10,8},{12,10},{14,12},{16,14},{18,16},{20... | collective-permute-start | bytes 786440 | tf_op jit(solution)/shard_map/ppermute | solution.py:14
  11.3 33.1 %copy-start = (f32[2,8,64,128]{3,2,1,0:T(8,128)}, f32[2,8,64,128]{3,2,1,0:T(8,128)S(1)}, u32[]{:S(2)}) copy-start(f32[2,8,64,128]{3,2,1,0:T(8,128)S(1)} %pad_maximum_fusion.2.own_ref) | copy-start | bytes 1572868
  11.3 33.1 %collective-permute-start.4 = (f32[2,8,64,128]{3,2,1,0:T(8,128)S(1)}, f32[2,8,64,128]{3,2,1,0:T(8,128)S(1)}, u32[]{:S(2)}, u32[]{:S(2)}) collective-permute-start(f32[2,8,64,128]{3,2,1,0:T(8,128)S(1)} %pad_maximum_fusion.2.own_ref), channel_id=1, source_target_pairs={{0,1},{1,0},{2,3},{3,2},{4,5},{5,4},{6,7},{7,6},{8,9},{9,8},{10,11... | collective-permute-start | bytes 1572872 | tf_op jit(solution)/shard_map/ppermute | solution.py:73
  17.9 25.7 %collective-permute-start.2 = (f32[8,1,64,128]{3,2,1,0:T(8,128)S(1)}, f32[8,1,64,128]{3,2,1,0:T(8,128)S(1)}, u32[]{:S(2)}, u32[]{:S(2)}) collective-permute-start(f32[8,1,64,128]{3,2,1,0:T(8,128)S(1)} %get-tuple-element.4), channel_id=1, source_target_pairs={{0,2},{2,4},{4,6},{6,8},{8,10},{10,12},{12,14},{14,16},{16,18},{18... | collective-permute-start | bytes 786440 | tf_op jit(solution)/shard_map/ppermute | solution.py:13
  18.0 25.6 %collective-permute-start.3 = (f32[8,1,64,128]{3,2,1,0:T(8,128)S(1)}, f32[8,1,64,128]{3,2,1,0:T(8,128)S(1)}, u32[]{:S(2)}, u32[]{:S(2)}) collective-permute-start(f32[8,1,64,128]{3,2,1,0:T(8,128)S(1)} %get-tuple-element.5), channel_id=1, source_target_pairs={{2,0},{4,2},{6,4},{8,6},{10,8},{12,10},{14,12},{16,14},{18,16},{20... | collective-permute-start | bytes 786440 | tf_op jit(solution)/shard_map/ppermute | solution.py:14
  44.4 0.8 %copy-start.1 = (f32[2,8,64,128]{3,2,1,0:T(8,128)}, f32[2,8,64,128]{3,2,1,0:T(8,128)S(1)}, u32[]{:S(2)}) copy-start(f32[2,8,64,128]{3,2,1,0:T(8,128)S(1)} %collective-permute-done.4.other_ref) | copy-start | bytes 1572868

commit v3 on v2

v3 whole, which is shorter than its diff:
```python
import jax
import jax.numpy as jnp
from jax import lax
from jax.experimental import pallas as pl
from jax.experimental.pallas import tpu as pltpu
from jax.sharding import PartitionSpec as P


def shift_along(cells, axis, step):
    count = lax.axis_size(axis)
    return lax.ppermute(cells, axis, [(i, (i + step) % count) for i in range(count)])


def step_kernel(rate_ref, index_ref, labels_ref, order_ref, adjoint_ref, below_ref, above_ref,
                own_ref, other_ref, order_next_ref, adjoint_order_ref):
    p = pl.program_id(0)
    rate = 0.1 * rate_ref[p]
    index = index_ref[p]
    rows = order_ref.shape[1]
    depth = order_ref.shape[2]
    width = order_ref.shape[3]
    level = lax.broadcasted_iota(jnp.int32, (depth, width), 0)
    top = level == depth - 1
    bottom = level == 0

    def laplace(centre, before, after):
        beside = before + after
        beside = beside + pltpu.roll(centre, 1, 1) + pltpu.roll(centre, width - 1, 1)
        upper = jnp.where(top, centre, pltpu.roll(centre, depth - 1, 0))
        lower = jnp.where(bottom, centre, pltpu.roll(centre, 1, 0))
        return beside + upper + lower - 6.0 * centre

    def load(j):
        if j < 0:
            return below_ref[0, 0, 0], rate * below_ref[1, 0, 0]
        if j >= rows:
            return above_ref[0, 0, 0], rate * above_ref[1, 0, 0]
        return order_ref[0, j], rate * adjoint_ref[0, j]

    prev = load(-1)
    cur = load(0)
    for j in range(rows):
        nxt = load(j + 1)
        o, w = cur
        adj = adjoint_ref[0, j]
        squares = own_ref[0, j] + other_ref[0, j]
        coupled = own_ref[1, j] + other_ref[1, j]
        sign = jnp.where(labels_ref[j : j + 1, :] != index, 1.0, -1.0)
        potential = sign * o - 2.0 * (o * o * o) + 3.0 * o * squares - 0.5 * laplace(o, prev[0], nxt[0])
        order_next_ref[0, j] = o - rate * potential
        local_part = (sign - 6.0 * o * o + 3.0 * squares) * w
        adjoint_order_ref[0, j] = adj - (local_part + 6.0 * o * coupled - 0.5 * laplace(w, prev[1], nxt[1]))
        prev, cur = cur, nxt


def local(order_field, adjoint_next, mobility, labels):
    count, rows, depth, width = order_field.shape
    first = lax.axis_index("op") * count
    indices = first + jnp.arange(count, dtype=jnp.int32)
    rates = mobility[:, None, None, None]
    weighted = 0.1 * rates * adjoint_next
    own = jnp.stack([jnp.sum(order_field * order_field, axis=0), jnp.sum(order_field * weighted, axis=0)])
    other = shift_along(own, "op", 1)
    pair = jnp.stack([order_field, adjoint_next])
    edges = jnp.concatenate([pair[:, :, :1], pair[:, :, -1:]], axis=2)
    edges, own = lax.optimization_barrier((edges, own))
    below = shift_along(edges[:, :, 1:], "space", 1)
    above = shift_along(edges[:, :, :1], "space", -1)
    block = pl.BlockSpec((1, rows, depth, width), lambda p, *_: (p, 0, 0, 0))
    halo = pl.BlockSpec((2, 1, 1, depth, width), lambda p, *_: (0, p, 0, 0, 0))
    sums = pl.BlockSpec((2, rows, depth, width), lambda p, *_: (0, 0, 0, 0))
    grid_spec = pltpu.PrefetchScalarGridSpec(
        num_scalar_prefetch=2,
        grid=(count,),
        in_specs=[pl.BlockSpec((rows, width), lambda p, *_: (0, 0)), block, block, halo, halo, sums, sums],
        out_specs=[block, block],
    )
    return pl.pallas_call(
        step_kernel,
        grid_spec=grid_spec,
        out_shape=[jax.ShapeDtypeStruct(order_field.shape, jnp.float32)] * 2,
    )(mobility, indices, labels, order_field, adjoint_next, below, above, own, other)


def solution(mesh):
    placed = (P("op", "space", None, None), P("op", "space", None, None), P("op"), P("space", None))
    return jax.shard_map(
        local,
        mesh=mesh,
        in_specs=placed,
        out_specs=(P("op", "space", None, None), P("op", "space", None, None)),
        check_vma=False,
    )
```

time: 55 us -> 54.3 us (0.987)
  waiting for transfers between devices: 18.3 us -> 28.3 us
  starting transfers between devices: 17.5 us -> 10.4 us
  local copies, waits for them, and re-layouts: 2.93 us -> 0.91 us
  other arithmetic: 5.74 us -> 4.3 us
    ppermute x5 -> x3, waiting for transfers between devices: 18.3 us -> 28.3 us  [shift_along(): lax.ppermute(cells, axis, [(i, (i + step) % count) for i in range(count)])]
    ppermute x5 -> x3, starting transfers between devices: 17.5 us -> 10.4 us  [shift_along(): lax.ppermute(cells, axis, [(i, (i + step) % count) for i in range(count)])]
    slice x2 -> x1, local copies, waits for them, and re-layouts: 2.14 us -> 0.1 us  [local(): above = shift_along(edges[:, :, :1], 'space', -1)]
    concatenate x2 -> x1, other arithmetic: 1.67 us -> 0.08 us  [local(): edges = jnp.concatenate([pair[:, :, :1], pair[:, :, -1:]], axis=2)]
  transfers between devices with their start and end apart: 5 -> 3, of which waited for: 1 -> 2; matrix products, arithmetic and copies ran while one was open for 13% -> 1% of each run, Pallas kernels for 0% -> 0%
where the time goes in v3:
time: 54.3 us; the launch traced here: 53.5 us
  waiting for transfers between devices  28.3 us (52%)
  starting transfers between devices  10.4 us (19%)
  Pallas kernels  8.96 us (17%)
  other arithmetic  4.3 us (8%)
  local copies, waits for them, and re-layouts  0.91 us (2%)
  between operations  0.68 us (1%)
    ppermute x3, waiting for transfers between devices, shift_along(): lax.ppermute(cells, axis, [(i, (i + step) % count) for i in range(count)])  28.3 us
    ppermute x3, starting transfers between devices, shift_along(): lax.ppermute(cells, axis, [(i, (i + step) % count) for i in range(count)])  10.4 us
    pallas_call x1, Pallas kernels, local(): pl.pallas_call(step_kernel, grid_spec=grid_spec, out_shape=[jax.ShapeDtyp...  8.96 us
    reduce_sum x1, other arithmetic, local(): jnp.sum(order_field * order_field, axis=0)  3.01 us
  transfers between devices with their start and end apart: 3, of which 2 were waited for; matrix products, arithmetic and copies ran while one was open for 1% of the time, Pallas kernels for 0%

profile of v3, /device:TPU:64, one launch (start us, length us, event | category | flops | bytes accessed | tf_op | source)
XLA Modules:
  0.0 53.5 jit_solution(2184060226232893770)
XLA Ops:
  0.6 0.7 %broadcast_multiply_fusion = f32[8]{0:T(128)S(1)} fusion(f32[8]{0:T(128)} %rate_ref.1), kind=kLoop, calls=%fused_computation.9 | loop fusion | flops 8 | bytes 64 | tf_op jit(solution)/shard_map/mul | solution.py:61
  1.3 0.0 copy-start
  1.3 0.0 copy-start.1
  1.3 3.0 %multiply_reduce_fusion.1 = (f32[8,64,128]{2,1,0:T(8,128)S(1)}, f32[8,64,128]{2,1,0:T(8,128)S(1)}) fusion(f32[8,8,64,128]{3,2,1,0:T(8,128)} %order_ref.1, f32[8,8,64,128]{3,2,1,0:T(8,128)} %adjoint_ref.1, f32[8]{0:T(128)S(1)} %broadcast_multiply_fusion), kind=kLoop, calls=%fused_computation.1 | loop fusion | flops 2490368 | bytes 4718624 | tf_op jit(solution)/shard_map/reduce_sum | solution.py:62
  4.4 0.0 copy-start.2
  4.4 5.5 %collective-permute-start.2 = (f32[2,8,64,128]{3,2,1,0:T(8,128)S(1)}, f32[2,8,64,128]{3,2,1,0:T(8,128)S(1)}, u32[]{:S(2)}, u32[]{:S(2)}) collective-permute-start(f32[2,8,64,128]{3,2,1,0:T(8,128)S(1)} %pad_maximum_fusion.own_ref), channel_id=1, source_target_pairs={{0,1},{1,0},{2,3},{3,2},{4,5},{5,4},{6,7},{7,6},{8,9},{9,8},{10,11... | collective-permute-start | bytes 1572872 | tf_op jit(solution)/shard_map/ppermute | solution.py:11
  9.8 0.0 copy-done
  9.8 0.0 copy-done.1
  9.8 0.1 fusion
  9.9 0.0 copy-done.2
  9.9 0.1 fusion.1
  10.1 4.9 %collective-permute-start.1 = (f32[2,8,1,64,128]{4,3,2,1,0:T(8,128)S(1)}, f32[2,8,1,64,128]{4,3,2,1,0:T(8,128)S(1)}, u32[]{:S(2)}, u32[]{:S(2)}) collective-permute-start(f32[2,8,1,64,128]{4,3,2,1,0:T(8,128)S(1)} %get-tuple-element.8), channel_id=1, source_target_pairs={{0,254},{2,0},{4,2},{6,4},{8,6},{10,8},{12,10},{14,12},{16,14},{18... | collective-permute-start | bytes 1572872 | tf_op jit(solution)/shard_map/ppermute | solution.py:11
  14.9 0.0 collective-permute-start
  14.9 0.5 iota_add_fusion.index_ref
  15.5 23.5 %collective-permute-done.2.other_ref = f32[2,8,64,128]{3,2,1,0:T(8,128)S(1)} collective-permute-done((f32[2,8,64,128]{3,2,1,0:T(8,128)S(1)}, f32[2,8,64,128]{3,2,1,0:T(8,128)S(1)}, u32[]{:S(2)}, u32[]{:S(2)}) %collective-permute-start.2) | collective-permute-done | bytes 524320 | tf_op jit(solution)/shard_map/ppermute | solution.py:11
  38.9 0.0 copy-start.3
  38.9 0.0 collective-permute-done.1.above_ref
  38.9 0.0 copy-start.4
  38.9 4.8 %collective-permute-done.below_ref = f32[2,8,1,64,128]{4,3,2,1,0:T(8,128)S(1)} collective-permute-done((f32[2,8,1,64,128]{4,3,2,1,0:T(8,128)S(1)}, f32[2,8,1,64,128]{4,3,2,1,0:T(8,128)S(1)}, u32[]{:S(2)}, u32[]{:S(2)}) %collective-permute-start) | collective-permute-done | bytes 524320 | tf_op jit(solution)/shard_map/ppermute | solution.py:11
  43.7 0.0 copy-done.3
  43.7 0.0 copy-done.4
  43.7 0.0 copy-start.5
  43.7 0.8 %copy-done.5 = f32[2,8,1,64,128]{4,3,2,1,0:T(8,128)} copy-done((f32[2,8,1,64,128]{4,3,2,1,0:T(8,128)}, f32[2,8,1,64,128]{4,3,2,1,0:T(8,128)S(1)}, u32[]{:S(2)}) %copy-start.5) | copy-done | bytes 524312
  44.5 9.0 %shard_map.59 = (f32[8,8,64,128]{3,2,1,0:T(8,128)}, f32[8,8,64,128]{3,2,1,0:T(8,128)}) custom-call(f32[8]{0:T(128)} %rate_ref.1, s32[8]{0:T(128)} %iota_add_fusion.index_ref, s32[8,128]{1,0:T(8,128)} %labels_ref.1, f32[8,8,64,128]{3,2,1,0:T(8,128)} %order_ref.1, f32[8,8,64,128]{3,2,1,0:T(8,128)} %adjoint_ref.1, f32[2,8,1,64,128]{4,3,2,1,0:T(8,128)} %copy-done.5, ...), custom_call_target="tpu_custom_call" | custom-call | tf_op jit(solution)/shard_map/pallas_call | solution.py:78
  (1 shorter events, 0.0 us)
Async XLA Ops:
  1.3 8.6 %copy-start = (f32[8,8,64,128]{3,2,1,0:T(8,128)S(1)}, f32[8,8,64,128]{3,2,1,0:T(8,128)}, u32[]{:S(2)}) copy-start(f32[8,8,64,128]{3,2,1,0:T(8,128)} %order_ref.1) | copy-start | bytes 6291460
  1.3 8.6 %copy-start.1 = (f32[8,8,64,128]{3,2,1,0:T(8,128)S(1)}, f32[8,8,64,128]{3,2,1,0:T(8,128)}, u32[]{:S(2)}) copy-start(f32[8,8,64,128]{3,2,1,0:T(8,128)} %adjoint_ref.1) | copy-start | bytes 6291460
  4.4 5.6 %copy-start.2 = (f32[2,8,64,128]{3,2,1,0:T(8,128)}, f32[2,8,64,128]{3,2,1,0:T(8,128)S(1)}, u32[]{:S(2)}) copy-start(f32[2,8,64,128]{3,2,1,0:T(8,128)S(1)} %pad_maximum_fusion.own_ref) | copy-start | bytes 1572868
  4.4 34.6 %collective-permute-start.2 = (f32[2,8,64,128]{3,2,1,0:T(8,128)S(1)}, f32[2,8,64,128]{3,2,1,0:T(8,128)S(1)}, u32[]{:S(2)}, u32[]{:S(2)}) collective-permute-start(f32[2,8,64,128]{3,2,1,0:T(8,128)S(1)} %pad_maximum_fusion.own_ref), channel_id=1, source_target_pairs={{0,1},{1,0},{2,3},{3,2},{4,5},{5,4},{6,7},{7,6},{8,9},{9,8},{10,11... | collective-permute-start | bytes 1572872 | tf_op jit(solution)/shard_map/ppermute | solution.py:11
  10.1 28.9 %collective-permute-start.1 = (f32[2,8,1,64,128]{4,3,2,1,0:T(8,128)S(1)}, f32[2,8,1,64,128]{4,3,2,1,0:T(8,128)S(1)}, u32[]{:S(2)}, u32[]{:S(2)}) collective-permute-start(f32[2,8,1,64,128]{4,3,2,1,0:T(8,128)S(1)} %get-tuple-element.8), channel_id=1, source_target_pairs={{0,254},{2,0},{4,2},{6,4},{8,6},{10,8},{12,10},{14,12},{16,14},{18... | collective-permute-start | bytes 1572872 | tf_op jit(solution)/shard_map/ppermute | solution.py:11
  14.9 28.8 %collective-permute-start = (f32[2,8,1,64,128]{4,3,2,1,0:T(8,128)S(1)}, f32[2,8,1,64,128]{4,3,2,1,0:T(8,128)S(1)}, u32[]{:S(2)}, u32[]{:S(2)}) collective-permute-start(f32[2,8,1,64,128]{4,3,2,1,0:T(8,128)S(1)} %get-tuple-element.9), channel_id=1, source_target_pairs={{0,2},{2,4},{4,6},{6,8},{8,10},{10,12},{12,14},{14,16},{16,18},{18... | collective-permute-start | bytes 1572872 | tf_op jit(solution)/shard_map/ppermute | solution.py:11
  38.9 4.8 %copy-start.3 = (f32[2,8,64,128]{3,2,1,0:T(8,128)}, f32[2,8,64,128]{3,2,1,0:T(8,128)S(1)}, u32[]{:S(2)}) copy-start(f32[2,8,64,128]{3,2,1,0:T(8,128)S(1)} %collective-permute-done.2.other_ref) | copy-start | bytes 1572868
  38.9 4.8 %copy-start.4 = (f32[2,8,1,64,128]{4,3,2,1,0:T(8,128)}, f32[2,8,1,64,128]{4,3,2,1,0:T(8,128)S(1)}, u32[]{:S(2)}) copy-start(f32[2,8,1,64,128]{4,3,2,1,0:T(8,128)S(1)} %collective-permute-done.1.above_ref) | copy-start | bytes 1572868
  43.7 0.8 %copy-start.5 = (f32[2,8,1,64,128]{4,3,2,1,0:T(8,128)}, f32[2,8,1,64,128]{4,3,2,1,0:T(8,128)S(1)}, u32[]{:S(2)}) copy-start(f32[2,8,1,64,128]{4,3,2,1,0:T(8,128)S(1)} %collective-permute-done.below_ref) | copy-start | bytes 1572868

commit v4 on v3

--- a/solution.py
+++ b/solution.py
@@ -11,14 +11,7 @@
     return lax.ppermute(cells, axis, [(i, (i + step) % count) for i in range(count)])
 
 
-def step_kernel(rate_ref, index_ref, labels_ref, order_ref, adjoint_ref, below_ref, above_ref,
-                own_ref, other_ref, order_next_ref, adjoint_order_ref):
-    p = pl.program_id(0)
-    rate = 0.1 * rate_ref[p]
-    index = index_ref[p]
-    rows = order_ref.shape[1]
-    depth = order_ref.shape[2]
-    width = order_ref.shape[3]
+def stencil(depth, width):
     level = lax.broadcasted_iota(jnp.int32, (depth, width), 0)
     top = level == depth - 1
     bottom = level == 0
@@ -30,6 +23,38 @@
         lower = jnp.where(bottom, centre, pltpu.roll(centre, 1, 0))
         return beside + upper + lower - 6.0 * centre
 
+    return laplace
+
+
+def inner_kernel(rate_ref, index_ref, labels_ref, order_ref, adjoint_ref, inner_order_ref, inner_adjoint_ref):
+    p = pl.program_id(0)
+    rate = 0.1 * rate_ref[p]
+    index = index_ref[p]
+    _, rows, depth, width = order_ref.shape
+    laplace = stencil(depth, width)
+
+    def load(j):
+        return order_ref[0, j], rate * adjoint_ref[0, j]
+
+    prev = load(0)
+    cur = load(1)
+    for j in range(1, rows - 1):
+        nxt = load(j + 1)
+        o, w = cur
+        sign = jnp.where(labels_ref[j : j + 1, :] != index, 1.0, -1.0)
+        inner_order_ref[0, j - 1] = sign * o - 2.0 * (o * o * o) - 0.5 * laplace(o, prev[0], nxt[0])
+        inner_adjoint_ref[0, j - 1] = (sign - 6.0 * o * o) * w - 0.5 * laplace(w, prev[1], nxt[1])
+        prev, cur = cur, nxt
+
+
+def step_kernel(rate_ref, index_ref, labels_ref, order_ref, adjoint_ref, below_ref, above_ref,
+                own_ref, other_ref, inner_order_ref, inner_adjoint_ref, order_next_ref, adjoint_order_ref):
+    p = pl.program_id(0)
+    rate = 0.1 * rate_ref[p]
+    index = index_ref[p]
+    _, rows, depth, width = order_ref.shape
+    laplace = stencil(depth, width)
+
     def load(j):
         if j < 0:
             return below_ref[0, 0, 0], rate * below_ref[1, 0, 0]
@@ -37,20 +62,22 @@
             return above_ref[0, 0, 0], rate * above_ref[1, 0, 0]
         return order_ref[0, j], rate * adjoint_ref[0, j]
 
-    prev = load(-1)
-    cur = load(0)
     for j in range(rows):
-        nxt = load(j + 1)
-        o, w = cur
+        o, w = load(j)
         adj = adjoint_ref[0, j]
         squares = own_ref[0, j] + other_ref[0, j]
         coupled = own_ref[1, j] + other_ref[1, j]
+        if 0 < j < rows - 1:
+            order_next_ref[0, j] = o - rate * (inner_order_ref[0, j - 1] + 3.0 * o * squares)
+            adjoint_order_ref[0, j] = adj - ((inner_adjoint_ref[0, j - 1] + 3.0 * squares * w) + 6.0 * o * coupled)
+            continue
+        prev = load(j - 1)
+        nxt = load(j + 1)
         sign = jnp.where(labels_ref[j : j + 1, :] != index, 1.0, -1.0)
         potential = sign * o - 2.0 * (o * o * o) + 3.0 * o * squares - 0.5 * laplace(o, prev[0], nxt[0])
         order_next_ref[0, j] = o - rate * potential
         local_part = (sign - 6.0 * o * o + 3.0 * squares) * w
         adjoint_order_ref[0, j] = adj - (local_part + 6.0 * o * coupled - 0.5 * laplace(w, prev[1], nxt[1]))
-        prev, cur = cur, nxt
 
 
 def local(order_field, adjoint_next, mobility, labels):
@@ -63,23 +90,30 @@
     other = shift_along(own, "op", 1)
     pair = jnp.stack([order_field, adjoint_next])
     edges = jnp.concatenate([pair[:, :, :1], pair[:, :, -1:]], axis=2)
-    edges, own = lax.optimization_barrier((edges, own))
+    edges, own, order_late, adjoint_late = lax.optimization_barrier((edges, own, order_field, adjoint_next))
     below = shift_along(edges[:, :, 1:], "space", 1)
     above = shift_along(edges[:, :, :1], "space", -1)
+    scalars = pltpu.PrefetchScalarGridSpec
     block = pl.BlockSpec((1, rows, depth, width), lambda p, *_: (p, 0, 0, 0))
+    inner = pl.BlockSpec((1, rows - 2, depth, width), lambda p, *_: (p, 0, 0, 0))
+    plane = pl.BlockSpec((rows, width), lambda p, *_: (0, 0))
+    inner_order, inner_adjoint = pl.pallas_call(
+        inner_kernel,
+        grid_spec=scalars(num_scalar_prefetch=2, grid=(count,), in_specs=[plane, block, block], out_specs=[inner, inner]),
+        out_shape=[jax.ShapeDtypeStruct((count, rows - 2, depth, width), jnp.float32)] * 2,
+    )(mobility, indices, labels, order_late, adjoint_late)
     halo = pl.BlockSpec((2, 1, 1, depth, width), lambda p, *_: (0, p, 0, 0, 0))
     sums = pl.BlockSpec((2, rows, depth, width), lambda p, *_: (0, 0, 0, 0))
-    grid_spec = pltpu.PrefetchScalarGridSpec(
-        num_scalar_prefetch=2,
-        grid=(count,),
-        in_specs=[pl.BlockSpec((rows, width), lambda p, *_: (0, 0)), block, block, halo, halo, sums, sums],
-        out_specs=[block, block],
-    )
     return pl.pallas_call(
         step_kernel,
-        grid_spec=grid_spec,
+        grid_spec=scalars(
+            num_scalar_prefetch=2,
+            grid=(count,),
+            in_specs=[plane, block, block, halo, halo, sums, sums, inner, inner],
+            out_specs=[block, block],
+        ),
         out_shape=[jax.ShapeDtypeStruct(order_field.shape, jnp.float32)] * 2,
-    )(mobility, indices, labels, order_field, adjoint_next, below, above, own, other)
+    )(mobility, indices, labels, order_field, adjoint_next, below, above, own, other, inner_order, inner_adjoint)
 
 
 def solution(mesh):

time: 54.3 us -> 54.3 us (level)
  waiting for transfers between devices: 28.3 us -> 20.3 us
  Pallas kernels: 8.96 us -> 16.8 us
    ppermute x3, waiting for transfers between devices: 28.3 us -> 20.3 us  [shift_along(): lax.ppermute(cells, axis, [(i, (i + step) % count) for i in range(count)])]
    pallas_call x1 -> x2, Pallas kernels: 8.96 us -> 16.8 us  [the longest x1 8.86 us: local(): pl.pallas_call(step_kernel, grid_spec=scalars(num_scalar_prefetch=2, grid...]
  transfers between devices with their start and end apart: 3 -> 3, of which waited for: 2 -> 2; matrix products, arithmetic and copies ran while one was open for 1% -> 1% of each run, Pallas kernels for 0% -> 15%
where the time goes in v4:
time: 54.3 us; the launch traced here: 53.4 us
  waiting for transfers between devices  20.3 us (37%)
  Pallas kernels  16.8 us (31%)
  starting transfers between devices  10.4 us (19%)
  other arithmetic  4.38 us (8%)
  local copies, waits for them, and re-layouts  0.91 us (2%)
  between operations  0.69 us (1%)
    ppermute x3, waiting for transfers between devices, shift_along(): lax.ppermute(cells, axis, [(i, (i + step) % count) for i in range(count)])  20.3 us
    ppermute x3, starting transfers between devices, shift_along(): lax.ppermute(cells, axis, [(i, (i + step) % count) for i in range(count)])  10.4 us
    pallas_call x1, Pallas kernels, local(): pl.pallas_call(step_kernel, grid_spec=scalars(num_scalar_prefetch=2, grid...  8.86 us
    pallas_call x1, Pallas kernels, local(): pl.pallas_call(inner_kernel, grid_spec=scalars(num_scalar_prefetch=2, gri...  7.9 us
    reduce_sum x1, other arithmetic, local(): jnp.sum(order_field * order_field, axis=0)  3.01 us
  transfers between devices with their start and end apart: 3, of which 2 were waited for; matrix products, arithmetic and copies ran while one was open for 1% of the time, Pallas kernels for 15%

profile of v4, /device:TPU:64, one launch (start us, length us, event | category | flops | bytes accessed | tf_op | source)
XLA Modules:
  0.0 53.4 jit_solution(5499972638618821732)
XLA Ops:
  0.6 0.7 %broadcast_multiply_fusion = f32[8]{0:T(128)S(1)} fusion(f32[8]{0:T(128)} %rate_ref.3), kind=kLoop, calls=%fused_computation.9 | loop fusion | flops 8 | bytes 64 | tf_op jit(solution)/shard_map/mul | solution.py:88
  1.3 0.0 copy-start
  1.3 0.0 copy-start.1
  1.3 3.0 %multiply_reduce_fusion.1 = (f32[8,64,128]{2,1,0:T(8,128)S(1)}, f32[8,64,128]{2,1,0:T(8,128)S(1)}) fusion(f32[8,8,64,128]{3,2,1,0:T(8,128)} %order_ref.2, f32[8,8,64,128]{3,2,1,0:T(8,128)} %adjoint_ref.2, f32[8]{0:T(128)S(1)} %broadcast_multiply_fusion), kind=kLoop, calls=%fused_computation.1 | loop fusion | flops 2490368 | bytes 4718624 | tf_op jit(solution)/shard_map/reduce_sum | solution.py:89
  4.4 0.0 copy-start.2
  4.4 5.5 %collective-permute-start.2 = (f32[2,8,64,128]{3,2,1,0:T(8,128)S(1)}, f32[2,8,64,128]{3,2,1,0:T(8,128)S(1)}, u32[]{:S(2)}, u32[]{:S(2)}) collective-permute-start(f32[2,8,64,128]{3,2,1,0:T(8,128)S(1)} %pad_maximum_fusion.own_ref), channel_id=1, source_target_pairs={{0,1},{1,0},{2,3},{3,2},{4,5},{5,4},{6,7},{7,6},{8,9},{9,8},{10,11... | collective-permute-start | bytes 1572872 | tf_op jit(solution)/shard_map/ppermute | solution.py:11
  9.8 0.0 copy-done
  9.8 0.0 copy-done.1
  9.8 0.1 fusion
  9.9 0.0 copy-done.2
  9.9 0.1 fusion.1
  10.1 4.9 %collective-permute-start.1 = (f32[2,8,1,64,128]{4,3,2,1,0:T(8,128)S(1)}, f32[2,8,1,64,128]{4,3,2,1,0:T(8,128)S(1)}, u32[]{:S(2)}, u32[]{:S(2)}) collective-permute-start(f32[2,8,1,64,128]{4,3,2,1,0:T(8,128)S(1)} %get-tuple-element.16), channel_id=1, source_target_pairs={{0,254},{2,0},{4,2},{6,4},{8,6},{10,8},{12,10},{14,12},{16,14},{18... | collective-permute-start | bytes 1572872 | tf_op jit(solution)/shard_map/ppermute | solution.py:11
  14.9 0.0 collective-permute-start
  14.9 0.6 %iota_add_fusion.index_ref = s32[8]{0:T(128)} fusion(s32[]{:T(128)S(6)} %mul.21), kind=kLoop, calls=%fused_computation.8 | loop fusion | flops 8 | bytes 36 | tf_op jit(solution)/shard_map/add | solution.py:86
  15.5 7.9 %shard_map.59 = (f32[8,6,64,128]{3,2,1,0:T(8,128)}, f32[8,6,64,128]{3,2,1,0:T(8,128)}) custom-call(f32[8]{0:T(128)} %rate_ref.3, s32[8]{0:T(128)} %iota_add_fusion.index_ref, s32[8,128]{1,0:T(8,128)} %labels_ref.3, f32[8,8,64,128]{3,2,1,0:T(8,128)} %order_ref.2, f32[8,8,64,128]{3,2,1,0:T(8,128)} %adjoint_ref.2), custom_call_target="tpu_custom_call" | custom-call | tf_op jit(solution)/shard_map/pallas_call | solution.py:100
  23.4 15.5 %collective-permute-done.2.other_ref = f32[2,8,64,128]{3,2,1,0:T(8,128)S(1)} collective-permute-done((f32[2,8,64,128]{3,2,1,0:T(8,128)S(1)}, f32[2,8,64,128]{3,2,1,0:T(8,128)S(1)}, u32[]{:S(2)}, u32[]{:S(2)}) %collective-permute-start.2) | collective-permute-done | bytes 524320 | tf_op jit(solution)/shard_map/ppermute | solution.py:11
  38.9 0.0 copy-start.3
  38.9 0.0 collective-permute-done.1.above_ref
  38.9 0.0 copy-start.4
  38.9 4.8 %collective-permute-done.below_ref = f32[2,8,1,64,128]{4,3,2,1,0:T(8,128)S(1)} collective-permute-done((f32[2,8,1,64,128]{4,3,2,1,0:T(8,128)S(1)}, f32[2,8,1,64,128]{4,3,2,1,0:T(8,128)S(1)}, u32[]{:S(2)}, u32[]{:S(2)}) %collective-permute-start) | collective-permute-done | bytes 524320 | tf_op jit(solution)/shard_map/ppermute | solution.py:11
  43.7 0.0 copy-start.5
  43.7 0.0 copy-done.3
  43.7 0.0 copy-done.4
  43.7 0.8 %copy-done.5 = f32[2,8,1,64,128]{4,3,2,1,0:T(8,128)} copy-done((f32[2,8,1,64,128]{4,3,2,1,0:T(8,128)}, f32[2,8,1,64,128]{4,3,2,1,0:T(8,128)S(1)}, u32[]{:S(2)}) %copy-start.5) | copy-done | bytes 524312
  44.5 8.9 %shard_map.60 = (f32[8,8,64,128]{3,2,1,0:T(8,128)}, f32[8,8,64,128]{3,2,1,0:T(8,128)}) custom-call(f32[8]{0:T(128)} %rate_ref.3, s32[8]{0:T(128)} %iota_add_fusion.index_ref, s32[8,128]{1,0:T(8,128)} %labels_ref.3, f32[8,8,64,128]{3,2,1,0:T(8,128)} %order_ref.2, f32[8,8,64,128]{3,2,1,0:T(8,128)} %adjoint_ref.2, f32[2,8,1,64,128]{4,3,2,1,0:T(8,128)} %copy-done.5, ...), custom_call_target="tpu_custom_call" | custom-call | tf_op jit(solution)/shard_map/pallas_call | solution.py:107
  (1 shorter events, 0.0 us)
Async XLA Ops:
  1.3 8.6 %copy-start = (f32[8,8,64,128]{3,2,1,0:T(8,128)S(1)}, f32[8,8,64,128]{3,2,1,0:T(8,128)}, u32[]{:S(2)}) copy-start(f32[8,8,64,128]{3,2,1,0:T(8,128)} %order_ref.2) | copy-start | bytes 6291460
  1.3 8.6 %copy-start.1 = (f32[8,8,64,128]{3,2,1,0:T(8,128)S(1)}, f32[8,8,64,128]{3,2,1,0:T(8,128)}, u32[]{:S(2)}) copy-start(f32[8,8,64,128]{3,2,1,0:T(8,128)} %adjoint_ref.2) | copy-start | bytes 6291460
  4.4 5.6 %copy-start.2 = (f32[2,8,64,128]{3,2,1,0:T(8,128)}, f32[2,8,64,128]{3,2,1,0:T(8,128)S(1)}, u32[]{:S(2)}) copy-start(f32[2,8,64,128]{3,2,1,0:T(8,128)S(1)} %pad_maximum_fusion.own_ref) | copy-start | bytes 1572868
  4.4 34.6 %collective-permute-start.2 = (f32[2,8,64,128]{3,2,1,0:T(8,128)S(1)}, f32[2,8,64,128]{3,2,1,0:T(8,128)S(1)}, u32[]{:S(2)}, u32[]{:S(2)}) collective-permute-start(f32[2,8,64,128]{3,2,1,0:T(8,128)S(1)} %pad_maximum_fusion.own_ref), channel_id=1, source_target_pairs={{0,1},{1,0},{2,3},{3,2},{4,5},{5,4},{6,7},{7,6},{8,9},{9,8},{10,11... | collective-permute-start | bytes 1572872 | tf_op jit(solution)/shard_map/ppermute | solution.py:11
  10.1 28.9 %collective-permute-start.1 = (f32[2,8,1,64,128]{4,3,2,1,0:T(8,128)S(1)}, f32[2,8,1,64,128]{4,3,2,1,0:T(8,128)S(1)}, u32[]{:S(2)}, u32[]{:S(2)}) collective-permute-start(f32[2,8,1,64,128]{4,3,2,1,0:T(8,128)S(1)} %get-tuple-element.16), channel_id=1, source_target_pairs={{0,254},{2,0},{4,2},{6,4},{8,6},{10,8},{12,10},{14,12},{16,14},{18... | collective-permute-start | bytes 1572872 | tf_op jit(solution)/shard_map/ppermute | solution.py:11
  14.9 28.8 %collective-permute-start = (f32[2,8,1,64,128]{4,3,2,1,0:T(8,128)S(1)}, f32[2,8,1,64,128]{4,3,2,1,0:T(8,128)S(1)}, u32[]{:S(2)}, u32[]{:S(2)}) collective-permute-start(f32[2,8,1,64,128]{4,3,2,1,0:T(8,128)S(1)} %get-tuple-element.17), channel_id=1, source_target_pairs={{0,2},{2,4},{4,6},{6,8},{8,10},{10,12},{12,14},{14,16},{16,18},{18... | collective-permute-start | bytes 1572872 | tf_op jit(solution)/shard_map/ppermute | solution.py:11
  38.9 4.8 %copy-start.3 = (f32[2,8,64,128]{3,2,1,0:T(8,128)}, f32[2,8,64,128]{3,2,1,0:T(8,128)S(1)}, u32[]{:S(2)}) copy-start(f32[2,8,64,128]{3,2,1,0:T(8,128)S(1)} %collective-permute-done.2.other_ref) | copy-start | bytes 1572868
  38.9 4.8 %copy-start.4 = (f32[2,8,1,64,128]{4,3,2,1,0:T(8,128)}, f32[2,8,1,64,128]{4,3,2,1,0:T(8,128)S(1)}, u32[]{:S(2)}) copy-start(f32[2,8,1,64,128]{4,3,2,1,0:T(8,128)S(1)} %collective-permute-done.1.above_ref) | copy-start | bytes 1572868
  43.7 0.8 %copy-start.5 = (f32[2,8,1,64,128]{4,3,2,1,0:T(8,128)}, f32[2,8,1,64,128]{4,3,2,1,0:T(8,128)S(1)}, u32[]{:S(2)}) copy-start(f32[2,8,1,64,128]{4,3,2,1,0:T(8,128)S(1)} %collective-permute-done.below_ref) | copy-start | bytes 1572868

commit v5 on v4

v5 whole, which is shorter than its diff:
```python
import jax
import jax.numpy as jnp
from jax import lax
from jax.experimental import pallas as pl
from jax.experimental.pallas import tpu as pltpu
from jax.sharding import PartitionSpec as P


def shift_along(cells, axis, step):
    count = lax.axis_size(axis)
    return lax.ppermute(cells, axis, [(i, (i + step) % count) for i in range(count)])


def stencil(depth, width):
    level = lax.broadcasted_iota(jnp.int32, (depth, width), 0)
    top = level == depth - 1
    bottom = level == 0

    def laplace(centre, beside):
        beside = beside + pltpu.roll(centre, 1, 1) + pltpu.roll(centre, width - 1, 1)
        upper = jnp.where(top, centre, pltpu.roll(centre, depth - 1, 0))
        lower = jnp.where(bottom, centre, pltpu.roll(centre, 1, 0))
        return beside + upper + lower - 6.0 * centre

    return laplace


def inner_kernel(rate_ref, index_ref, labels_ref, order_ref, adjoint_ref, inner_order_ref, inner_adjoint_ref):
    p = pl.program_id(0)
    rate = 0.1 * rate_ref[p]
    index = index_ref[p]
    _, rows, depth, width = order_ref.shape
    laplace = stencil(depth, width)

    def load(j):
        return order_ref[0, j], rate * adjoint_ref[0, j]

    prev = None
    cur = load(0)
    for j in range(rows):
        nxt = load(j + 1) if j + 1 < rows else None
        o, w = cur
        if prev is None:
            beside = nxt
        elif nxt is None:
            beside = prev
        else:
            beside = (prev[0] + nxt[0], prev[1] + nxt[1])
        sign = jnp.where(labels_ref[j : j + 1, :] != index, 1.0, -1.0)
        inner_order_ref[0, j] = sign * o - 2.0 * (o * o * o) - 0.5 * laplace(o, beside[0])
        inner_adjoint_ref[0, j] = (sign - 6.0 * o * o) * w - 0.5 * laplace(w, beside[1])
        prev, cur = cur, nxt


def final_kernel(rate_ref, order_ref, adjoint_ref, sums_ref, inner_order_ref, inner_adjoint_ref,
                 order_next_ref, adjoint_order_ref):
    p = pl.program_id(0)
    rate = 0.1 * rate_ref[p]
    rows = order_ref.shape[1]
    for j in range(rows):
        o = order_ref[0, j]
        adj = adjoint_ref[0, j]
        w = rate * adj
        squares = sums_ref[0, j]
        order_next_ref[0, j] = o - rate * (inner_order_ref[0, j] + o * squares)
        adjoint_order_ref[0, j] = adj - ((inner_adjoint_ref[0, j] + w * squares) + o * sums_ref[1, j])


def edge_kernel(rate_ref, below_ref, above_ref, order_next_in, adjoint_order_in, order_next_ref, adjoint_order_ref):
    side = pl.program_id(0)
    count = order_next_in.shape[0]
    for p in range(count):
        rate = 0.1 * rate_ref[p]
        order_row = jnp.where(side == 0, below_ref[0, p, 0], above_ref[0, p, 0])
        adjoint_row = jnp.where(side == 0, below_ref[1, p, 0], above_ref[1, p, 0])
        order_next_ref[p, 0] = order_next_in[p, 0] + (0.5 * rate) * order_row
        adjoint_order_ref[p, 0] = adjoint_order_in[p, 0] + 0.5 * (rate * adjoint_row)


def local(order_field, adjoint_next, mobility, labels):
    count, rows, depth, width = order_field.shape
    first = lax.axis_index("op") * count
    indices = first + jnp.arange(count, dtype=jnp.int32)
    rates = mobility[:, None, None, None]
    weighted = 0.1 * rates * adjoint_next
    own = jnp.stack([jnp.sum(order_field * order_field, axis=0), jnp.sum(order_field * weighted, axis=0)])
    other = shift_along(own, "op", 1)
    pair = jnp.stack([order_field, adjoint_next])
    edges = jnp.concatenate([pair[:, :, :1], pair[:, :, -1:]], axis=2)
    edges, own, order_late, adjoint_late = lax.optimization_barrier((edges, own, order_field, adjoint_next))
    below = shift_along(edges[:, :, 1:], "space", 1)
    above = shift_along(edges[:, :, :1], "space", -1)
    scalars = pltpu.PrefetchScalarGridSpec
    block = pl.BlockSpec((1, rows, depth, width), lambda p, *_: (p, 0, 0, 0))
    plane = pl.BlockSpec((rows, width), lambda p, *_: (0, 0))
    inner_order, inner_adjoint = pl.pallas_call(
        inner_kernel,
        grid_spec=scalars(num_scalar_prefetch=2, grid=(count,), in_specs=[plane, block, block], out_specs=[block, block]),
        out_shape=[jax.ShapeDtypeStruct(order_field.shape, jnp.float32)] * 2,
    )(mobility, indices, labels, order_late, adjoint_late)
    total = own + other
    sums = jnp.stack([3.0 * total[0], 6.0 * total[1]])
    whole = pl.BlockSpec((2, rows, depth, width), lambda p, *_: (0, 0, 0, 0))
    order_next, adjoint_order = pl.pallas_call(
        final_kernel,
        grid_spec=scalars(num_scalar_prefetch=1, grid=(count,), in_specs=[block, block, whole, block, block], out_specs=[block, block]),
        out_shape=[jax.ShapeDtypeStruct(order_field.shape, jnp.float32)] * 2,
    )(mobility, order_field, adjoint_next, sums, inner_order, inner_adjoint)
    halo = pl.BlockSpec((2, count, 1, depth, width), lambda s, *_: (0, 0, 0, 0, 0))
    row = pl.BlockSpec((count, 1, depth, width), lambda s, *_: (0, s * (rows - 1), 0, 0))
    return pl.pallas_call(
        edge_kernel,
        grid_spec=scalars(num_scalar_prefetch=1, grid=(2,), in_specs=[halo, halo, row, row], out_specs=[row, row]),
        out_shape=[jax.ShapeDtypeStruct(order_field.shape, jnp.float32)] * 2,
        input_output_aliases={3: 0, 4: 1},
    )(mobility, below, above, order_next, adjoint_order)


def solution(mesh):
    placed = (P("op", "space", None, None), P("op", "space", None, None), P("op"), P("space", None))
    return jax.shard_map(
        local,
        mesh=mesh,
        in_specs=placed,
        out_specs=(P("op", "space", None, None), P("op", "space", None, None)),
        check_vma=False,
    )
```

time: 54.3 us -> 53 us (0.976)
  waiting for transfers between devices: 20.3 us -> 15.1 us
  Pallas kernels: 16.8 us -> 20 us
  other arithmetic: 4.38 us -> 5.24 us
    ppermute x3, waiting for transfers between devices: 20.3 us -> 15.1 us  [shift_along(): lax.ppermute(cells, axis, [(i, (i + step) % count) for i in range(count)])]
    pallas_call x1 -> x2, Pallas kernels: 8.86 us -> 11.7 us  [the longest x1 8.56 us: local(): pl.pallas_call(final_kernel, grid_spec=scalars(num_scalar_prefetch=1, gri...]
    another operation x0 -> x1, other arithmetic: none -> 0.84 us  [local(): sums = jnp.stack([3.0 * total[0], 6.0 * total[1]])]
  transfers between devices with their start and end apart: 3 -> 3, of which waited for: 2 -> 1; matrix products, arithmetic and copies ran while one was open for 1% -> 3% of each run, Pallas kernels for 15% -> 32%
where the time goes in v5:
time: 53 us; the launch traced here: 52.5 us
  Pallas kernels  20 us (38%)
  waiting for transfers between devices  15.1 us (28%)
  starting transfers between devices  10.4 us (20%)
  other arithmetic  5.24 us (10%)
  local copies, waits for them, and re-layouts  1.06 us (2%)
  between operations  0.71 us (1%)
    ppermute x3, waiting for transfers between devices, shift_along(): lax.ppermute(cells, axis, [(i, (i + step) % count) for i in range(count)])  15.1 us
    ppermute x3, starting transfers between devices, shift_along(): lax.ppermute(cells, axis, [(i, (i + step) % count) for i in range(count)])  10.4 us
    pallas_call x1, Pallas kernels, local(): pl.pallas_call(final_kernel, grid_spec=scalars(num_scalar_prefetch=1, gri...  8.56 us
    pallas_call x1, Pallas kernels, local(): pl.pallas_call(inner_kernel, grid_spec=scalars(num_scalar_prefetch=2, gri...  8.35 us
    pallas_call x1, Pallas kernels, local(): pl.pallas_call(edge_kernel, grid_spec=scalars(num_scalar_prefetch=1, grid...  3.09 us
    reduce_sum x1, other arithmetic, local(): jnp.sum(order_field * order_field, axis=0)  3.01 us
  transfers between devices with their start and end apart: 3, of which 1 were waited for; matrix products, arithmetic and copies ran while one was open for 3% of the time, Pallas kernels for 32%

profile of v5, /device:TPU:64, one launch (start us, length us, event | category | flops | bytes accessed | tf_op | source)
XLA Modules:
  0.0 52.5 jit_solution(2691012587867868880)
XLA Ops:
  0.6 0.7 %broadcast_multiply_fusion = f32[8]{0:T(128)S(1)} fusion(f32[8]{0:T(128)} %rate_ref.5), kind=kLoop, calls=%fused_computation.12 | loop fusion | flops 8 | bytes 64 | tf_op jit(solution)/shard_map/mul | solution.py:85
  1.3 0.0 copy-start
  1.3 0.0 copy-start.1
  1.3 3.0 %multiply_reduce_fusion.1 = (f32[8,64,128]{2,1,0:T(8,128)S(1)}, f32[8,64,128]{2,1,0:T(8,128)S(1)}) fusion(f32[8,8,64,128]{3,2,1,0:T(8,128)} %order_ref.2, f32[8,8,64,128]{3,2,1,0:T(8,128)} %adjoint_ref.2, f32[8]{0:T(128)S(1)} %broadcast_multiply_fusion), kind=kLoop, calls=%fused_computation.1 | loop fusion | flops 2490368 | bytes 4718624 | tf_op jit(solution)/shard_map/reduce_sum | solution.py:86
  4.4 5.5 %collective-permute-start.2 = (f32[2,8,64,128]{3,2,1,0:T(8,128)S(1)}, f32[2,8,64,128]{3,2,1,0:T(8,128)S(1)}, u32[]{:S(2)}, u32[]{:S(2)}) collective-permute-start(f32[2,8,64,128]{3,2,1,0:T(8,128)S(1)} %pad_maximum_fusion), channel_id=1, source_target_pairs={{0,1},{1,0},{2,3},{3,2},{4,5},{5,4},{6,7},{7,6},{8,9},{9,8},{10,11... | collective-permute-start | bytes 1572872 | tf_op jit(solution)/shard_map/ppermute | solution.py:11
  9.8 0.0 copy-done
  9.8 0.0 copy-done.1
  9.8 0.1 fusion
  9.9 0.1 fusion.1
  10.0 4.9 %collective-permute-start.1 = (f32[2,8,1,64,128]{4,3,2,1,0:T(8,128)S(1)}, f32[2,8,1,64,128]{4,3,2,1,0:T(8,128)S(1)}, u32[]{:S(2)}, u32[]{:S(2)}) collective-permute-start(f32[2,8,1,64,128]{4,3,2,1,0:T(8,128)S(1)} %get-tuple-element.20), channel_id=1, source_target_pairs={{0,254},{2,0},{4,2},{6,4},{8,6},{10,8},{12,10},{14,12},{16,14},{18... | collective-permute-start | bytes 1572872 | tf_op jit(solution)/shard_map/ppermute | solution.py:11
  14.9 0.0 collective-permute-start
  14.9 0.5 iota_add_fusion.index_ref
  15.4 8.4 %shard_map.59 = (f32[8,8,64,128]{3,2,1,0:T(8,128)}, f32[8,8,64,128]{3,2,1,0:T(8,128)}) custom-call(f32[8]{0:T(128)} %rate_ref.5, s32[8]{0:T(128)} %iota_add_fusion.index_ref, s32[8,128]{1,0:T(8,128)} %labels_ref.1, f32[8,8,64,128]{3,2,1,0:T(8,128)} %order_ref.2, f32[8,8,64,128]{3,2,1,0:T(8,128)} %adjoint_ref.2), custom_call_target="tpu_custom_call" | custom-call | tf_op jit(solution)/shard_map/pallas_call | solution.py:96
  23.8 15.1 %collective-permute-done.2 = f32[2,8,64,128]{3,2,1,0:T(8,128)S(1)} collective-permute-done((f32[2,8,64,128]{3,2,1,0:T(8,128)S(1)}, f32[2,8,64,128]{3,2,1,0:T(8,128)S(1)}, u32[]{:S(2)}, u32[]{:S(2)}) %collective-permute-start.2) | collective-permute-done | bytes 524320 | tf_op jit(solution)/shard_map/ppermute | solution.py:11
  38.9 0.1 add.9
  39.0 0.8 %pad_maximum_fusion.1.sums_ref = f32[2,8,64,128]{3,2,1,0:T(8,128)} fusion(f32[1,8,64,128]{3,2,1,0:T(8,128)S(1)} %get-tuple-element.23, f32[1,8,64,128]{3,2,1,0:T(8,128)S(1)} %get-tuple-element.22), kind=kLoop, calls=%fused_computation.8 | loop fusion | flops 131072 | bytes 1048576 | tf_op jit(solution)/shard_map/stack | solution.py:102
  39.9 8.6 %shard_map.60 = (f32[8,8,64,128]{3,2,1,0:T(8,128)}, f32[8,8,64,128]{3,2,1,0:T(8,128)}) custom-call(f32[8]{0:T(128)} %rate_ref.5, f32[8,8,64,128]{3,2,1,0:T(8,128)} %order_ref.2, f32[8,8,64,128]{3,2,1,0:T(8,128)} %adjoint_ref.2, f32[2,8,64,128]{3,2,1,0:T(8,128)} %pad_maximum_fusion.1.sums_ref, f32[8,8,64,128]{3,2,1,0:T(8,128)} %get-tuple-element.14.inner_order_ref, ...), custom_call_target="tpu_custom_call" | custom-call | tf_op jit(solution)/shard_map/pallas_call | solution.py:104
  48.4 0.0 collective-permute-done.1.above_ref
  48.4 0.0 copy-start.2
  48.5 0.0 collective-permute-done.below_ref
  48.5 0.0 copy-start.3
  48.5 0.8 %copy-done.2 = f32[2,8,1,64,128]{4,3,2,1,0:T(8,128)} copy-done((f32[2,8,1,64,128]{4,3,2,1,0:T(8,128)}, f32[2,8,1,64,128]{4,3,2,1,0:T(8,128)S(1)}, u32[]{:S(2)}) %copy-start.2) | copy-done | bytes 524312
  49.2 0.2 copy-done.3
  49.4 3.1 %shard_map.61 = (f32[8,8,64,128]{3,2,1,0:T(8,128)}, f32[8,8,64,128]{3,2,1,0:T(8,128)}) custom-call(f32[8]{0:T(128)} %rate_ref.5, f32[2,8,1,64,128]{4,3,2,1,0:T(8,128)} %copy-done.3, f32[2,8,1,64,128]{4,3,2,1,0:T(8,128)} %copy-done.2, f32[8,8,64,128]{3,2,1,0:T(8,128)} %get-tuple-element.16.order_next_in, ...), custom_call_target="tpu_custom_call", output_to_operand_aliasing={{0}: (3, {}), {1}: (4, {})} | custom-call | tf_op jit(solution)/shard_map/pallas_call | solution.py:111
  (2 shorter events, 0.1 us)
Async XLA Ops:
  1.3 8.5 %copy-start = (f32[8,8,64,128]{3,2,1,0:T(8,128)S(1)}, f32[8,8,64,128]{3,2,1,0:T(8,128)}, u32[]{:S(2)}) copy-start(f32[8,8,64,128]{3,2,1,0:T(8,128)} %adjoint_ref.2) | copy-start | bytes 6291460
  1.3 8.5 %copy-start.1 = (f32[8,8,64,128]{3,2,1,0:T(8,128)S(1)}, f32[8,8,64,128]{3,2,1,0:T(8,128)}, u32[]{:S(2)}) copy-start(f32[8,8,64,128]{3,2,1,0:T(8,128)} %order_ref.2) | copy-start | bytes 6291460
  4.4 34.6 %collective-permute-start.2 = (f32[2,8,64,128]{3,2,1,0:T(8,128)S(1)}, f32[2,8,64,128]{3,2,1,0:T(8,128)S(1)}, u32[]{:S(2)}, u32[]{:S(2)}) collective-permute-start(f32[2,8,64,128]{3,2,1,0:T(8,128)S(1)} %pad_maximum_fusion), channel_id=1, source_target_pairs={{0,1},{1,0},{2,3},{3,2},{4,5},{5,4},{6,7},{7,6},{8,9},{9,8},{10,11... | collective-permute-start | bytes 1572872 | tf_op jit(solution)/shard_map/ppermute | solution.py:11
  10.0 38.4 %collective-permute-start.1 = (f32[2,8,1,64,128]{4,3,2,1,0:T(8,128)S(1)}, f32[2,8,1,64,128]{4,3,2,1,0:T(8,128)S(1)}, u32[]{:S(2)}, u32[]{:S(2)}) collective-permute-start(f32[2,8,1,64,128]{4,3,2,1,0:T(8,128)S(1)} %get-tuple-element.20), channel_id=1, source_target_pairs={{0,254},{2,0},{4,2},{6,4},{8,6},{10,8},{12,10},{14,12},{16,14},{18... | collective-permute-start | bytes 1572872 | tf_op jit(solution)/shard_map/ppermute | solution.py:11
  14.9 33.5 %collective-permute-start = (f32[2,8,1,64,128]{4,3,2,1,0:T(8,128)S(1)}, f32[2,8,1,64,128]{4,3,2,1,0:T(8,128)S(1)}, u32[]{:S(2)}, u32[]{:S(2)}) collective-permute-start(f32[2,8,1,64,128]{4,3,2,1,0:T(8,128)S(1)} %get-tuple-element.21), channel_id=1, source_target_pairs={{0,2},{2,4},{4,6},{6,8},{8,10},{10,12},{12,14},{14,16},{16,18},{18... | collective-permute-start | bytes 1572872 | tf_op jit(solution)/shard_map/ppermute | solution.py:11
  48.4 0.8 %copy-start.2 = (f32[2,8,1,64,128]{4,3,2,1,0:T(8,128)}, f32[2,8,1,64,128]{4,3,2,1,0:T(8,128)S(1)}, u32[]{:S(2)}) copy-start(f32[2,8,1,64,128]{4,3,2,1,0:T(8,128)S(1)} %collective-permute-done.1.above_ref) | copy-start | bytes 1572868
  48.5 1.0 %copy-start.3 = (f32[2,8,1,64,128]{4,3,2,1,0:T(8,128)}, f32[2,8,1,64,128]{4,3,2,1,0:T(8,128)S(1)}, u32[]{:S(2)}) copy-start(f32[2,8,1,64,128]{4,3,2,1,0:T(8,128)S(1)} %collective-permute-done.below_ref) | copy-start | bytes 1572868

commit v6 on v5

--- a/solution.py
+++ b/solution.py
@@ -106,14 +106,14 @@
         grid_spec=scalars(num_scalar_prefetch=1, grid=(count,), in_specs=[block, block, whole, block, block], out_specs=[block, block]),
         out_shape=[jax.ShapeDtypeStruct(order_field.shape, jnp.float32)] * 2,
     )(mobility, order_field, adjoint_next, sums, inner_order, inner_adjoint)
-    halo = pl.BlockSpec((2, count, 1, depth, width), lambda s, *_: (0, 0, 0, 0, 0))
+    on_chip = pl.BlockSpec(memory_space=pltpu.VMEM)
     row = pl.BlockSpec((count, 1, depth, width), lambda s, *_: (0, s * (rows - 1), 0, 0))
     return pl.pallas_call(
         edge_kernel,
-        grid_spec=scalars(num_scalar_prefetch=1, grid=(2,), in_specs=[halo, halo, row, row], out_specs=[row, row]),
+        grid_spec=scalars(num_scalar_prefetch=1, grid=(2,), in_specs=[on_chip, on_chip, row, row], out_specs=[row, row]),
         out_shape=[jax.ShapeDtypeStruct(order_field.shape, jnp.float32)] * 2,
         input_output_aliases={3: 0, 4: 1},
-    )(mobility, below, above, order_next, adjoint_order)
+    )(mobility, *[pltpu.with_memory_space_constraint(x, pltpu.VMEM) for x in (below, above)], order_next, adjoint_order)
 
 
 def solution(mesh):

time: 53 us -> 51.7 us (0.975)
  local copies, waits for them, and re-layouts: 1.06 us -> 0.11 us
    unnamed x8 -> x4, local copies, waits for them, and re-layouts: 0.96 us -> 0.01 us
  transfers between devices with their start and end apart: 3 -> 3, of which waited for: 1 -> 1; matrix products, arithmetic and copies ran while one was open for 3% -> 3% of each run, Pallas kernels for 32% -> 33%
where the time goes in v6:
time: 51.7 us; the launch traced here: 51.2 us
  Pallas kernels  19.7 us (38%)
  waiting for transfers between devices  15.1 us (29%)
  starting transfers between devices  10.4 us (20%)
  other arithmetic  5.25 us (10%)
  between operations  0.69 us (1%)
    ppermute x3, waiting for transfers between devices, shift_along(): lax.ppermute(cells, axis, [(i, (i + step) % count) for i in range(count)])  15.1 us
    ppermute x3, starting transfers between devices, shift_along(): lax.ppermute(cells, axis, [(i, (i + step) % count) for i in range(count)])  10.4 us
    pallas_call x1, Pallas kernels, local(): pl.pallas_call(final_kernel, grid_spec=scalars(num_scalar_prefetch=1, gri...  8.56 us
    pallas_call x1, Pallas kernels, local(): pl.pallas_call(inner_kernel, grid_spec=scalars(num_scalar_prefetch=2, gri...  8.37 us
    reduce_sum x1, other arithmetic, local(): jnp.sum(order_field * order_field, axis=0)  3.01 us
    pallas_call x1, Pallas kernels, local(): pl.pallas_call(edge_kernel, grid_spec=scalars(num_scalar_prefetch=1, grid...  2.75 us
  transfers between devices with their start and end apart: 3, of which 1 were waited for; matrix products, arithmetic and copies ran while one was open for 3% of the time, Pallas kernels for 33%

profile of v6, /device:TPU:64, one launch (start us, length us, event | category | flops | bytes accessed | tf_op | source)
XLA Modules:
  0.0 51.2 jit_solution(10789656952333383729)
XLA Ops:
  0.6 0.7 %broadcast_multiply_fusion = f32[8]{0:T(128)S(1)} fusion(f32[8]{0:T(128)} %rate_ref.5), kind=kLoop, calls=%fused_computation.12 | loop fusion | flops 8 | bytes 64 | tf_op jit(solution)/shard_map/mul | solution.py:85
  1.3 0.0 copy-start
  1.3 0.0 copy-start.1
  1.3 3.0 %multiply_reduce_fusion.1 = (f32[8,64,128]{2,1,0:T(8,128)S(1)}, f32[8,64,128]{2,1,0:T(8,128)S(1)}) fusion(f32[8,8,64,128]{3,2,1,0:T(8,128)} %order_ref.2, f32[8,8,64,128]{3,2,1,0:T(8,128)} %adjoint_ref.2, f32[8]{0:T(128)S(1)} %broadcast_multiply_fusion), kind=kLoop, calls=%fused_computation.1 | loop fusion | flops 2490368 | bytes 4718624 | tf_op jit(solution)/shard_map/reduce_sum | solution.py:86
  4.4 5.5 %collective-permute-start.2 = (f32[2,8,64,128]{3,2,1,0:T(8,128)S(1)}, f32[2,8,64,128]{3,2,1,0:T(8,128)S(1)}, u32[]{:S(2)}, u32[]{:S(2)}) collective-permute-start(f32[2,8,64,128]{3,2,1,0:T(8,128)S(1)} %pad_maximum_fusion), channel_id=1, source_target_pairs={{0,1},{1,0},{2,3},{3,2},{4,5},{5,4},{6,7},{7,6},{8,9},{9,8},{10,11... | collective-permute-start | bytes 1572872 | tf_op jit(solution)/shard_map/ppermute | solution.py:11
  9.8 0.0 copy-done
  9.8 0.0 copy-done.1
  9.8 0.1 fusion
  9.9 0.1 fusion.1
  10.0 4.9 %collective-permute-start.1 = (f32[2,8,1,64,128]{4,3,2,1,0:T(8,128)S(1)}, f32[2,8,1,64,128]{4,3,2,1,0:T(8,128)S(1)}, u32[]{:S(2)}, u32[]{:S(2)}) collective-permute-start(f32[2,8,1,64,128]{4,3,2,1,0:T(8,128)S(1)} %get-tuple-element.20), channel_id=1, source_target_pairs={{0,254},{2,0},{4,2},{6,4},{8,6},{10,8},{12,10},{14,12},{16,14},{18... | collective-permute-start | bytes 1572872 | tf_op jit(solution)/shard_map/ppermute | solution.py:11
  14.9 0.0 collective-permute-start
  14.9 0.5 %iota_add_fusion.index_ref = s32[8]{0:T(128)} fusion(s32[]{:T(128)S(6)} %mul.44), kind=kLoop, calls=%fused_computation.11 | loop fusion | flops 8 | bytes 36 | tf_op jit(solution)/shard_map/add | solution.py:83
  15.4 8.4 %shard_map.59 = (f32[8,8,64,128]{3,2,1,0:T(8,128)}, f32[8,8,64,128]{3,2,1,0:T(8,128)}) custom-call(f32[8]{0:T(128)} %rate_ref.5, s32[8]{0:T(128)} %iota_add_fusion.index_ref, s32[8,128]{1,0:T(8,128)} %labels_ref.1, f32[8,8,64,128]{3,2,1,0:T(8,128)} %order_ref.2, f32[8,8,64,128]{3,2,1,0:T(8,128)} %adjoint_ref.2), custom_call_target="tpu_custom_call" | custom-call | tf_op jit(solution)/shard_map/pallas_call | solution.py:96
  23.8 15.1 %collective-permute-done.2 = f32[2,8,64,128]{3,2,1,0:T(8,128)S(1)} collective-permute-done((f32[2,8,64,128]{3,2,1,0:T(8,128)S(1)}, f32[2,8,64,128]{3,2,1,0:T(8,128)S(1)}, u32[]{:S(2)}, u32[]{:S(2)}) %collective-permute-start.2) | collective-permute-done | bytes 524320 | tf_op jit(solution)/shard_map/ppermute | solution.py:11
  38.9 0.1 add.9
  39.0 0.9 %pad_maximum_fusion.1.sums_ref = f32[2,8,64,128]{3,2,1,0:T(8,128)} fusion(f32[1,8,64,128]{3,2,1,0:T(8,128)S(1)} %get-tuple-element.23, f32[1,8,64,128]{3,2,1,0:T(8,128)S(1)} %get-tuple-element.22), kind=kLoop, calls=%fused_computation.8 | loop fusion | flops 131072 | bytes 1048576 | tf_op jit(solution)/shard_map/stack | solution.py:102
  39.9 8.6 %shard_map.60 = (f32[8,8,64,128]{3,2,1,0:T(8,128)}, f32[8,8,64,128]{3,2,1,0:T(8,128)}) custom-call(f32[8]{0:T(128)} %rate_ref.5, f32[8,8,64,128]{3,2,1,0:T(8,128)} %order_ref.2, f32[8,8,64,128]{3,2,1,0:T(8,128)} %adjoint_ref.2, f32[2,8,64,128]{3,2,1,0:T(8,128)} %pad_maximum_fusion.1.sums_ref, f32[8,8,64,128]{3,2,1,0:T(8,128)} %get-tuple-element.14.inner_order_ref, ...), custom_call_target="tpu_custom_call" | custom-call | tf_op jit(solution)/shard_map/pallas_call | solution.py:104
  48.5 0.0 collective-permute-done.1.above_ref
  48.5 0.0 collective-permute-done.below_ref
  48.5 2.8 %shard_map.61 = (f32[8,8,64,128]{3,2,1,0:T(8,128)}, f32[8,8,64,128]{3,2,1,0:T(8,128)}) custom-call(f32[8]{0:T(128)} %rate_ref.5, f32[2,8,1,64,128]{4,3,2,1,0:T(8,128)S(1)} %collective-permute-done.below_ref, f32[2,8,1,64,128]{4,3,2,1,0:T(8,128)S(1)} %collective-permute-done.1.above_ref, ...), custom_call_target="tpu_custom_call", output_to_operand_aliasing={{0}: (3, {}), {1}: (4, {})} | custom-call | tf_op jit(solution)/shard_map/pallas_call | solution.py:111
  (2 shorter events, 0.1 us)
Async XLA Ops:
  1.3 8.5 %copy-start = (f32[8,8,64,128]{3,2,1,0:T(8,128)S(1)}, f32[8,8,64,128]{3,2,1,0:T(8,128)}, u32[]{:S(2)}) copy-start(f32[8,8,64,128]{3,2,1,0:T(8,128)} %adjoint_ref.2) | copy-start | bytes 6291460
  1.3 8.5 %copy-start.1 = (f32[8,8,64,128]{3,2,1,0:T(8,128)S(1)}, f32[8,8,64,128]{3,2,1,0:T(8,128)}, u32[]{:S(2)}) copy-start(f32[8,8,64,128]{3,2,1,0:T(8,128)} %order_ref.2) | copy-start | bytes 6291460
  4.4 34.6 %collective-permute-start.2 = (f32[2,8,64,128]{3,2,1,0:T(8,128)S(1)}, f32[2,8,64,128]{3,2,1,0:T(8,128)S(1)}, u32[]{:S(2)}, u32[]{:S(2)}) collective-permute-start(f32[2,8,64,128]{3,2,1,0:T(8,128)S(1)} %pad_maximum_fusion), channel_id=1, source_target_pairs={{0,1},{1,0},{2,3},{3,2},{4,5},{5,4},{6,7},{7,6},{8,9},{9,8},{10,11... | collective-permute-start | bytes 1572872 | tf_op jit(solution)/shard_map/ppermute | solution.py:11
  10.0 38.4 %collective-permute-start.1 = (f32[2,8,1,64,128]{4,3,2,1,0:T(8,128)S(1)}, f32[2,8,1,64,128]{4,3,2,1,0:T(8,128)S(1)}, u32[]{:S(2)}, u32[]{:S(2)}) collective-permute-start(f32[2,8,1,64,128]{4,3,2,1,0:T(8,128)S(1)} %get-tuple-element.20), channel_id=1, source_target_pairs={{0,254},{2,0},{4,2},{6,4},{8,6},{10,8},{12,10},{14,12},{16,14},{18... | collective-permute-start | bytes 1572872 | tf_op jit(solution)/shard_map/ppermute | solution.py:11
  14.9 33.6 %collective-permute-start = (f32[2,8,1,64,128]{4,3,2,1,0:T(8,128)S(1)}, f32[2,8,1,64,128]{4,3,2,1,0:T(8,128)S(1)}, u32[]{:S(2)}, u32[]{:S(2)}) collective-permute-start(f32[2,8,1,64,128]{4,3,2,1,0:T(8,128)S(1)} %get-tuple-element.21), channel_id=1, source_target_pairs={{0,2},{2,4},{4,6},{6,8},{8,10},{10,12},{12,14},{14,16},{16,18},{18... | collective-permute-start | bytes 1572872 | tf_op jit(solution)/shard_map/ppermute | solution.py:11

commit v7 on v6

--- a/solution.py
+++ b/solution.py
@@ -52,7 +52,21 @@
         prev, cur = cur, nxt
 
 
-def final_kernel(rate_ref, order_ref, adjoint_ref, sums_ref, inner_order_ref, inner_adjoint_ref,
+def sums_kernel(rate_ref, order_ref, adjoint_ref, own_ref):
+    count, rows = order_ref.shape[:2]
+    for j in range(rows):
+        squares = None
+        coupled = None
+        for p in range(count):
+            o = order_ref[p, j]
+            w = (0.1 * rate_ref[p]) * adjoint_ref[p, j]
+            squares = o * o if squares is None else squares + o * o
+            coupled = o * w if coupled is None else coupled + o * w
+        own_ref[0, j] = squares
+        own_ref[1, j] = coupled
+
+
+def final_kernel(rate_ref, order_ref, adjoint_ref, own_ref, other_ref, inner_order_ref, inner_adjoint_ref,
                  order_next_ref, adjoint_order_ref):
     p = pl.program_id(0)
     rate = 0.1 * rate_ref[p]
@@ -61,9 +75,10 @@
         o = order_ref[0, j]
         adj = adjoint_ref[0, j]
         w = rate * adj
-        squares = sums_ref[0, j]
+        squares = 3.0 * (own_ref[0, j] + other_ref[0, j])
+        coupled = 6.0 * (own_ref[1, j] + other_ref[1, j])
         order_next_ref[0, j] = o - rate * (inner_order_ref[0, j] + o * squares)
-        adjoint_order_ref[0, j] = adj - ((inner_adjoint_ref[0, j] + w * squares) + o * sums_ref[1, j])
+        adjoint_order_ref[0, j] = adj - ((inner_adjoint_ref[0, j] + w * squares) + o * coupled)
 
 
 def edge_kernel(rate_ref, below_ref, above_ref, order_next_in, adjoint_order_in, order_next_ref, adjoint_order_ref):
@@ -81,9 +96,18 @@
     count, rows, depth, width = order_field.shape
     first = lax.axis_index("op") * count
     indices = first + jnp.arange(count, dtype=jnp.int32)
-    rates = mobility[:, None, None, None]
-    weighted = 0.1 * rates * adjoint_next
-    own = jnp.stack([jnp.sum(order_field * order_field, axis=0), jnp.sum(order_field * weighted, axis=0)])
+    step = 2
+    chunk = pl.BlockSpec((count, step, depth, width), lambda r, *_: (0, r, 0, 0))
+    own = pl.pallas_call(
+        sums_kernel,
+        grid_spec=pltpu.PrefetchScalarGridSpec(
+            num_scalar_prefetch=1,
+            grid=(rows // step,),
+            in_specs=[chunk, chunk],
+            out_specs=pl.BlockSpec((2, step, depth, width), lambda r, *_: (0, r, 0, 0)),
+        ),
+        out_shape=jax.ShapeDtypeStruct((2, rows, depth, width), jnp.float32),
+    )(mobility, order_field, adjoint_next)
     other = shift_along(own, "op", 1)
     pair = jnp.stack([order_field, adjoint_next])
     edges = jnp.concatenate([pair[:, :, :1], pair[:, :, -1:]], axis=2)
@@ -98,15 +122,13 @@
         grid_spec=scalars(num_scalar_prefetch=2, grid=(count,), in_specs=[plane, block, block], out_specs=[block, block]),
         out_shape=[jax.ShapeDtypeStruct(order_field.shape, jnp.float32)] * 2,
     )(mobility, indices, labels, order_late, adjoint_late)
-    total = own + other
-    sums = jnp.stack([3.0 * total[0], 6.0 * total[1]])
-    whole = pl.BlockSpec((2, rows, depth, width), lambda p, *_: (0, 0, 0, 0))
+    on_chip = pl.BlockSpec(memory_space=pltpu.VMEM)
     order_next, adjoint_order = pl.pallas_call(
         final_kernel,
-        grid_spec=scalars(num_scalar_prefetch=1, grid=(count,), in_specs=[block, block, whole, block, block], out_specs=[block, block]),
+        grid_spec=scalars(num_scalar_prefetch=1, grid=(count,), in_specs=[block, block, on_chip, on_chip, block, block], out_specs=[block, block]),
         out_shape=[jax.ShapeDtypeStruct(order_field.shape, jnp.float32)] * 2,
-    )(mobility, order_field, adjoint_next, sums, inner_order, inner_adjoint)
-    on_chip = pl.BlockSpec(memory_space=pltpu.VMEM)
+    )(mobility, order_field, adjoint_next, *[pltpu.with_memory_space_constraint(x, pltpu.VMEM) for x in (own, other)],
+      inner_order, inner_adjoint)
     row = pl.BlockSpec((count, 1, depth, width), lambda s, *_: (0, s * (rows - 1), 0, 0))
     return pl.pallas_call(
         edge_kernel,

time: 51.7 us -> 51.9 us (level)
  Pallas kernels: 19.7 us -> 24.5 us
  other arithmetic: 5.25 us -> 1.8 us
  waiting for transfers between devices: 15.1 us -> 14 us
    pallas_call x0 -> x1, Pallas kernels: none -> 4.78 us  [local(): pl.pallas_call(sums_kernel, grid_spec=pltpu.PrefetchScalarGridSpec(num_sc...]
    reduce_sum x1 -> x0, other arithmetic: 3.01 us -> none  [local(): jnp.sum(order_field * order_field, axis=0)]
    concatenate x1, other arithmetic: 0.07 us -> 1.28 us  [local(): edges = jnp.concatenate([pair[:, :, :1], pair[:, :, -1:]], axis=2)]
    ppermute x3, waiting for transfers between devices: 15.1 us -> 14 us  [shift_along(): lax.ppermute(cells, axis, [(i, (i + step) % count) for i in range(count)])]
    another operation x2 -> x0, other arithmetic: 0.89 us -> none  [the longest x1 0.86 us: local(): sums = jnp.stack([3.0 * total[0], 6.0 * total[1]])]
    mul x2 -> x0, other arithmetic: 0.7 us -> none  [the longest x1 0.66 us: local(): weighted = 0.1 * rates * adjoint_next]
  transfers between devices with their start and end apart: 3 -> 3, of which waited for: 1 -> 1; matrix products, arithmetic and copies ran while one was open for 3% -> 4% of each run, Pallas kernels for 33% -> 33%
where the time goes in v7:
time: 51.9 us; the launch traced here: 51.3 us
  Pallas kernels  24.5 us (47%)
  waiting for transfers between devices  14 us (27%)
  starting transfers between devices  10.3 us (20%)
  other arithmetic  1.8 us (3%)
  between operations  0.66 us (1%)
    ppermute x3, waiting for transfers between devices, shift_along(): lax.ppermute(cells, axis, [(i, (i + step) % count) for i in range(count)])  14 us
    ppermute x3, starting transfers between devices, shift_along(): lax.ppermute(cells, axis, [(i, (i + step) % count) for i in range(count)])  10.3 us
    pallas_call x1, Pallas kernels, local(): pl.pallas_call(inner_kernel, grid_spec=scalars(num_scalar_prefetch=2, gri...  8.51 us
    pallas_call x1, Pallas kernels, local(): pl.pallas_call(final_kernel, grid_spec=scalars(num_scalar_prefetch=1, gri...  8.44 us
    pallas_call x1, Pallas kernels, local(): pl.pallas_call(sums_kernel, grid_spec=pltpu.PrefetchScalarGridSpec(num_sc...  4.78 us
    pallas_call x1, Pallas kernels, local(): pl.pallas_call(edge_kernel, grid_spec=scalars(num_scalar_prefetch=1, grid...  2.75 us
    concatenate x1, other arithmetic, local(): edges = jnp.concatenate([pair[:, :, :1], pair[:, :, -1:]], axis=2)  1.28 us
  transfers between devices with their start and end apart: 3, of which 1 were waited for; matrix products, arithmetic and copies ran while one was open for 4% of the time, Pallas kernels for 33%

profile of v7, /device:TPU:64, one launch (start us, length us, event | category | flops | bytes accessed | tf_op | source)
XLA Modules:
  0.0 51.3 jit_solution(5948342825664995941)
XLA Ops:
  0.6 0.0 copy-start.1
  0.6 4.8 %shard_map.59.own_ref = f32[2,8,64,128]{3,2,1,0:T(8,128)} custom-call(f32[8]{0:T(128)} %rate_ref.7, f32[8,8,64,128]{3,2,1,0:T(8,128)} %order_ref.4, f32[8,8,64,128]{3,2,1,0:T(8,128)} %adjoint_ref.4), custom_call_target="tpu_custom_call" | custom-call | tf_op jit(solution)/shard_map/pallas_call | solution.py:101
  5.4 5.4 %collective-permute-start.2 = (f32[2,8,64,128]{3,2,1,0:T(8,128)}, f32[2,8,64,128]{3,2,1,0:T(8,128)S(1)}, u32[]{:S(2)}, u32[]{:S(2)}) collective-permute-start(f32[2,8,64,128]{3,2,1,0:T(8,128)} %shard_map.59.own_ref), channel_id=1, source_target_pairs={{0,1},{1,0},{2,3},{3,2},{4,5},{5,4},{6,7},{7,6},{8,9},{9,8},{10,11... | collective-permute-start | bytes 1572872 | tf_op jit(solution)/shard_map/ppermute | solution.py:11
  10.8 0.0 copy-done.1
  10.8 1.3 %fusion = f32[2,8,2,64,128]{4,3,2,1,0:T(8,128)S(1)} fusion(f32[1,8,8,64,128]{4,3,2,1,0:T(8,128)S(1)} %bitcast.2, f32[1,8,8,64,128]{4,3,2,1,0:T(8,128)} %bitcast.3), kind=kLoop, calls=%fused_computation.1 | loop fusion | flops 2359296 | bytes 5242880 | tf_op jit(solution)/shard_map/concatenate | solution.py:113
  12.1 0.1 fusion.1
  12.2 4.9 %collective-permute-start.1 = (f32[2,8,1,64,128]{4,3,2,1,0:T(8,128)S(1)}, f32[2,8,1,64,128]{4,3,2,1,0:T(8,128)S(1)}, u32[]{:S(2)}, u32[]{:S(2)}) collective-permute-start(f32[2,8,1,64,128]{4,3,2,1,0:T(8,128)S(1)} %get-tuple-element.18), channel_id=1, source_target_pairs={{0,254},{2,0},{4,2},{6,4},{8,6},{10,8},{12,10},{14,12},{16,14},{18... | collective-permute-start | bytes 1572872 | tf_op jit(solution)/shard_map/ppermute | solution.py:11
  17.1 0.0 collective-permute-start
  17.1 0.5 iota_add_fusion.index_ref
  17.6 0.0 copy-start
  17.6 8.5 %shard_map.60 = (f32[8,8,64,128]{3,2,1,0:T(8,128)}, f32[8,8,64,128]{3,2,1,0:T(8,128)}) custom-call(f32[8]{0:T(128)} %rate_ref.7, s32[8]{0:T(128)} %iota_add_fusion.index_ref, s32[8,128]{1,0:T(8,128)} %labels_ref.1, f32[8,8,64,128]{3,2,1,0:T(8,128)} %order_ref.4, f32[8,8,64,128]{3,2,1,0:T(8,128)} %adjoint_ref.4), custom_call_target="tpu_custom_call" | custom-call | tf_op jit(solution)/shard_map/pallas_call | solution.py:120
  26.1 14.0 %collective-permute-done.2.other_ref = f32[2,8,64,128]{3,2,1,0:T(8,128)S(1)} collective-permute-done((f32[2,8,64,128]{3,2,1,0:T(8,128)}, f32[2,8,64,128]{3,2,1,0:T(8,128)S(1)}, u32[]{:S(2)}, u32[]{:S(2)}) %collective-permute-start.2) | collective-permute-done | bytes 524320 | tf_op jit(solution)/shard_map/ppermute | solution.py:11
  40.1 0.0 copy-done
  40.1 8.4 %shard_map.61 = (f32[8,8,64,128]{3,2,1,0:T(8,128)}, f32[8,8,64,128]{3,2,1,0:T(8,128)}) custom-call(f32[8]{0:T(128)} %rate_ref.7, f32[8,8,64,128]{3,2,1,0:T(8,128)} %order_ref.4, f32[8,8,64,128]{3,2,1,0:T(8,128)} %adjoint_ref.4, f32[2,8,64,128]{3,2,1,0:T(8,128)S(1)} %copy-done, f32[2,8,64,128]{3,2,1,0:T(8,128)S(1)} %collective-permute-done.2.other_ref, ...), custom_call_target="tpu_custom_call" | custom-call | tf_op jit(solution)/shard_map/pallas_call | solution.py:126
  48.6 0.0 collective-permute-done.1.above_ref
  48.6 0.0 collective-permute-done.below_ref
  48.6 2.8 %shard_map.62 = (f32[8,8,64,128]{3,2,1,0:T(8,128)}, f32[8,8,64,128]{3,2,1,0:T(8,128)}) custom-call(f32[8]{0:T(128)} %rate_ref.7, f32[2,8,1,64,128]{4,3,2,1,0:T(8,128)S(1)} %collective-permute-done.below_ref, f32[2,8,1,64,128]{4,3,2,1,0:T(8,128)S(1)} %collective-permute-done.1.above_ref, ...), custom_call_target="tpu_custom_call", output_to_operand_aliasing={{0}: (3, {}), {1}: (4, {})} | custom-call | tf_op jit(solution)/shard_map/pallas_call | solution.py:133
Async XLA Ops:
  0.6 10.2 %copy-start.1 = (f32[8,8,64,128]{3,2,1,0:T(8,128)S(1)}, f32[8,8,64,128]{3,2,1,0:T(8,128)}, u32[]{:S(2)}) copy-start(f32[8,8,64,128]{3,2,1,0:T(8,128)} %adjoint_ref.4) | copy-start | bytes 6291460
  5.4 34.7 %collective-permute-start.2 = (f32[2,8,64,128]{3,2,1,0:T(8,128)}, f32[2,8,64,128]{3,2,1,0:T(8,128)S(1)}, u32[]{:S(2)}, u32[]{:S(2)}) collective-permute-start(f32[2,8,64,128]{3,2,1,0:T(8,128)} %shard_map.59.own_ref), channel_id=1, source_target_pairs={{0,1},{1,0},{2,3},{3,2},{4,5},{5,4},{6,7},{7,6},{8,9},{9,8},{10,11... | collective-permute-start | bytes 1572872 | tf_op jit(solution)/shard_map/ppermute | solution.py:11
  12.2 36.3 %collective-permute-start.1 = (f32[2,8,1,64,128]{4,3,2,1,0:T(8,128)S(1)}, f32[2,8,1,64,128]{4,3,2,1,0:T(8,128)S(1)}, u32[]{:S(2)}, u32[]{:S(2)}) collective-permute-start(f32[2,8,1,64,128]{4,3,2,1,0:T(8,128)S(1)} %get-tuple-element.18), channel_id=1, source_target_pairs={{0,254},{2,0},{4,2},{6,4},{8,6},{10,8},{12,10},{14,12},{16,14},{18... | collective-permute-start | bytes 1572872 | tf_op jit(solution)/shard_map/ppermute | solution.py:11
  17.1 31.5 %collective-permute-start = (f32[2,8,1,64,128]{4,3,2,1,0:T(8,128)S(1)}, f32[2,8,1,64,128]{4,3,2,1,0:T(8,128)S(1)}, u32[]{:S(2)}, u32[]{:S(2)}) collective-permute-start(f32[2,8,1,64,128]{4,3,2,1,0:T(8,128)S(1)} %get-tuple-element.19), channel_id=1, source_target_pairs={{0,2},{2,4},{4,6},{6,8},{8,10},{10,12},{12,14},{14,16},{16,18},{18... | collective-permute-start | bytes 1572872 | tf_op jit(solution)/shard_map/ppermute | solution.py:11
  17.6 22.5 %copy-start = (f32[2,8,64,128]{3,2,1,0:T(8,128)S(1)}, f32[2,8,64,128]{3,2,1,0:T(8,128)}, u32[]{:S(2)}) copy-start(f32[2,8,64,128]{3,2,1,0:T(8,128)} %shard_map.59.own_ref) | copy-start | bytes 1572868

commit v8 on v6

--- a/solution.py
+++ b/solution.py
@@ -52,7 +52,7 @@
         prev, cur = cur, nxt
 
 
-def final_kernel(rate_ref, order_ref, adjoint_ref, sums_ref, inner_order_ref, inner_adjoint_ref,
+def final_kernel(rate_ref, order_ref, adjoint_ref, own_ref, other_ref, inner_order_ref, inner_adjoint_ref,
                  order_next_ref, adjoint_order_ref):
     p = pl.program_id(0)
     rate = 0.1 * rate_ref[p]
@@ -61,9 +61,10 @@
         o = order_ref[0, j]
         adj = adjoint_ref[0, j]
         w = rate * adj
-        squares = sums_ref[0, j]
+        squares = 3.0 * (own_ref[0, j] + other_ref[0, j])
+        coupled = 6.0 * (own_ref[1, j] + other_ref[1, j])
         order_next_ref[0, j] = o - rate * (inner_order_ref[0, j] + o * squares)
-        adjoint_order_ref[0, j] = adj - ((inner_adjoint_ref[0, j] + w * squares) + o * sums_ref[1, j])
+        adjoint_order_ref[0, j] = adj - ((inner_adjoint_ref[0, j] + w * squares) + o * coupled)
 
 
 def edge_kernel(rate_ref, below_ref, above_ref, order_next_in, adjoint_order_in, order_next_ref, adjoint_order_ref):
@@ -98,15 +99,13 @@
         grid_spec=scalars(num_scalar_prefetch=2, grid=(count,), in_specs=[plane, block, block], out_specs=[block, block]),
         out_shape=[jax.ShapeDtypeStruct(order_field.shape, jnp.float32)] * 2,
     )(mobility, indices, labels, order_late, adjoint_late)
-    total = own + other
-    sums = jnp.stack([3.0 * total[0], 6.0 * total[1]])
-    whole = pl.BlockSpec((2, rows, depth, width), lambda p, *_: (0, 0, 0, 0))
+    on_chip = pl.BlockSpec(memory_space=pltpu.VMEM)
     order_next, adjoint_order = pl.pallas_call(
         final_kernel,
-        grid_spec=scalars(num_scalar_prefetch=1, grid=(count,), in_specs=[block, block, whole, block, block], out_specs=[block, block]),
+        grid_spec=scalars(num_scalar_prefetch=1, grid=(count,), in_specs=[block, block, on_chip, on_chip, block, block], out_specs=[block, block]),
         out_shape=[jax.ShapeDtypeStruct(order_field.shape, jnp.float32)] * 2,
-    )(mobility, order_field, adjoint_next, sums, inner_order, inner_adjoint)
-    on_chip = pl.BlockSpec(memory_space=pltpu.VMEM)
+    )(mobility, order_field, adjoint_next, *[pltpu.with_memory_space_constraint(x, pltpu.VMEM) for x in (own, other)],
+      inner_order, inner_adjoint)
     row = pl.BlockSpec((count, 1, depth, width), lambda s, *_: (0, s * (rows - 1), 0, 0))
     return pl.pallas_call(
         edge_kernel,

time: 51.7 us -> 50.6 us (0.979)
  other arithmetic: 5.25 us -> 4.29 us
    another operation x1 -> x0, other arithmetic: 0.86 us -> none  [local(): sums = jnp.stack([3.0 * total[0], 6.0 * total[1]])]
  transfers between devices with their start and end apart: 3 -> 3, of which waited for: 1 -> 1; matrix products, arithmetic and copies ran while one was open for 3% -> 1% of each run, Pallas kernels for 33% -> 34%
where the time goes in v8:
time: 50.6 us; the launch traced here: 50.1 us
  Pallas kernels  19.6 us (39%)
  waiting for transfers between devices  15.1 us (30%)
  starting transfers between devices  10.4 us (21%)
  other arithmetic  4.29 us (8%)
  between operations  0.67 us (1%)
    ppermute x3, waiting for transfers between devices, shift_along(): lax.ppermute(cells, axis, [(i, (i + step) % count) for i in range(count)])  15.1 us
    ppermute x3, starting transfers between devices, shift_along(): lax.ppermute(cells, axis, [(i, (i + step) % count) for i in range(count)])  10.4 us
    pallas_call x1, Pallas kernels, local(): pl.pallas_call(final_kernel, grid_spec=scalars(num_scalar_prefetch=1, gri...  8.44 us
    pallas_call x1, Pallas kernels, local(): pl.pallas_call(inner_kernel, grid_spec=scalars(num_scalar_prefetch=2, gri...  8.41 us
    reduce_sum x1, other arithmetic, local(): jnp.sum(order_field * order_field, axis=0)  3.01 us
    pallas_call x1, Pallas kernels, local(): pl.pallas_call(edge_kernel, grid_spec=scalars(num_scalar_prefetch=1, grid...  2.75 us
  transfers between devices with their start and end apart: 3, of which 1 were waited for; matrix products, arithmetic and copies ran while one was open for 1% of the time, Pallas kernels for 34%

profile of v8, /device:TPU:64, one launch (start us, length us, event | category | flops | bytes accessed | tf_op | source)
XLA Modules:
  0.0 50.1 jit_solution(15282058364267242647)
XLA Ops:
  0.6 0.7 %broadcast_multiply_fusion = f32[8]{0:T(128)S(1)} fusion(f32[8]{0:T(128)} %rate_ref.5), kind=kLoop, calls=%fused_computation.9 | loop fusion | flops 8 | bytes 64 | tf_op jit(solution)/shard_map/mul | solution.py:86
  1.3 0.0 copy-start
  1.3 0.0 copy-start.1
  1.3 3.0 %multiply_reduce_fusion.1 = (f32[8,64,128]{2,1,0:T(8,128)S(1)}, f32[8,64,128]{2,1,0:T(8,128)S(1)}) fusion(f32[8,8,64,128]{3,2,1,0:T(8,128)} %order_ref.2, f32[8,8,64,128]{3,2,1,0:T(8,128)} %adjoint_ref.2, f32[8]{0:T(128)S(1)} %broadcast_multiply_fusion), kind=kLoop, calls=%fused_computation.1 | loop fusion | flops 2490368 | bytes 4718624 | tf_op jit(solution)/shard_map/reduce_sum | solution.py:87
  4.4 5.5 %collective-permute-start.2 = (f32[2,8,64,128]{3,2,1,0:T(8,128)S(1)}, f32[2,8,64,128]{3,2,1,0:T(8,128)S(1)}, u32[]{:S(2)}, u32[]{:S(2)}) collective-permute-start(f32[2,8,64,128]{3,2,1,0:T(8,128)S(1)} %pad_maximum_fusion.own_ref), channel_id=1, source_target_pairs={{0,1},{1,0},{2,3},{3,2},{4,5},{5,4},{6,7},{7,6},{8,9},{9,8},{10,11... | collective-permute-start | bytes 1572872 | tf_op jit(solution)/shard_map/ppermute | solution.py:11
  9.8 0.0 copy-done
  9.8 0.0 copy-done.1
  9.8 0.1 fusion
  9.9 0.1 fusion.1
  10.0 4.9 %collective-permute-start.1 = (f32[2,8,1,64,128]{4,3,2,1,0:T(8,128)S(1)}, f32[2,8,1,64,128]{4,3,2,1,0:T(8,128)S(1)}, u32[]{:S(2)}, u32[]{:S(2)}) collective-permute-start(f32[2,8,1,64,128]{4,3,2,1,0:T(8,128)S(1)} %get-tuple-element.20), channel_id=1, source_target_pairs={{0,254},{2,0},{4,2},{6,4},{8,6},{10,8},{12,10},{14,12},{16,14},{18... | collective-permute-start | bytes 1572872 | tf_op jit(solution)/shard_map/ppermute | solution.py:11
  14.9 0.0 collective-permute-start
  14.9 0.5 %iota_add_fusion.index_ref = s32[8]{0:T(128)} fusion(s32[]{:T(128)S(6)} %mul.26), kind=kLoop, calls=%fused_computation.8 | loop fusion | flops 8 | bytes 36 | tf_op jit(solution)/shard_map/add | solution.py:84
  15.4 8.4 %shard_map.59 = (f32[8,8,64,128]{3,2,1,0:T(8,128)}, f32[8,8,64,128]{3,2,1,0:T(8,128)}) custom-call(f32[8]{0:T(128)} %rate_ref.5, s32[8]{0:T(128)} %iota_add_fusion.index_ref, s32[8,128]{1,0:T(8,128)} %labels_ref.1, f32[8,8,64,128]{3,2,1,0:T(8,128)} %order_ref.2, f32[8,8,64,128]{3,2,1,0:T(8,128)} %adjoint_ref.2), custom_call_target="tpu_custom_call" | custom-call | tf_op jit(solution)/shard_map/pallas_call | solution.py:97
  23.8 15.1 %collective-permute-done.2.other_ref = f32[2,8,64,128]{3,2,1,0:T(8,128)S(1)} collective-permute-done((f32[2,8,64,128]{3,2,1,0:T(8,128)S(1)}, f32[2,8,64,128]{3,2,1,0:T(8,128)S(1)}, u32[]{:S(2)}, u32[]{:S(2)}) %collective-permute-start.2) | collective-permute-done | bytes 524320 | tf_op jit(solution)/shard_map/ppermute | solution.py:11
  38.9 8.4 %shard_map.60 = (f32[8,8,64,128]{3,2,1,0:T(8,128)}, f32[8,8,64,128]{3,2,1,0:T(8,128)}) custom-call(f32[8]{0:T(128)} %rate_ref.5, f32[8,8,64,128]{3,2,1,0:T(8,128)} %order_ref.2, f32[8,8,64,128]{3,2,1,0:T(8,128)} %adjoint_ref.2, f32[2,8,64,128]{3,2,1,0:T(8,128)S(1)} %pad_maximum_fusion.own_ref, f32[2,8,64,128]{3,2,1,0:T(8,128)S(1)} %collective-permute-done.2.other_ref, ...), custom_call_target="tpu_custom_call" | custom-call | tf_op jit(solution)/shard_map/pallas_call | solution.py:103
  47.4 0.0 collective-permute-done.1.above_ref
  47.4 0.0 collective-permute-done.below_ref
  47.4 2.8 %shard_map.61 = (f32[8,8,64,128]{3,2,1,0:T(8,128)}, f32[8,8,64,128]{3,2,1,0:T(8,128)}) custom-call(f32[8]{0:T(128)} %rate_ref.5, f32[2,8,1,64,128]{4,3,2,1,0:T(8,128)S(1)} %collective-permute-done.below_ref, f32[2,8,1,64,128]{4,3,2,1,0:T(8,128)S(1)} %collective-permute-done.1.above_ref, ...), custom_call_target="tpu_custom_call", output_to_operand_aliasing={{0}: (3, {}), {1}: (4, {})} | custom-call | tf_op jit(solution)/shard_map/pallas_call | solution.py:110
  (1 shorter events, 0.0 us)
Async XLA Ops:
  1.3 8.5 %copy-start = (f32[8,8,64,128]{3,2,1,0:T(8,128)S(1)}, f32[8,8,64,128]{3,2,1,0:T(8,128)}, u32[]{:S(2)}) copy-start(f32[8,8,64,128]{3,2,1,0:T(8,128)} %adjoint_ref.2) | copy-start | bytes 6291460
  1.3 8.5 %copy-start.1 = (f32[8,8,64,128]{3,2,1,0:T(8,128)S(1)}, f32[8,8,64,128]{3,2,1,0:T(8,128)}, u32[]{:S(2)}) copy-start(f32[8,8,64,128]{3,2,1,0:T(8,128)} %order_ref.2) | copy-start | bytes 6291460
  4.4 34.6 %collective-permute-start.2 = (f32[2,8,64,128]{3,2,1,0:T(8,128)S(1)}, f32[2,8,64,128]{3,2,1,0:T(8,128)S(1)}, u32[]{:S(2)}, u32[]{:S(2)}) collective-permute-start(f32[2,8,64,128]{3,2,1,0:T(8,128)S(1)} %pad_maximum_fusion.own_ref), channel_id=1, source_target_pairs={{0,1},{1,0},{2,3},{3,2},{4,5},{5,4},{6,7},{7,6},{8,9},{9,8},{10,11... | collective-permute-start | bytes 1572872 | tf_op jit(solution)/shard_map/ppermute | solution.py:11
  10.0 37.3 %collective-permute-start.1 = (f32[2,8,1,64,128]{4,3,2,1,0:T(8,128)S(1)}, f32[2,8,1,64,128]{4,3,2,1,0:T(8,128)S(1)}, u32[]{:S(2)}, u32[]{:S(2)}) collective-permute-start(f32[2,8,1,64,128]{4,3,2,1,0:T(8,128)S(1)} %get-tuple-element.20), channel_id=1, source_target_pairs={{0,254},{2,0},{4,2},{6,4},{8,6},{10,8},{12,10},{14,12},{16,14},{18... | collective-permute-start | bytes 1572872 | tf_op jit(solution)/shard_map/ppermute | solution.py:11
  14.9 32.5 %collective-permute-start = (f32[2,8,1,64,128]{4,3,2,1,0:T(8,128)S(1)}, f32[2,8,1,64,128]{4,3,2,1,0:T(8,128)S(1)}, u32[]{:S(2)}, u32[]{:S(2)}) collective-permute-start(f32[2,8,1,64,128]{4,3,2,1,0:T(8,128)S(1)} %get-tuple-element.21), channel_id=1, source_target_pairs={{0,2},{2,4},{4,6},{6,8},{8,10},{10,12},{12,14},{14,16},{16,18},{18... | collective-permute-start | bytes 1572872 | tf_op jit(solution)/shard_map/ppermute | solution.py:11

commit v9 on v8

--- a/solution.py
+++ b/solution.py
@@ -67,15 +67,31 @@
         adjoint_order_ref[0, j] = adj - ((inner_adjoint_ref[0, j] + w * squares) + o * coupled)
 
 
-def edge_kernel(rate_ref, below_ref, above_ref, order_next_in, adjoint_order_in, order_next_ref, adjoint_order_ref):
-    side = pl.program_id(0)
-    count = order_next_in.shape[0]
-    for p in range(count):
-        rate = 0.1 * rate_ref[p]
-        order_row = jnp.where(side == 0, below_ref[0, p, 0], above_ref[0, p, 0])
-        adjoint_row = jnp.where(side == 0, below_ref[1, p, 0], above_ref[1, p, 0])
-        order_next_ref[p, 0] = order_next_in[p, 0] + (0.5 * rate) * order_row
-        adjoint_order_ref[p, 0] = adjoint_order_in[p, 0] + 0.5 * (rate * adjoint_row)
+def edge_kernel(rate_ref, below_ref, above_ref, order_next_in, adjoint_order_in, order_next_ref, adjoint_order_ref,
+                rows_buf, load_sem, store_sem):
+    count, rows = order_next_in.shape[:2]
+    sides = (0, rows - 1)
+    loads = []
+    for a, source in enumerate((order_next_in, adjoint_order_in)):
+        for s, r in enumerate(sides):
+            copy = pltpu.make_async_copy(source.at[:, pl.ds(r, 1)], rows_buf.at[a, s], load_sem.at[a, s])
+            copy.start()
+            loads.append(copy)
+    for copy in loads:
+        copy.wait()
+    for s, halo in enumerate((below_ref, above_ref)):
+        for p in range(count):
+            rate = 0.1 * rate_ref[p]
+            rows_buf[0, s, p, 0] = rows_buf[0, s, p, 0] + (0.5 * rate) * halo[0, p, 0]
+            rows_buf[1, s, p, 0] = rows_buf[1, s, p, 0] + 0.5 * (rate * halo[1, p, 0])
+    stores = []
+    for a, target in enumerate((order_next_ref, adjoint_order_ref)):
+        for s, r in enumerate(sides):
+            copy = pltpu.make_async_copy(rows_buf.at[a, s], target.at[:, pl.ds(r, 1)], store_sem.at[a, s])
+            copy.start()
+            stores.append(copy)
+    for copy in stores:
+        copy.wait()
 
 
 def local(order_field, adjoint_next, mobility, labels):
@@ -106,11 +122,17 @@
         out_shape=[jax.ShapeDtypeStruct(order_field.shape, jnp.float32)] * 2,
     )(mobility, order_field, adjoint_next, *[pltpu.with_memory_space_constraint(x, pltpu.VMEM) for x in (own, other)],
       inner_order, inner_adjoint)
-    row = pl.BlockSpec((count, 1, depth, width), lambda s, *_: (0, s * (rows - 1), 0, 0))
+    anywhere = pl.BlockSpec(memory_space=pl.ANY)
     return pl.pallas_call(
         edge_kernel,
-        grid_spec=scalars(num_scalar_prefetch=1, grid=(2,), in_specs=[on_chip, on_chip, row, row], out_specs=[row, row]),
+        in_specs=[pl.BlockSpec(memory_space=pltpu.SMEM), on_chip, on_chip, anywhere, anywhere],
+        out_specs=[anywhere, anywhere],
         out_shape=[jax.ShapeDtypeStruct(order_field.shape, jnp.float32)] * 2,
+        scratch_shapes=[
+            pltpu.VMEM((2, 2, count, 1, depth, width), jnp.float32),
+            pltpu.SemaphoreType.DMA((2, 2)),
+            pltpu.SemaphoreType.DMA((2, 2)),
+        ],
         input_output_aliases={3: 0, 4: 1},
     )(mobility, *[pltpu.with_memory_space_constraint(x, pltpu.VMEM) for x in (below, above)], order_next, adjoint_order)
 

time: 50.6 us -> 50.8 us (level)
  transfers between devices with their start and end apart: 3 -> 3, of which waited for: 1 -> 1; matrix products, arithmetic and copies ran while one was open for 1% -> 1% of each run, Pallas kernels for 34% -> 33%
where the time goes in v9:
time: 50.8 us; the launch traced here: 50.4 us
  Pallas kernels  19.8 us (39%)
  waiting for transfers between devices  15.1 us (30%)
  starting transfers between devices  10.4 us (20%)
  other arithmetic  4.29 us (8%)
  between operations  0.67 us (1%)
    ppermute x3, waiting for transfers between devices, shift_along(): lax.ppermute(cells, axis, [(i, (i + step) % count) for i in range(count)])  15.1 us
    ppermute x3, starting transfers between devices, shift_along(): lax.ppermute(cells, axis, [(i, (i + step) % count) for i in range(count)])  10.4 us
    pallas_call x1, Pallas kernels, local(): pl.pallas_call(final_kernel, grid_spec=scalars(num_scalar_prefetch=1, gri...  8.44 us
    pallas_call x1, Pallas kernels, local(): pl.pallas_call(inner_kernel, grid_spec=scalars(num_scalar_prefetch=2, gri...  8.41 us
    reduce_sum x1, other arithmetic, local(): jnp.sum(order_field * order_field, axis=0)  3.01 us
    pallas_call x1, Pallas kernels, local(): pl.pallas_call(edge_kernel, in_specs=[pl.BlockSpec(memory_space=pltpu.SME...  2.99 us
  transfers between devices with their start and end apart: 3, of which 1 were waited for; matrix products, arithmetic and copies ran while one was open for 1% of the time, Pallas kernels for 33%

profile of v9, /device:TPU:64, one launch (start us, length us, event | category | flops | bytes accessed | tf_op | source)
XLA Modules:
  0.0 50.4 jit_solution(14617104202621741690)
XLA Ops:
  0.6 0.7 %broadcast_multiply_fusion = f32[8]{0:T(128)S(1)} fusion(f32[8]{0:T(128)} %rate_ref.5), kind=kLoop, calls=%fused_computation.9 | loop fusion | flops 8 | bytes 64 | tf_op jit(solution)/shard_map/mul | solution.py:102
  1.3 0.0 copy-start
  1.3 0.0 copy-start.1
  1.3 3.0 %multiply_reduce_fusion.1 = (f32[8,64,128]{2,1,0:T(8,128)S(1)}, f32[8,64,128]{2,1,0:T(8,128)S(1)}) fusion(f32[8,8,64,128]{3,2,1,0:T(8,128)} %order_ref.2, f32[8,8,64,128]{3,2,1,0:T(8,128)} %adjoint_ref.2, f32[8]{0:T(128)S(1)} %broadcast_multiply_fusion), kind=kLoop, calls=%fused_computation.1 | loop fusion | flops 2490368 | bytes 4718624 | tf_op jit(solution)/shard_map/reduce_sum | solution.py:103
  4.4 5.5 %collective-permute-start.2 = (f32[2,8,64,128]{3,2,1,0:T(8,128)S(1)}, f32[2,8,64,128]{3,2,1,0:T(8,128)S(1)}, u32[]{:S(2)}, u32[]{:S(2)}) collective-permute-start(f32[2,8,64,128]{3,2,1,0:T(8,128)S(1)} %pad_maximum_fusion.own_ref), channel_id=1, source_target_pairs={{0,1},{1,0},{2,3},{3,2},{4,5},{5,4},{6,7},{7,6},{8,9},{9,8},{10,11... | collective-permute-start | bytes 1572872 | tf_op jit(solution)/shard_map/ppermute | solution.py:11
  9.8 0.0 copy-done
  9.8 0.0 copy-done.1
  9.8 0.1 fusion
  9.9 0.1 fusion.1
  10.0 4.9 %collective-permute-start.1 = (f32[2,8,1,64,128]{4,3,2,1,0:T(8,128)S(1)}, f32[2,8,1,64,128]{4,3,2,1,0:T(8,128)S(1)}, u32[]{:S(2)}, u32[]{:S(2)}) collective-permute-start(f32[2,8,1,64,128]{4,3,2,1,0:T(8,128)S(1)} %get-tuple-element.20), channel_id=1, source_target_pairs={{0,254},{2,0},{4,2},{6,4},{8,6},{10,8},{12,10},{14,12},{16,14},{18... | collective-permute-start | bytes 1572872 | tf_op jit(solution)/shard_map/ppermute | solution.py:11
  14.9 0.0 collective-permute-start
  14.9 0.5 %iota_add_fusion.index_ref = s32[8]{0:T(128)} fusion(s32[]{:T(128)S(6)} %mul.26), kind=kLoop, calls=%fused_computation.8 | loop fusion | flops 8 | bytes 36 | tf_op jit(solution)/shard_map/add | solution.py:100
  15.4 8.4 %shard_map.59 = (f32[8,8,64,128]{3,2,1,0:T(8,128)}, f32[8,8,64,128]{3,2,1,0:T(8,128)}) custom-call(f32[8]{0:T(128)} %rate_ref.5, s32[8]{0:T(128)} %iota_add_fusion.index_ref, s32[8,128]{1,0:T(8,128)} %labels_ref.1, f32[8,8,64,128]{3,2,1,0:T(8,128)} %order_ref.2, f32[8,8,64,128]{3,2,1,0:T(8,128)} %adjoint_ref.2), custom_call_target="tpu_custom_call" | custom-call | tf_op jit(solution)/shard_map/pallas_call | solution.py:113
  23.8 15.1 %collective-permute-done.2.other_ref = f32[2,8,64,128]{3,2,1,0:T(8,128)S(1)} collective-permute-done((f32[2,8,64,128]{3,2,1,0:T(8,128)S(1)}, f32[2,8,64,128]{3,2,1,0:T(8,128)S(1)}, u32[]{:S(2)}, u32[]{:S(2)}) %collective-permute-start.2) | collective-permute-done | bytes 524320 | tf_op jit(solution)/shard_map/ppermute | solution.py:11
  38.9 8.4 %shard_map.60 = (f32[8,8,64,128]{3,2,1,0:T(8,128)}, f32[8,8,64,128]{3,2,1,0:T(8,128)}) custom-call(f32[8]{0:T(128)} %rate_ref.5, f32[8,8,64,128]{3,2,1,0:T(8,128)} %order_ref.2, f32[8,8,64,128]{3,2,1,0:T(8,128)} %adjoint_ref.2, f32[2,8,64,128]{3,2,1,0:T(8,128)S(1)} %pad_maximum_fusion.own_ref, f32[2,8,64,128]{3,2,1,0:T(8,128)S(1)} %collective-permute-done.2.other_ref, ...), custom_call_target="tpu_custom_call" | custom-call | tf_op jit(solution)/shard_map/pallas_call | solution.py:119
  47.4 0.0 collective-permute-done.1.above_ref
  47.4 0.0 collective-permute-done.below_ref
  47.4 3.0 %shard_map.61 = (f32[8,8,64,128]{3,2,1,0:T(8,128)}, f32[8,8,64,128]{3,2,1,0:T(8,128)}) custom-call(f32[8]{0:T(128)} %rate_ref.5, f32[2,8,1,64,128]{4,3,2,1,0:T(8,128)S(1)} %collective-permute-done.below_ref, f32[2,8,1,64,128]{4,3,2,1,0:T(8,128)S(1)} %collective-permute-done.1.above_ref, ...), custom_call_target="tpu_custom_call", output_to_operand_aliasing={{0}: (3, {}), {1}: (4, {})} | custom-call | tf_op jit(solution)/shard_map/pallas_call | solution.py:126
  (1 shorter events, 0.0 us)
Async XLA Ops:
  1.3 8.5 %copy-start = (f32[8,8,64,128]{3,2,1,0:T(8,128)S(1)}, f32[8,8,64,128]{3,2,1,0:T(8,128)}, u32[]{:S(2)}) copy-start(f32[8,8,64,128]{3,2,1,0:T(8,128)} %adjoint_ref.2) | copy-start | bytes 6291460
  1.3 8.5 %copy-start.1 = (f32[8,8,64,128]{3,2,1,0:T(8,128)S(1)}, f32[8,8,64,128]{3,2,1,0:T(8,128)}, u32[]{:S(2)}) copy-start(f32[8,8,64,128]{3,2,1,0:T(8,128)} %order_ref.2) | copy-start | bytes 6291460
  4.4 34.6 %collective-permute-start.2 = (f32[2,8,64,128]{3,2,1,0:T(8,128)S(1)}, f32[2,8,64,128]{3,2,1,0:T(8,128)S(1)}, u32[]{:S(2)}, u32[]{:S(2)}) collective-permute-start(f32[2,8,64,128]{3,2,1,0:T(8,128)S(1)} %pad_maximum_fusion.own_ref), channel_id=1, source_target_pairs={{0,1},{1,0},{2,3},{3,2},{4,5},{5,4},{6,7},{7,6},{8,9},{9,8},{10,11... | collective-permute-start | bytes 1572872 | tf_op jit(solution)/shard_map/ppermute | solution.py:11
  10.0 37.3 %collective-permute-start.1 = (f32[2,8,1,64,128]{4,3,2,1,0:T(8,128)S(1)}, f32[2,8,1,64,128]{4,3,2,1,0:T(8,128)S(1)}, u32[]{:S(2)}, u32[]{:S(2)}) collective-permute-start(f32[2,8,1,64,128]{4,3,2,1,0:T(8,128)S(1)} %get-tuple-element.20), channel_id=1, source_target_pairs={{0,254},{2,0},{4,2},{6,4},{8,6},{10,8},{12,10},{14,12},{16,14},{18... | collective-permute-start | bytes 1572872 | tf_op jit(solution)/shard_map/ppermute | solution.py:11
  14.9 32.5 %collective-permute-start = (f32[2,8,1,64,128]{4,3,2,1,0:T(8,128)S(1)}, f32[2,8,1,64,128]{4,3,2,1,0:T(8,128)S(1)}, u32[]{:S(2)}, u32[]{:S(2)}) collective-permute-start(f32[2,8,1,64,128]{4,3,2,1,0:T(8,128)S(1)} %get-tuple-element.21), channel_id=1, source_target_pairs={{0,2},{2,4},{4,6},{6,8},{8,10},{10,12},{12,14},{14,16},{16,18},{18... | collective-permute-start | bytes 1572872 | tf_op jit(solution)/shard_map/ppermute | solution.py:11

commit v10 on v8

--- a/solution.py
+++ b/solution.py
@@ -52,8 +52,8 @@
         prev, cur = cur, nxt
 
 
-def final_kernel(rate_ref, order_ref, adjoint_ref, own_ref, other_ref, inner_order_ref, inner_adjoint_ref,
-                 order_next_ref, adjoint_order_ref):
+def final_kernel(rate_ref, order_ref, adjoint_ref, own_ref, other_ref, inner_order_ref, inner_adjoint_ref, *refs):
+    order_next_ref, adjoint_order_ref = refs[-2:]
     p = pl.program_id(0)
     rate = 0.1 * rate_ref[p]
     rows = order_ref.shape[1]
@@ -84,11 +84,13 @@
     indices = first + jnp.arange(count, dtype=jnp.int32)
     rates = mobility[:, None, None, None]
     weighted = 0.1 * rates * adjoint_next
+    half = rows // 2
     own = jnp.stack([jnp.sum(order_field * order_field, axis=0), jnp.sum(order_field * weighted, axis=0)])
-    other = shift_along(own, "op", 1)
+    owns = [own[:, :half], own[:, half:]]
+    others = [shift_along(own, "op", 1) for own in owns]
     pair = jnp.stack([order_field, adjoint_next])
     edges = jnp.concatenate([pair[:, :, :1], pair[:, :, -1:]], axis=2)
-    edges, own, order_late, adjoint_late = lax.optimization_barrier((edges, own, order_field, adjoint_next))
+    edges, owns, order_late, adjoint_late = lax.optimization_barrier((edges, owns, order_field, adjoint_next))
     below = shift_along(edges[:, :, 1:], "space", 1)
     above = shift_along(edges[:, :, :1], "space", -1)
     scalars = pltpu.PrefetchScalarGridSpec
@@ -100,17 +102,34 @@
         out_shape=[jax.ShapeDtypeStruct(order_field.shape, jnp.float32)] * 2,
     )(mobility, indices, labels, order_late, adjoint_late)
     on_chip = pl.BlockSpec(memory_space=pltpu.VMEM)
-    order_next, adjoint_order = pl.pallas_call(
-        final_kernel,
-        grid_spec=scalars(num_scalar_prefetch=1, grid=(count,), in_specs=[block, block, on_chip, on_chip, block, block], out_specs=[block, block]),
-        out_shape=[jax.ShapeDtypeStruct(order_field.shape, jnp.float32)] * 2,
-    )(mobility, order_field, adjoint_next, *[pltpu.with_memory_space_constraint(x, pltpu.VMEM) for x in (own, other)],
-      inner_order, inner_adjoint)
+    cells = jax.ShapeDtypeStruct(order_field.shape, jnp.float32)
+    outputs = []
+    for h in range(2):
+        part = pl.BlockSpec((1, half, depth, width), lambda p, *_, h=h: (p, h, 0, 0))
+        extra = {}
+        if outputs:
+            extra = dict(input_output_aliases={7: 0, 8: 1})
+        outputs = pl.pallas_call(
+            final_kernel,
+            grid_spec=scalars(
+                num_scalar_prefetch=1,
+                grid=(count,),
+                in_specs=[part, part, on_chip, on_chip, part, part] + [pl.BlockSpec(memory_space=pl.ANY)] * len(outputs),
+                out_specs=[part, part],
+            ),
+            out_shape=[cells, cells],
+            **extra,
+        )(mobility, order_field, adjoint_next, *[pltpu.with_memory_space_constraint(x, pltpu.VMEM) for x in (owns[h], others[h])],
+          inner_order, inner_adjoint, *outputs)
+    order_next, adjoint_order = outputs
+    halo = pl.BlockSpec((2, count, 1, depth, width), lambda s, *_: (0, 0, 0, 0, 0))
     row = pl.BlockSpec((count, 1, depth, width), lambda s, *_: (0, s * (rows - 1), 0, 0))
     return pl.pallas_call(
         edge_kernel,
-        grid_spec=scalars(num_scalar_prefetch=1, grid=(2,), in_specs=[on_chip, on_chip, row, row], out_specs=[row, row]),
-        out_shape=[jax.ShapeDtypeStruct(order_field.shape, jnp.float32)] * 2,
+        grid_spec=scalars(
+            num_scalar_prefetch=1, grid=(2,), in_specs=[on_chip, on_chip, row, row], out_specs=[row, row]
+        ),
+        out_shape=[cells, cells],
         input_output_aliases={3: 0, 4: 1},
     )(mobility, *[pltpu.with_memory_space_constraint(x, pltpu.VMEM) for x in (below, above)], order_next, adjoint_order)
 

time: 50.6 us -> 57 us (1.13)
  the two profiles are of different devices: /device:TPU:64 before, /device:TPU:0 now
where the time goes in v10:
time: 57 us; the launch traced here: 56.5 us
  Pallas kernels  24.9 us (44%)
  waiting for transfers between devices  13.1 us (23%)
  starting transfers between devices  13 us (23%)
  other arithmetic  4.28 us (8%)
  between operations  0.68 us (1%)
    pallas_call x2, Pallas kernels, local(): pl.pallas_call(final_kernel, grid_spec=scalars(num_scalar_prefetch=1, gri...  13.8 us
    ppermute x4, waiting for transfers between devices, shift_along(): lax.ppermute(cells, axis, [(i, (i + step) % count) for i in range(count)])  13.1 us
    ppermute x4, starting transfers between devices, shift_along(): lax.ppermute(cells, axis, [(i, (i + step) % count) for i in range(count)])  13 us
    pallas_call x1, Pallas kernels, local(): pl.pallas_call(inner_kernel, grid_spec=scalars(num_scalar_prefetch=2, gri...  8.35 us
    reduce_sum x1, other arithmetic, local(): jnp.sum(order_field * weighted, axis=0)  3 us
    pallas_call x1, Pallas kernels, local(): pl.pallas_call(edge_kernel, grid_spec=scalars(num_scalar_prefetch=1, grid...  2.75 us
  transfers between devices with their start and end apart: 4, of which 1 were waited for; matrix products, arithmetic and copies ran while one was open for 1% of the time, Pallas kernels for 39%

profile of v10, /device:TPU:0, one launch (start us, length us, event | category | flops | bytes accessed | tf_op | source)
XLA Modules:
  0.0 56.5 jit_solution(40171485265244714)
XLA Ops:
  0.6 0.7 %broadcast_multiply_fusion = f32[8]{0:T(128)S(1)} fusion(f32[8]{0:T(128)} %rate_ref.7), kind=kLoop, calls=%fused_computation.12 | loop fusion | flops 8 | bytes 64 | tf_op jit(solution)/shard_map/mul | solution.py:86
  1.3 0.0 copy-start
  1.3 0.0 copy-start.1
  1.3 3.0 %multiply_reduce_fusion = (f32[8,64,128]{2,1,0:T(8,128)S(1)}, f32[8,64,128]{2,1,0:T(8,128)S(1)}) fusion(f32[8,8,64,128]{3,2,1,0:T(8,128)} %order_ref.4, f32[8,8,64,128]{3,2,1,0:T(8,128)} %adjoint_ref.4, f32[8]{0:T(128)S(1)} %broadcast_multiply_fusion), kind=kLoop, calls=%fused_computation | loop fusion | flops 2490368 | bytes 4718624 | tf_op jit(solution)/shard_map/reduce_sum | solution.py:88
  4.3 0.0 copy-done
  4.4 0.4 copy-done.1
  4.8 0.1 fusion
  4.8 0.1 fusion.2
  5.0 7.0 %collective-permute-start.1 = (f32[2,8,1,64,128]{4,3,2,1,0:T(8,128)S(1)}, f32[2,8,1,64,128]{4,3,2,1,0:T(8,128)S(1)}, u32[]{:S(2)}, u32[]{:S(2)}) collective-permute-start(f32[2,8,1,64,128]{4,3,2,1,0:T(8,128)S(1)} %get-tuple-element.26), channel_id=1, source_target_pairs={{0,254},{2,0},{4,2},{6,4},{8,6},{10,8},{12,10},{14,12},{16,14},{18... | collective-permute-start | bytes 1572872 | tf_op jit(solution)/shard_map/ppermute | solution.py:11
  12.0 0.0 collective-permute-start
  12.0 4.5 %collective-permute-start.3 = (f32[2,4,64,128]{3,2,1,0:T(8,128)S(1)}, f32[2,4,64,128]{3,2,1,0:T(8,128)S(1)}, u32[]{:S(2)}, u32[]{:S(2)}) collective-permute-start(f32[2,4,64,128]{3,2,1,0:T(8,128)S(1)} %get-tuple-element.19.own_ref), channel_id=1, source_target_pairs={{0,1},{1,0},{2,3},{3,2},{4,5},{5,4},{6,7},{7,6},{8,9},{9,8},{10,11... | collective-permute-start | bytes 786440 | tf_op jit(solution)/shard_map/ppermute | solution.py:11
  16.5 1.4 %collective-permute-start.2 = (f32[2,4,64,128]{3,2,1,0:T(8,128)S(1)}, f32[2,4,64,128]{3,2,1,0:T(8,128)S(1)}, u32[]{:S(2)}, u32[]{:S(2)}) collective-permute-start(f32[2,4,64,128]{3,2,1,0:T(8,128)S(1)} %get-tuple-element.14.own_ref), channel_id=1, source_target_pairs={{0,1},{1,0},{2,3},{3,2},{4,5},{5,4},{6,7},{7,6},{8,9},{9,8},{10,11... | collective-permute-start | bytes 786440 | tf_op jit(solution)/shard_map/ppermute | solution.py:11
  17.9 0.5 iota_add_fusion.index_ref
  18.5 8.4 %shard_map.59 = (f32[8,8,64,128]{3,2,1,0:T(8,128)}, f32[8,8,64,128]{3,2,1,0:T(8,128)}) custom-call(f32[8]{0:T(128)} %rate_ref.7, s32[8]{0:T(128)} %iota_add_fusion.index_ref, s32[8,128]{1,0:T(8,128)} %labels_ref.1, f32[8,8,64,128]{3,2,1,0:T(8,128)} %order_ref.4, f32[8,8,64,128]{3,2,1,0:T(8,128)} %adjoint_ref.4), custom_call_target="tpu_custom_call" | custom-call | tf_op jit(solution)/shard_map/pallas_call | solution.py:99
  26.8 13.1 %collective-permute-done.3.other_ref = f32[2,4,64,128]{3,2,1,0:T(8,128)S(1)} collective-permute-done((f32[2,4,64,128]{3,2,1,0:T(8,128)S(1)}, f32[2,4,64,128]{3,2,1,0:T(8,128)S(1)}, u32[]{:S(2)}, u32[]{:S(2)}) %collective-permute-start.3) | collective-permute-done | bytes 262176 | tf_op jit(solution)/shard_map/ppermute | solution.py:11
  39.9 6.9 %shard_map.60 = (f32[8,8,64,128]{3,2,1,0:T(8,128)}, f32[8,8,64,128]{3,2,1,0:T(8,128)}) custom-call(f32[8]{0:T(128)} %rate_ref.7, f32[8,8,64,128]{3,2,1,0:T(8,128)} %order_ref.4, f32[8,8,64,128]{3,2,1,0:T(8,128)} %adjoint_ref.4, f32[2,4,64,128]{3,2,1,0:T(8,128)S(1)} %get-tuple-element.19.own_ref, f32[2,4,64,128]{3,2,1,0:T(8,128)S(1)} %collective-permute-done.3.other_ref, ...), custom_call_target="tpu_custom_call" | custom-call | tf_op jit(solution)/shard_map/pallas_call | solution.py:112
  46.8 0.0 collective-permute-done.2.other_ref
  46.8 6.9 %shard_map.61 = (f32[8,8,64,128]{3,2,1,0:T(8,128)}, f32[8,8,64,128]{3,2,1,0:T(8,128)}) custom-call(f32[8]{0:T(128)} %rate_ref.7, f32[8,8,64,128]{3,2,1,0:T(8,128)} %order_ref.4, f32[8,8,64,128]{3,2,1,0:T(8,128)} %adjoint_ref.4, f32[2,4,64,128]{3,2,1,0:T(8,128)S(1)} %get-tuple-element.14.own_ref, ...), custom_call_target="tpu_custom_call", output_to_operand_aliasing={{0}: (7, {}), {1}: (8, {})} | custom-call | tf_op jit(solution)/shard_map/pallas_call | solution.py:112
  53.7 0.0 collective-permute-done.1.above_ref
  53.7 0.0 collective-permute-done.below_ref
  53.7 2.8 %shard_map.62 = (f32[8,8,64,128]{3,2,1,0:T(8,128)}, f32[8,8,64,128]{3,2,1,0:T(8,128)}) custom-call(f32[8]{0:T(128)} %rate_ref.7, f32[2,8,1,64,128]{4,3,2,1,0:T(8,128)S(1)} %collective-permute-done.below_ref, f32[2,8,1,64,128]{4,3,2,1,0:T(8,128)S(1)} %collective-permute-done.1.above_ref, ...), custom_call_target="tpu_custom_call", output_to_operand_aliasing={{0}: (3, {}), {1}: (4, {})} | custom-call | tf_op jit(solution)/shard_map/pallas_call | solution.py:127
  (1 shorter events, 0.0 us)
Async XLA Ops:
  1.3 3.1 %copy-start = (f32[8,8,64,128]{3,2,1,0:T(8,128)S(1)}, f32[8,8,64,128]{3,2,1,0:T(8,128)}, u32[]{:S(2)}) copy-start(f32[8,8,64,128]{3,2,1,0:T(8,128)} %adjoint_ref.4) | copy-start | bytes 6291460
  1.3 3.5 %copy-start.1 = (f32[8,8,64,128]{3,2,1,0:T(8,128)S(1)}, f32[8,8,64,128]{3,2,1,0:T(8,128)}, u32[]{:S(2)}) copy-start(f32[8,8,64,128]{3,2,1,0:T(8,128)} %order_ref.4) | copy-start | bytes 6291460
  5.0 48.7 %collective-permute-start.1 = (f32[2,8,1,64,128]{4,3,2,1,0:T(8,128)S(1)}, f32[2,8,1,64,128]{4,3,2,1,0:T(8,128)S(1)}, u32[]{:S(2)}, u32[]{:S(2)}) collective-permute-start(f32[2,8,1,64,128]{4,3,2,1,0:T(8,128)S(1)} %get-tuple-element.26), channel_id=1, source_target_pairs={{0,254},{2,0},{4,2},{6,4},{8,6},{10,8},{12,10},{14,12},{16,14},{18... | collective-permute-start | bytes 1572872 | tf_op jit(solution)/shard_map/ppermute | solution.py:11
  12.0 41.7 %collective-permute-start = (f32[2,8,1,64,128]{4,3,2,1,0:T(8,128)S(1)}, f32[2,8,1,64,128]{4,3,2,1,0:T(8,128)S(1)}, u32[]{:S(2)}, u32[]{:S(2)}) collective-permute-start(f32[2,8,1,64,128]{4,3,2,1,0:T(8,128)S(1)} %get-tuple-element.27), channel_id=1, source_target_pairs={{0,2},{2,4},{4,6},{6,8},{8,10},{10,12},{12,14},{14,16},{16,18},{18... | collective-permute-start | bytes 1572872 | tf_op jit(solution)/shard_map/ppermute | solution.py:11
  12.0 27.9 %collective-permute-start.3 = (f32[2,4,64,128]{3,2,1,0:T(8,128)S(1)}, f32[2,4,64,128]{3,2,1,0:T(8,128)S(1)}, u32[]{:S(2)}, u32[]{:S(2)}) collective-permute-start(f32[2,4,64,128]{3,2,1,0:T(8,128)S(1)} %get-tuple-element.19.own_ref), channel_id=1, source_target_pairs={{0,1},{1,0},{2,3},{3,2},{4,5},{5,4},{6,7},{7,6},{8,9},{9,8},{10,11... | collective-permute-start | bytes 786440 | tf_op jit(solution)/shard_map/ppermute | solution.py:11
  16.5 30.3 %collective-permute-start.2 = (f32[2,4,64,128]{3,2,1,0:T(8,128)S(1)}, f32[2,4,64,128]{3,2,1,0:T(8,128)S(1)}, u32[]{:S(2)}, u32[]{:S(2)}) collective-permute-start(f32[2,4,64,128]{3,2,1,0:T(8,128)S(1)} %get-tuple-element.14.own_ref), channel_id=1, source_target_pairs={{0,1},{1,0},{2,3},{3,2},{4,5},{5,4},{6,7},{7,6},{8,9},{9,8},{10,11... | collective-permute-start | bytes 786440 | tf_op jit(solution)/shard_map/ppermute | solution.py:11

commit v11 on v8

--- a/solution.py
+++ b/solution.py
@@ -26,14 +26,20 @@
 
 
 def inner_kernel(rate_ref, index_ref, labels_ref, order_ref, adjoint_ref, inner_order_ref, inner_adjoint_ref):
-    p = pl.program_id(0)
+    group = order_ref.shape[0]
+    for q in range(group):
+        inner_one(q, pl.program_id(0) * group + q, rate_ref, index_ref, labels_ref, order_ref, adjoint_ref,
+                  inner_order_ref, inner_adjoint_ref)
+
+
+def inner_one(q, p, rate_ref, index_ref, labels_ref, order_ref, adjoint_ref, inner_order_ref, inner_adjoint_ref):
     rate = 0.1 * rate_ref[p]
     index = index_ref[p]
     _, rows, depth, width = order_ref.shape
     laplace = stencil(depth, width)
 
     def load(j):
-        return order_ref[0, j], rate * adjoint_ref[0, j]
+        return order_ref[q, j], rate * adjoint_ref[q, j]
 
     prev = None
     cur = load(0)
@@ -47,24 +53,31 @@
         else:
             beside = (prev[0] + nxt[0], prev[1] + nxt[1])
         sign = jnp.where(labels_ref[j : j + 1, :] != index, 1.0, -1.0)
-        inner_order_ref[0, j] = sign * o - 2.0 * (o * o * o) - 0.5 * laplace(o, beside[0])
-        inner_adjoint_ref[0, j] = (sign - 6.0 * o * o) * w - 0.5 * laplace(w, beside[1])
+        inner_order_ref[q, j] = sign * o - 2.0 * (o * o * o) - 0.5 * laplace(o, beside[0])
+        inner_adjoint_ref[q, j] = (sign - 6.0 * o * o) * w - 0.5 * laplace(w, beside[1])
         prev, cur = cur, nxt
 
 
 def final_kernel(rate_ref, order_ref, adjoint_ref, own_ref, other_ref, inner_order_ref, inner_adjoint_ref,
                  order_next_ref, adjoint_order_ref):
-    p = pl.program_id(0)
+    group, rows = order_ref.shape[:2]
+    for q in range(group):
+        final_one(q, pl.program_id(0) * group + q, rate_ref, order_ref, adjoint_ref, own_ref, other_ref,
+                  inner_order_ref, inner_adjoint_ref, order_next_ref, adjoint_order_ref)
+
+
+def final_one(q, p, rate_ref, order_ref, adjoint_ref, own_ref, other_ref, inner_order_ref, inner_adjoint_ref,
+              order_next_ref, adjoint_order_ref):
     rate = 0.1 * rate_ref[p]
     rows = order_ref.shape[1]
     for j in range(rows):
-        o = order_ref[0, j]
-        adj = adjoint_ref[0, j]
+        o = order_ref[q, j]
+        adj = adjoint_ref[q, j]
         w = rate * adj
         squares = 3.0 * (own_ref[0, j] + other_ref[0, j])
         coupled = 6.0 * (own_ref[1, j] + other_ref[1, j])
-        order_next_ref[0, j] = o - rate * (inner_order_ref[0, j] + o * squares)
-        adjoint_order_ref[0, j] = adj - ((inner_adjoint_ref[0, j] + w * squares) + o * coupled)
+        order_next_ref[q, j] = o - rate * (inner_order_ref[q, j] + o * squares)
+        adjoint_order_ref[q, j] = adj - ((inner_adjoint_ref[q, j] + w * squares) + o * coupled)
 
 
 def edge_kernel(rate_ref, below_ref, above_ref, order_next_in, adjoint_order_in, order_next_ref, adjoint_order_ref):
@@ -92,17 +105,18 @@
     below = shift_along(edges[:, :, 1:], "space", 1)
     above = shift_along(edges[:, :, :1], "space", -1)
     scalars = pltpu.PrefetchScalarGridSpec
-    block = pl.BlockSpec((1, rows, depth, width), lambda p, *_: (p, 0, 0, 0))
+    group = 2
+    block = pl.BlockSpec((group, rows, depth, width), lambda p, *_: (p, 0, 0, 0))
     plane = pl.BlockSpec((rows, width), lambda p, *_: (0, 0))
     inner_order, inner_adjoint = pl.pallas_call(
         inner_kernel,
-        grid_spec=scalars(num_scalar_prefetch=2, grid=(count,), in_specs=[plane, block, block], out_specs=[block, block]),
+        grid_spec=scalars(num_scalar_prefetch=2, grid=(count // group,), in_specs=[plane, block, block], out_specs=[block, block]),
         out_shape=[jax.ShapeDtypeStruct(order_field.shape, jnp.float32)] * 2,
     )(mobility, indices, labels, order_late, adjoint_late)
     on_chip = pl.BlockSpec(memory_space=pltpu.VMEM)
     order_next, adjoint_order = pl.pallas_call(
         final_kernel,
-        grid_spec=scalars(num_scalar_prefetch=1, grid=(count,), in_specs=[block, block, on_chip, on_chip, block, block], out_specs=[block, block]),
+        grid_spec=scalars(num_scalar_prefetch=1, grid=(count // group,), in_specs=[block, block, on_chip, on_chip, block, block], out_specs=[block, block]),
         out_shape=[jax.ShapeDtypeStruct(order_field.shape, jnp.float32)] * 2,
     )(mobility, order_field, adjoint_next, *[pltpu.with_memory_space_constraint(x, pltpu.VMEM) for x in (own, other)],
       inner_order, inner_adjoint)

time: 50.6 us -> 48.6 us (0.960)
  Pallas kernels: 19.6 us -> 16 us
  waiting for transfers between devices: 15.1 us -> 16.9 us
    ppermute x3, waiting for transfers between devices: 15.1 us -> 16.9 us  [shift_along(): lax.ppermute(cells, axis, [(i, (i + step) % count) for i in range(count)])]
    pallas_call x1, Pallas kernels: 8.41 us -> 6.57 us  [local(): pl.pallas_call(inner_kernel, grid_spec=scalars(num_scalar_prefetch=2, gri...]
    pallas_call x1, Pallas kernels: 8.44 us -> 6.63 us  [local(): pl.pallas_call(final_kernel, grid_spec=scalars(num_scalar_prefetch=1, gri...]
  transfers between devices with their start and end apart: 3 -> 3, of which waited for: 1 -> 1; matrix products, arithmetic and copies ran while one was open for 1% -> 1% of each run, Pallas kernels for 34% -> 27%
where the time goes in v11:
time: 48.6 us; the launch traced here: 48.3 us
  waiting for transfers between devices  16.9 us (35%)
  Pallas kernels  16 us (33%)
  starting transfers between devices  10.4 us (21%)
  other arithmetic  4.29 us (9%)
  between operations  0.67 us (1%)
    ppermute x3, waiting for transfers between devices, shift_along(): lax.ppermute(cells, axis, [(i, (i + step) % count) for i in range(count)])  16.9 us
    ppermute x3, starting transfers between devices, shift_along(): lax.ppermute(cells, axis, [(i, (i + step) % count) for i in range(count)])  10.4 us
    pallas_call x1, Pallas kernels, local(): pl.pallas_call(final_kernel, grid_spec=scalars(num_scalar_prefetch=1, gri...  6.63 us
    pallas_call x1, Pallas kernels, local(): pl.pallas_call(inner_kernel, grid_spec=scalars(num_scalar_prefetch=2, gri...  6.57 us
    reduce_sum x1, other arithmetic, local(): jnp.sum(order_field * order_field, axis=0)  3.01 us
    pallas_call x1, Pallas kernels, local(): pl.pallas_call(edge_kernel, grid_spec=scalars(num_scalar_prefetch=1, grid...  2.75 us
  transfers between devices with their start and end apart: 3, of which 1 were waited for; matrix products, arithmetic and copies ran while one was open for 1% of the time, Pallas kernels for 27%

profile of v11, /device:TPU:64, one launch (start us, length us, event | category | flops | bytes accessed | tf_op | source)
XLA Modules:
  0.0 48.3 jit_solution(8161749231562721775)
XLA Ops:
  0.6 0.7 %broadcast_multiply_fusion = f32[8]{0:T(128)S(1)} fusion(f32[8]{0:T(128)} %rate_ref.5), kind=kLoop, calls=%fused_computation.9 | loop fusion | flops 8 | bytes 64 | tf_op jit(solution)/shard_map/mul | solution.py:99
  1.3 0.0 copy-start
  1.3 0.0 copy-start.1
  1.3 3.0 %multiply_reduce_fusion.1 = (f32[8,64,128]{2,1,0:T(8,128)S(1)}, f32[8,64,128]{2,1,0:T(8,128)S(1)}) fusion(f32[8,8,64,128]{3,2,1,0:T(8,128)} %order_ref.2, f32[8,8,64,128]{3,2,1,0:T(8,128)} %adjoint_ref.2, f32[8]{0:T(128)S(1)} %broadcast_multiply_fusion), kind=kLoop, calls=%fused_computation.1 | loop fusion | flops 2490368 | bytes 4718624 | tf_op jit(solution)/shard_map/reduce_sum | solution.py:100
  4.4 5.5 %collective-permute-start.2 = (f32[2,8,64,128]{3,2,1,0:T(8,128)S(1)}, f32[2,8,64,128]{3,2,1,0:T(8,128)S(1)}, u32[]{:S(2)}, u32[]{:S(2)}) collective-permute-start(f32[2,8,64,128]{3,2,1,0:T(8,128)S(1)} %pad_maximum_fusion.own_ref), channel_id=1, source_target_pairs={{0,1},{1,0},{2,3},{3,2},{4,5},{5,4},{6,7},{7,6},{8,9},{9,8},{10,11... | collective-permute-start | bytes 1572872 | tf_op jit(solution)/shard_map/ppermute | solution.py:11
  9.8 0.0 copy-done
  9.8 0.0 copy-done.1
  9.8 0.1 fusion
  9.9 0.1 fusion.1
  10.0 4.9 %collective-permute-start.1 = (f32[2,8,1,64,128]{4,3,2,1,0:T(8,128)S(1)}, f32[2,8,1,64,128]{4,3,2,1,0:T(8,128)S(1)}, u32[]{:S(2)}, u32[]{:S(2)}) collective-permute-start(f32[2,8,1,64,128]{4,3,2,1,0:T(8,128)S(1)} %get-tuple-element.20), channel_id=1, source_target_pairs={{0,254},{2,0},{4,2},{6,4},{8,6},{10,8},{12,10},{14,12},{16,14},{18... | collective-permute-start | bytes 1572872 | tf_op jit(solution)/shard_map/ppermute | solution.py:11
  14.9 0.0 collective-permute-start
  14.9 0.5 %iota_add_fusion.index_ref = s32[8]{0:T(128)} fusion(s32[]{:T(128)S(6)} %mul.26), kind=kLoop, calls=%fused_computation.8 | loop fusion | flops 8 | bytes 36 | tf_op jit(solution)/shard_map/add | solution.py:97
  15.4 6.6 %shard_map.59 = (f32[8,8,64,128]{3,2,1,0:T(8,128)}, f32[8,8,64,128]{3,2,1,0:T(8,128)}) custom-call(f32[8]{0:T(128)} %rate_ref.5, s32[8]{0:T(128)} %iota_add_fusion.index_ref, s32[8,128]{1,0:T(8,128)} %labels_ref.1, f32[8,8,64,128]{3,2,1,0:T(8,128)} %order_ref.2, f32[8,8,64,128]{3,2,1,0:T(8,128)} %adjoint_ref.2), custom_call_target="tpu_custom_call" | custom-call | tf_op jit(solution)/shard_map/pallas_call | solution.py:111
  22.0 16.9 %collective-permute-done.2.other_ref = f32[2,8,64,128]{3,2,1,0:T(8,128)S(1)} collective-permute-done((f32[2,8,64,128]{3,2,1,0:T(8,128)S(1)}, f32[2,8,64,128]{3,2,1,0:T(8,128)S(1)}, u32[]{:S(2)}, u32[]{:S(2)}) %collective-permute-start.2) | collective-permute-done | bytes 524320 | tf_op jit(solution)/shard_map/ppermute | solution.py:11
  38.9 6.6 %shard_map.60 = (f32[8,8,64,128]{3,2,1,0:T(8,128)}, f32[8,8,64,128]{3,2,1,0:T(8,128)}) custom-call(f32[8]{0:T(128)} %rate_ref.5, f32[8,8,64,128]{3,2,1,0:T(8,128)} %order_ref.2, f32[8,8,64,128]{3,2,1,0:T(8,128)} %adjoint_ref.2, f32[2,8,64,128]{3,2,1,0:T(8,128)S(1)} %pad_maximum_fusion.own_ref, f32[2,8,64,128]{3,2,1,0:T(8,128)S(1)} %collective-permute-done.2.other_ref, ...), custom_call_target="tpu_custom_call" | custom-call | tf_op jit(solution)/shard_map/pallas_call | solution.py:117
  45.6 0.0 collective-permute-done.1.above_ref
  45.6 0.0 collective-permute-done.below_ref
  45.6 2.8 %shard_map.61 = (f32[8,8,64,128]{3,2,1,0:T(8,128)}, f32[8,8,64,128]{3,2,1,0:T(8,128)}) custom-call(f32[8]{0:T(128)} %rate_ref.5, f32[2,8,1,64,128]{4,3,2,1,0:T(8,128)S(1)} %collective-permute-done.below_ref, f32[2,8,1,64,128]{4,3,2,1,0:T(8,128)S(1)} %collective-permute-done.1.above_ref, ...), custom_call_target="tpu_custom_call", output_to_operand_aliasing={{0}: (3, {}), {1}: (4, {})} | custom-call | tf_op jit(solution)/shard_map/pallas_call | solution.py:124
  (1 shorter events, 0.0 us)
Async XLA Ops:
  1.3 8.5 %copy-start = (f32[8,8,64,128]{3,2,1,0:T(8,128)S(1)}, f32[8,8,64,128]{3,2,1,0:T(8,128)}, u32[]{:S(2)}) copy-start(f32[8,8,64,128]{3,2,1,0:T(8,128)} %adjoint_ref.2) | copy-start | bytes 6291460
  1.3 8.5 %copy-start.1 = (f32[8,8,64,128]{3,2,1,0:T(8,128)S(1)}, f32[8,8,64,128]{3,2,1,0:T(8,128)}, u32[]{:S(2)}) copy-start(f32[8,8,64,128]{3,2,1,0:T(8,128)} %order_ref.2) | copy-start | bytes 6291460
  4.4 34.6 %collective-permute-start.2 = (f32[2,8,64,128]{3,2,1,0:T(8,128)S(1)}, f32[2,8,64,128]{3,2,1,0:T(8,128)S(1)}, u32[]{:S(2)}, u32[]{:S(2)}) collective-permute-start(f32[2,8,64,128]{3,2,1,0:T(8,128)S(1)} %pad_maximum_fusion.own_ref), channel_id=1, source_target_pairs={{0,1},{1,0},{2,3},{3,2},{4,5},{5,4},{6,7},{7,6},{8,9},{9,8},{10,11... | collective-permute-start | bytes 1572872 | tf_op jit(solution)/shard_map/ppermute | solution.py:11
  10.0 35.5 %collective-permute-start.1 = (f32[2,8,1,64,128]{4,3,2,1,0:T(8,128)S(1)}, f32[2,8,1,64,128]{4,3,2,1,0:T(8,128)S(1)}, u32[]{:S(2)}, u32[]{:S(2)}) collective-permute-start(f32[2,8,1,64,128]{4,3,2,1,0:T(8,128)S(1)} %get-tuple-element.20), channel_id=1, source_target_pairs={{0,254},{2,0},{4,2},{6,4},{8,6},{10,8},{12,10},{14,12},{16,14},{18... | collective-permute-start | bytes 1572872 | tf_op jit(solution)/shard_map/ppermute | solution.py:11
  14.9 30.6 %collective-permute-start = (f32[2,8,1,64,128]{4,3,2,1,0:T(8,128)S(1)}, f32[2,8,1,64,128]{4,3,2,1,0:T(8,128)S(1)}, u32[]{:S(2)}, u32[]{:S(2)}) collective-permute-start(f32[2,8,1,64,128]{4,3,2,1,0:T(8,128)S(1)} %get-tuple-element.21), channel_id=1, source_target_pairs={{0,2},{2,4},{4,6},{6,8},{8,10},{10,12},{12,14},{14,16},{16,18},{18... | collective-permute-start | bytes 1572872 | tf_op jit(solution)/shard_map/ppermute | solution.py:11

commit v12 on v11

--- a/solution.py
+++ b/solution.py
@@ -105,7 +105,7 @@
     below = shift_along(edges[:, :, 1:], "space", 1)
     above = shift_along(edges[:, :, :1], "space", -1)
     scalars = pltpu.PrefetchScalarGridSpec
-    group = 2
+    group = 4
     block = pl.BlockSpec((group, rows, depth, width), lambda p, *_: (p, 0, 0, 0))
     plane = pl.BlockSpec((rows, width), lambda p, *_: (0, 0))
     inner_order, inner_adjoint = pl.pallas_call(

time: 48.6 us -> 47.7 us (0.981)
  Pallas kernels: 16 us -> 14.8 us
    pallas_call x1, Pallas kernels: 6.63 us -> 5.88 us  [local(): pl.pallas_call(final_kernel, grid_spec=scalars(num_scalar_prefetch=1, gri...]
  transfers between devices with their start and end apart: 3 -> 3, of which waited for: 1 -> 1; matrix products, arithmetic and copies ran while one was open for 1% -> 1% of each run, Pallas kernels for 27% -> 25%
where the time goes in v12:
time: 47.7 us; the launch traced here: 47.6 us
  waiting for transfers between devices  17.3 us (36%)
  Pallas kernels  14.8 us (31%)
  starting transfers between devices  10.4 us (22%)
  other arithmetic  4.29 us (9%)
  between operations  0.67 us (1%)
    ppermute x3, waiting for transfers between devices, shift_along(): lax.ppermute(cells, axis, [(i, (i + step) % count) for i in range(count)])  17.3 us
    ppermute x3, starting transfers between devices, shift_along(): lax.ppermute(cells, axis, [(i, (i + step) % count) for i in range(count)])  10.4 us
    pallas_call x1, Pallas kernels, local(): pl.pallas_call(inner_kernel, grid_spec=scalars(num_scalar_prefetch=2, gri...  6.16 us
    pallas_call x1, Pallas kernels, local(): pl.pallas_call(final_kernel, grid_spec=scalars(num_scalar_prefetch=1, gri...  5.88 us
    reduce_sum x1, other arithmetic, local(): jnp.sum(order_field * order_field, axis=0)  3.01 us
    pallas_call x1, Pallas kernels, local(): pl.pallas_call(edge_kernel, grid_spec=scalars(num_scalar_prefetch=1, grid...  2.75 us
  transfers between devices with their start and end apart: 3, of which 1 were waited for; matrix products, arithmetic and copies ran while one was open for 1% of the time, Pallas kernels for 25%

profile of v12, /device:TPU:64, one launch (start us, length us, event | category | flops | bytes accessed | tf_op | source)
XLA Modules:
  0.0 47.6 jit_solution(11972454959700054074)
XLA Ops:
  0.6 0.7 %broadcast_multiply_fusion = f32[8]{0:T(128)S(1)} fusion(f32[8]{0:T(128)} %rate_ref.5), kind=kLoop, calls=%fused_computation.9 | loop fusion | flops 8 | bytes 64 | tf_op jit(solution)/shard_map/mul | solution.py:99
  1.3 0.0 copy-start
  1.3 0.0 copy-start.1
  1.3 3.0 %multiply_reduce_fusion.1 = (f32[8,64,128]{2,1,0:T(8,128)S(1)}, f32[8,64,128]{2,1,0:T(8,128)S(1)}) fusion(f32[8,8,64,128]{3,2,1,0:T(8,128)} %order_ref.2, f32[8,8,64,128]{3,2,1,0:T(8,128)} %adjoint_ref.2, f32[8]{0:T(128)S(1)} %broadcast_multiply_fusion), kind=kLoop, calls=%fused_computation.1 | loop fusion | flops 2490368 | bytes 4718624 | tf_op jit(solution)/shard_map/reduce_sum | solution.py:100
  4.4 5.5 %collective-permute-start.2 = (f32[2,8,64,128]{3,2,1,0:T(8,128)S(1)}, f32[2,8,64,128]{3,2,1,0:T(8,128)S(1)}, u32[]{:S(2)}, u32[]{:S(2)}) collective-permute-start(f32[2,8,64,128]{3,2,1,0:T(8,128)S(1)} %pad_maximum_fusion.own_ref), channel_id=1, source_target_pairs={{0,1},{1,0},{2,3},{3,2},{4,5},{5,4},{6,7},{7,6},{8,9},{9,8},{10,11... | collective-permute-start | bytes 1572872 | tf_op jit(solution)/shard_map/ppermute | solution.py:11
  9.8 0.0 copy-done
  9.8 0.0 copy-done.1
  9.8 0.1 fusion
  9.9 0.1 fusion.1
  10.0 4.9 %collective-permute-start.1 = (f32[2,8,1,64,128]{4,3,2,1,0:T(8,128)S(1)}, f32[2,8,1,64,128]{4,3,2,1,0:T(8,128)S(1)}, u32[]{:S(2)}, u32[]{:S(2)}) collective-permute-start(f32[2,8,1,64,128]{4,3,2,1,0:T(8,128)S(1)} %get-tuple-element.20), channel_id=1, source_target_pairs={{0,254},{2,0},{4,2},{6,4},{8,6},{10,8},{12,10},{14,12},{16,14},{18... | collective-permute-start | bytes 1572872 | tf_op jit(solution)/shard_map/ppermute | solution.py:11
  14.9 0.0 collective-permute-start
  14.9 0.5 %iota_add_fusion.index_ref = s32[8]{0:T(128)} fusion(s32[]{:T(128)S(6)} %mul.26), kind=kLoop, calls=%fused_computation.8 | loop fusion | flops 8 | bytes 36 | tf_op jit(solution)/shard_map/add | solution.py:97
  15.4 6.2 %shard_map.59 = (f32[8,8,64,128]{3,2,1,0:T(8,128)}, f32[8,8,64,128]{3,2,1,0:T(8,128)}) custom-call(f32[8]{0:T(128)} %rate_ref.5, s32[8]{0:T(128)} %iota_add_fusion.index_ref, s32[8,128]{1,0:T(8,128)} %labels_ref.1, f32[8,8,64,128]{3,2,1,0:T(8,128)} %order_ref.2, f32[8,8,64,128]{3,2,1,0:T(8,128)} %adjoint_ref.2), custom_call_target="tpu_custom_call" | custom-call | tf_op jit(solution)/shard_map/pallas_call | solution.py:111
  21.6 17.3 %collective-permute-done.2.other_ref = f32[2,8,64,128]{3,2,1,0:T(8,128)S(1)} collective-permute-done((f32[2,8,64,128]{3,2,1,0:T(8,128)S(1)}, f32[2,8,64,128]{3,2,1,0:T(8,128)S(1)}, u32[]{:S(2)}, u32[]{:S(2)}) %collective-permute-start.2) | collective-permute-done | bytes 524320 | tf_op jit(solution)/shard_map/ppermute | solution.py:11
  38.9 5.9 %shard_map.60 = (f32[8,8,64,128]{3,2,1,0:T(8,128)}, f32[8,8,64,128]{3,2,1,0:T(8,128)}) custom-call(f32[8]{0:T(128)} %rate_ref.5, f32[8,8,64,128]{3,2,1,0:T(8,128)} %order_ref.2, f32[8,8,64,128]{3,2,1,0:T(8,128)} %adjoint_ref.2, f32[2,8,64,128]{3,2,1,0:T(8,128)S(1)} %pad_maximum_fusion.own_ref, f32[2,8,64,128]{3,2,1,0:T(8,128)S(1)} %collective-permute-done.2.other_ref, ...), custom_call_target="tpu_custom_call" | custom-call | tf_op jit(solution)/shard_map/pallas_call | solution.py:117
  44.8 0.0 collective-permute-done.1.above_ref
  44.8 0.0 collective-permute-done.below_ref
  44.8 2.8 %shard_map.61 = (f32[8,8,64,128]{3,2,1,0:T(8,128)}, f32[8,8,64,128]{3,2,1,0:T(8,128)}) custom-call(f32[8]{0:T(128)} %rate_ref.5, f32[2,8,1,64,128]{4,3,2,1,0:T(8,128)S(1)} %collective-permute-done.below_ref, f32[2,8,1,64,128]{4,3,2,1,0:T(8,128)S(1)} %collective-permute-done.1.above_ref, ...), custom_call_target="tpu_custom_call", output_to_operand_aliasing={{0}: (3, {}), {1}: (4, {})} | custom-call | tf_op jit(solution)/shard_map/pallas_call | solution.py:124
  (1 shorter events, 0.0 us)
Async XLA Ops:
  1.3 8.5 %copy-start = (f32[8,8,64,128]{3,2,1,0:T(8,128)S(1)}, f32[8,8,64,128]{3,2,1,0:T(8,128)}, u32[]{:S(2)}) copy-start(f32[8,8,64,128]{3,2,1,0:T(8,128)} %adjoint_ref.2) | copy-start | bytes 6291460
  1.3 8.5 %copy-start.1 = (f32[8,8,64,128]{3,2,1,0:T(8,128)S(1)}, f32[8,8,64,128]{3,2,1,0:T(8,128)}, u32[]{:S(2)}) copy-start(f32[8,8,64,128]{3,2,1,0:T(8,128)} %order_ref.2) | copy-start | bytes 6291460
  4.4 34.6 %collective-permute-start.2 = (f32[2,8,64,128]{3,2,1,0:T(8,128)S(1)}, f32[2,8,64,128]{3,2,1,0:T(8,128)S(1)}, u32[]{:S(2)}, u32[]{:S(2)}) collective-permute-start(f32[2,8,64,128]{3,2,1,0:T(8,128)S(1)} %pad_maximum_fusion.own_ref), channel_id=1, source_target_pairs={{0,1},{1,0},{2,3},{3,2},{4,5},{5,4},{6,7},{7,6},{8,9},{9,8},{10,11... | collective-permute-start | bytes 1572872 | tf_op jit(solution)/shard_map/ppermute | solution.py:11
  10.0 34.8 %collective-permute-start.1 = (f32[2,8,1,64,128]{4,3,2,1,0:T(8,128)S(1)}, f32[2,8,1,64,128]{4,3,2,1,0:T(8,128)S(1)}, u32[]{:S(2)}, u32[]{:S(2)}) collective-permute-start(f32[2,8,1,64,128]{4,3,2,1,0:T(8,128)S(1)} %get-tuple-element.20), channel_id=1, source_target_pairs={{0,254},{2,0},{4,2},{6,4},{8,6},{10,8},{12,10},{14,12},{16,14},{18... | collective-permute-start | bytes 1572872 | tf_op jit(solution)/shard_map/ppermute | solution.py:11
  14.9 29.9 %collective-permute-start = (f32[2,8,1,64,128]{4,3,2,1,0:T(8,128)S(1)}, f32[2,8,1,64,128]{4,3,2,1,0:T(8,128)S(1)}, u32[]{:S(2)}, u32[]{:S(2)}) collective-permute-start(f32[2,8,1,64,128]{4,3,2,1,0:T(8,128)S(1)} %get-tuple-element.21), channel_id=1, source_target_pairs={{0,2},{2,4},{4,6},{6,8},{8,10},{10,12},{12,14},{14,16},{16,18},{18... | collective-permute-start | bytes 1572872 | tf_op jit(solution)/shard_map/ppermute | solution.py:11

commit v13 on v12

--- a/solution.py
+++ b/solution.py
@@ -59,11 +59,15 @@
 
 
 def final_kernel(rate_ref, order_ref, adjoint_ref, own_ref, other_ref, inner_order_ref, inner_adjoint_ref,
-                 order_next_ref, adjoint_order_ref):
+                 order_next_ref, adjoint_order_ref, edge_ref):
     group, rows = order_ref.shape[:2]
     for q in range(group):
-        final_one(q, pl.program_id(0) * group + q, rate_ref, order_ref, adjoint_ref, own_ref, other_ref,
+        p = pl.program_id(0) * group + q
+        final_one(q, p, rate_ref, order_ref, adjoint_ref, own_ref, other_ref,
                   inner_order_ref, inner_adjoint_ref, order_next_ref, adjoint_order_ref)
+        for s, r in enumerate((0, rows - 1)):
+            edge_ref[0, s, p] = order_next_ref[q, r]
+            edge_ref[1, s, p] = adjoint_order_ref[q, r]
 
 
 def final_one(q, p, rate_ref, order_ref, adjoint_ref, own_ref, other_ref, inner_order_ref, inner_adjoint_ref,
@@ -80,15 +84,22 @@
         adjoint_order_ref[q, j] = adj - ((inner_adjoint_ref[q, j] + w * squares) + o * coupled)
 
 
-def edge_kernel(rate_ref, below_ref, above_ref, order_next_in, adjoint_order_in, order_next_ref, adjoint_order_ref):
-    side = pl.program_id(0)
-    count = order_next_in.shape[0]
-    for p in range(count):
-        rate = 0.1 * rate_ref[p]
-        order_row = jnp.where(side == 0, below_ref[0, p, 0], above_ref[0, p, 0])
-        adjoint_row = jnp.where(side == 0, below_ref[1, p, 0], above_ref[1, p, 0])
-        order_next_ref[p, 0] = order_next_in[p, 0] + (0.5 * rate) * order_row
-        adjoint_order_ref[p, 0] = adjoint_order_in[p, 0] + 0.5 * (rate * adjoint_row)
+def edge_kernel(rate_ref, below_ref, above_ref, edge_ref, order_next_in, adjoint_order_in, order_next_ref, adjoint_order_ref,
+                rows_buf, store_sem):
+    count, rows = order_next_in.shape[:2]
+    for s, halo in enumerate((below_ref, above_ref)):
+        for p in range(count):
+            rate = 0.1 * rate_ref[p]
+            rows_buf[0, s, p, 0] = edge_ref[0, s, p] + (0.5 * rate) * halo[0, p, 0]
+            rows_buf[1, s, p, 0] = edge_ref[1, s, p] + 0.5 * (rate * halo[1, p, 0])
+    stores = []
+    for a, target in enumerate((order_next_ref, adjoint_order_ref)):
+        for s, r in enumerate((0, rows - 1)):
+            copy = pltpu.make_async_copy(rows_buf.at[a, s], target.at[:, pl.ds(r, 1)], store_sem.at[a, s])
+            copy.start()
+            stores.append(copy)
+    for copy in stores:
+        copy.wait()
 
 
 def local(order_field, adjoint_next, mobility, labels):
@@ -114,19 +125,28 @@
         out_shape=[jax.ShapeDtypeStruct(order_field.shape, jnp.float32)] * 2,
     )(mobility, indices, labels, order_late, adjoint_late)
     on_chip = pl.BlockSpec(memory_space=pltpu.VMEM)
-    order_next, adjoint_order = pl.pallas_call(
+    whole = pl.BlockSpec((2, rows, depth, width), lambda p, *_: (0, 0, 0, 0))
+    order_next, adjoint_order, edge_rows = pl.pallas_call(
         final_kernel,
-        grid_spec=scalars(num_scalar_prefetch=1, grid=(count // group,), in_specs=[block, block, on_chip, on_chip, block, block], out_specs=[block, block]),
-        out_shape=[jax.ShapeDtypeStruct(order_field.shape, jnp.float32)] * 2,
-    )(mobility, order_field, adjoint_next, *[pltpu.with_memory_space_constraint(x, pltpu.VMEM) for x in (own, other)],
+        grid_spec=scalars(
+            num_scalar_prefetch=1,
+            grid=(count // group,),
+            in_specs=[block, block, whole, whole, block, block],
+            out_specs=[block, block, on_chip],
+        ),
+        out_shape=[jax.ShapeDtypeStruct(order_field.shape, jnp.float32)] * 2
+        + [pltpu.VMEM((2, 2, count, depth, width), jnp.float32)],
+    )(mobility, order_field, adjoint_next, own, other,
       inner_order, inner_adjoint)
-    row = pl.BlockSpec((count, 1, depth, width), lambda s, *_: (0, s * (rows - 1), 0, 0))
+    anywhere = pl.BlockSpec(memory_space=pl.ANY)
     return pl.pallas_call(
         edge_kernel,
-        grid_spec=scalars(num_scalar_prefetch=1, grid=(2,), in_specs=[on_chip, on_chip, row, row], out_specs=[row, row]),
+        in_specs=[pl.BlockSpec(memory_space=pltpu.SMEM), on_chip, on_chip, on_chip, anywhere, anywhere],
+        out_specs=[anywhere, anywhere],
         out_shape=[jax.ShapeDtypeStruct(order_field.shape, jnp.float32)] * 2,
-        input_output_aliases={3: 0, 4: 1},
-    )(mobility, *[pltpu.with_memory_space_constraint(x, pltpu.VMEM) for x in (below, above)], order_next, adjoint_order)
+        scratch_shapes=[pltpu.VMEM((2, 2, count, 1, depth, width), jnp.float32), pltpu.SemaphoreType.DMA((2, 2))],
+        input_output_aliases={4: 0, 5: 1},
+    )(mobility, *[pltpu.with_memory_space_constraint(x, pltpu.VMEM) for x in (below, above, edge_rows)], order_next, adjoint_order)
 
 
 def solution(mesh):

time: 47.7 us -> 47.9 us (level)
  local copies, waits for them, and re-layouts: 0.11 us -> 1.84 us
  waiting for transfers between devices: 17.3 us -> 16.5 us
  Pallas kernels: 14.8 us -> 14.1 us
    pallas_call x1, Pallas kernels: 2.75 us -> 1.77 us  [local(): pl.pallas_call(edge_kernel, in_specs=[pl.BlockSpec(memory_space=pltpu.SME...]
    slice x1, local copies, waits for them, and re-layouts: 0.1 us -> 1.05 us  [local(): above = shift_along(edges[:, :, :1], 'space', -1)]
    ppermute x3, waiting for transfers between devices: 17.3 us -> 16.5 us  [shift_along(): lax.ppermute(cells, axis, [(i, (i + step) % count) for i in range(count)])]
    unnamed x4 -> x8, local copies, waits for them, and re-layouts: 0.01 us -> 0.79 us
  transfers between devices with their start and end apart: 3 -> 3, of which waited for: 1 -> 1; matrix products, arithmetic and copies ran while one was open for 1% -> 3% of each run, Pallas kernels for 25% -> 26%
where the time goes in v13:
time: 47.9 us; the launch traced here: 47.7 us
  waiting for transfers between devices  16.5 us (34%)
  Pallas kernels  14.1 us (29%)
  starting transfers between devices  10.3 us (22%)
  other arithmetic  4.29 us (9%)
  local copies, waits for them, and re-layouts  1.84 us (4%)
  between operations  0.69 us (1%)
    ppermute x3, waiting for transfers between devices, shift_along(): lax.ppermute(cells, axis, [(i, (i + step) % count) for i in range(count)])  16.5 us
    ppermute x3, starting transfers between devices, shift_along(): lax.ppermute(cells, axis, [(i, (i + step) % count) for i in range(count)])  10.3 us
    pallas_call x1, Pallas kernels, local(): pl.pallas_call(final_kernel, grid_spec=scalars(num_scalar_prefetch=1, gri...  6.23 us
    pallas_call x1, Pallas kernels, local(): pl.pallas_call(inner_kernel, grid_spec=scalars(num_scalar_prefetch=2, gri...  6.15 us
    reduce_sum x1, other arithmetic, local(): jnp.sum(order_field * order_field, axis=0)  3.01 us
    pallas_call x1, Pallas kernels, local(): pl.pallas_call(edge_kernel, in_specs=[pl.BlockSpec(memory_space=pltpu.SME...  1.77 us
    slice x1, local copies, waits for them, and re-layouts, local(): above = shift_along(edges[:, :, :1], 'space', -1)  1.05 us
  transfers between devices with their start and end apart: 3, of which 1 were waited for; matrix products, arithmetic and copies ran while one was open for 3% of the time, Pallas kernels for 26%

profile of v13, /device:TPU:64, one launch (start us, length us, event | category | flops | bytes accessed | tf_op | source)
XLA Modules:
  0.0 47.7 jit_solution(9215120188908200698)
XLA Ops:
  0.6 0.7 %broadcast_multiply_fusion = f32[8]{0:T(128)S(1)} fusion(f32[8]{0:T(128)} %rate_ref.5), kind=kLoop, calls=%fused_computation.9 | loop fusion | flops 8 | bytes 64 | tf_op jit(solution)/shard_map/mul | solution.py:110
  1.3 0.0 copy-start
  1.3 0.0 copy-start.1
  1.3 3.0 %multiply_reduce_fusion.1 = (f32[8,64,128]{2,1,0:T(8,128)S(1)}, f32[8,64,128]{2,1,0:T(8,128)S(1)}) fusion(f32[8,8,64,128]{3,2,1,0:T(8,128)} %order_ref.2, f32[8,8,64,128]{3,2,1,0:T(8,128)} %adjoint_ref.2, f32[8]{0:T(128)S(1)} %broadcast_multiply_fusion), kind=kLoop, calls=%fused_computation.1 | loop fusion | flops 2490368 | bytes 4718624 | tf_op jit(solution)/shard_map/reduce_sum | solution.py:111
  4.4 0.0 copy-start.2
  4.4 5.5 %collective-permute-start.2 = (f32[2,8,64,128]{3,2,1,0:T(8,128)S(1)}, f32[2,8,64,128]{3,2,1,0:T(8,128)S(1)}, u32[]{:S(2)}, u32[]{:S(2)}) collective-permute-start(f32[2,8,64,128]{3,2,1,0:T(8,128)S(1)} %pad_maximum_fusion.own_ref), channel_id=1, source_target_pairs={{0,1},{1,0},{2,3},{3,2},{4,5},{5,4},{6,7},{7,6},{8,9},{9,8},{10,11... | collective-permute-start | bytes 1572872 | tf_op jit(solution)/shard_map/ppermute | solution.py:11
  9.8 0.0 copy-done
  9.8 0.0 copy-done.1
  9.8 0.1 fusion
  9.9 0.0 copy-done.2
  9.9 1.1 %fusion.1 = (f32[2,8,1,64,128]{4,3,2,1,0:T(8,128)}, f32[2,8,1,64,128]{4,3,2,1,0:T(8,128)}) fusion(f32[2,8,2,64,128]{4,3,2,1,0:T(8,128)S(1)} %fusion), kind=kLoop, calls=%fused_computation.10 | loop fusion | bytes 2097152 | tf_op jit(solution)/shard_map/slice | solution.py:117
  11.0 4.8 %collective-permute-start.1 = (f32[2,8,1,64,128]{4,3,2,1,0:T(8,128)}, f32[2,8,1,64,128]{4,3,2,1,0:T(8,128)S(1)}, u32[]{:S(2)}, u32[]{:S(2)}) collective-permute-start(f32[2,8,1,64,128]{4,3,2,1,0:T(8,128)} %get-tuple-element.22), channel_id=1, source_target_pairs={{0,254},{2,0},{4,2},{6,4},{8,6},{10,8},{12,10},{14,12},{16,14},{18... | collective-permute-start | bytes 1572872 | tf_op jit(solution)/shard_map/ppermute | solution.py:11
  15.8 0.0 collective-permute-start
  15.8 0.5 %iota_add_fusion.index_ref = s32[8]{0:T(128)} fusion(s32[]{:T(128)S(6)} %mul.26), kind=kLoop, calls=%fused_computation.8 | loop fusion | flops 8 | bytes 36 | tf_op jit(solution)/shard_map/add | solution.py:108
  16.3 6.1 %shard_map.59 = (f32[8,8,64,128]{3,2,1,0:T(8,128)}, f32[8,8,64,128]{3,2,1,0:T(8,128)}) custom-call(f32[8]{0:T(128)} %rate_ref.5, s32[8]{0:T(128)} %iota_add_fusion.index_ref, s32[8,128]{1,0:T(8,128)} %labels_ref.1, f32[8,8,64,128]{3,2,1,0:T(8,128)} %order_ref.2, f32[8,8,64,128]{3,2,1,0:T(8,128)} %adjoint_ref.2), custom_call_target="tpu_custom_call" | custom-call | tf_op jit(solution)/shard_map/pallas_call | solution.py:122
  22.5 16.5 %collective-permute-done.2.other_ref = f32[2,8,64,128]{3,2,1,0:T(8,128)S(1)} collective-permute-done((f32[2,8,64,128]{3,2,1,0:T(8,128)S(1)}, f32[2,8,64,128]{3,2,1,0:T(8,128)S(1)}, u32[]{:S(2)}, u32[]{:S(2)}) %collective-permute-start.2) | collective-permute-done | bytes 524320 | tf_op jit(solution)/shard_map/ppermute | solution.py:11
  38.9 0.0 copy-start.3
  38.9 0.8 %copy-done.3 = f32[2,8,64,128]{3,2,1,0:T(8,128)} copy-done((f32[2,8,64,128]{3,2,1,0:T(8,128)}, f32[2,8,64,128]{3,2,1,0:T(8,128)S(1)}, u32[]{:S(2)}) %copy-start.3) | copy-done | bytes 524312
  39.7 6.2 %shard_map.60 = (f32[8,8,64,128]{3,2,1,0:T(8,128)}, f32[8,8,64,128]{3,2,1,0:T(8,128)}, f32[2,2,8,64,128]{4,3,2,1,0:T(8,128)S(1)}) custom-call(f32[8]{0:T(128)} %rate_ref.5, f32[8,8,64,128]{3,2,1,0:T(8,128)} %order_ref.2, f32[8,8,64,128]{3,2,1,0:T(8,128)} %adjoint_ref.2, f32[2,8,64,128]{3,2,1,0:T(8,128)} %copy-done.2, f32[2,8,64,128]{3,2,1,0:T(8,128)} %copy-done.3, ...), custom_call_target="tpu_custom_call" | custom-call | tf_op jit(solution)/shard_map/pallas_call | solution.py:129
  46.0 0.0 collective-permute-done.1.above_ref
  46.0 0.0 collective-permute-done.below_ref
  46.0 1.8 %shard_map.61 = (f32[8,8,64,128]{3,2,1,0:T(8,128)}, f32[8,8,64,128]{3,2,1,0:T(8,128)}) custom-call(f32[8]{0:T(128)} %rate_ref.5, f32[2,8,1,64,128]{4,3,2,1,0:T(8,128)S(1)} %collective-permute-done.below_ref, f32[2,8,1,64,128]{4,3,2,1,0:T(8,128)S(1)} %collective-permute-done.1.above_ref, ...), custom_call_target="tpu_custom_call", output_to_operand_aliasing={{0}: (4, {}), {1}: (5, {})} | custom-call | tf_op jit(solution)/shard_map/pallas_call | solution.py:142
  (1 shorter events, 0.0 us)
Async XLA Ops:
  1.3 8.6 %copy-start = (f32[8,8,64,128]{3,2,1,0:T(8,128)S(1)}, f32[8,8,64,128]{3,2,1,0:T(8,128)}, u32[]{:S(2)}) copy-start(f32[8,8,64,128]{3,2,1,0:T(8,128)} %adjoint_ref.2) | copy-start | bytes 6291460
  1.3 8.6 %copy-start.1 = (f32[8,8,64,128]{3,2,1,0:T(8,128)S(1)}, f32[8,8,64,128]{3,2,1,0:T(8,128)}, u32[]{:S(2)}) copy-start(f32[8,8,64,128]{3,2,1,0:T(8,128)} %order_ref.2) | copy-start | bytes 6291460
  4.4 5.6 %copy-start.2 = (f32[2,8,64,128]{3,2,1,0:T(8,128)}, f32[2,8,64,128]{3,2,1,0:T(8,128)S(1)}, u32[]{:S(2)}) copy-start(f32[2,8,64,128]{3,2,1,0:T(8,128)S(1)} %pad_maximum_fusion.own_ref) | copy-start | bytes 1572868
  4.4 34.6 %collective-permute-start.2 = (f32[2,8,64,128]{3,2,1,0:T(8,128)S(1)}, f32[2,8,64,128]{3,2,1,0:T(8,128)S(1)}, u32[]{:S(2)}, u32[]{:S(2)}) collective-permute-start(f32[2,8,64,128]{3,2,1,0:T(8,128)S(1)} %pad_maximum_fusion.own_ref), channel_id=1, source_target_pairs={{0,1},{1,0},{2,3},{3,2},{4,5},{5,4},{6,7},{7,6},{8,9},{9,8},{10,11... | collective-permute-start | bytes 1572872 | tf_op jit(solution)/shard_map/ppermute | solution.py:11
  11.0 35.0 %collective-permute-start.1 = (f32[2,8,1,64,128]{4,3,2,1,0:T(8,128)}, f32[2,8,1,64,128]{4,3,2,1,0:T(8,128)S(1)}, u32[]{:S(2)}, u32[]{:S(2)}) collective-permute-start(f32[2,8,1,64,128]{4,3,2,1,0:T(8,128)} %get-tuple-element.22), channel_id=1, source_target_pairs={{0,254},{2,0},{4,2},{6,4},{8,6},{10,8},{12,10},{14,12},{16,14},{18... | collective-permute-start | bytes 1572872 | tf_op jit(solution)/shard_map/ppermute | solution.py:11
  15.8 30.2 %collective-permute-start = (f32[2,8,1,64,128]{4,3,2,1,0:T(8,128)}, f32[2,8,1,64,128]{4,3,2,1,0:T(8,128)S(1)}, u32[]{:S(2)}, u32[]{:S(2)}) collective-permute-start(f32[2,8,1,64,128]{4,3,2,1,0:T(8,128)} %get-tuple-element.23), channel_id=1, source_target_pairs={{0,2},{2,4},{4,6},{6,8},{8,10},{10,12},{12,14},{14,16},{16,18},{18... | collective-permute-start | bytes 1572872 | tf_op jit(solution)/shard_map/ppermute | solution.py:11
  38.9 0.8 %copy-start.3 = (f32[2,8,64,128]{3,2,1,0:T(8,128)}, f32[2,8,64,128]{3,2,1,0:T(8,128)S(1)}, u32[]{:S(2)}) copy-start(f32[2,8,64,128]{3,2,1,0:T(8,128)S(1)} %collective-permute-done.2.other_ref) | copy-start | bytes 1572868

commit v14 on v12

--- a/solution.py
+++ b/solution.py
@@ -98,7 +98,8 @@
     rates = mobility[:, None, None, None]
     weighted = 0.1 * rates * adjoint_next
     own = jnp.stack([jnp.sum(order_field * order_field, axis=0), jnp.sum(order_field * weighted, axis=0)])
-    other = shift_along(own, "op", 1)
+    both = lax.all_to_all(jnp.stack([own, own]), "op", 0, 0, tiled=False)
+    other = both[1 - lax.axis_index("op")]
     pair = jnp.stack([order_field, adjoint_next])
     edges = jnp.concatenate([pair[:, :, :1], pair[:, :, -1:]], axis=2)
     edges, own, order_late, adjoint_late = lax.optimization_barrier((edges, own, order_field, adjoint_next))

time: 47.7 us -> 57.1 us (1.20)
  the two profiles are of different devices: /device:TPU:64 before, /device:TPU:62 now
where the time goes in v14:
time: 57.1 us; the launch traced here: 56.8 us
  waiting for transfers between devices  25.5 us (45%)
  Pallas kernels  14.8 us (26%)
  starting transfers between devices  8.14 us (14%)
  other arithmetic  6.51 us (11%)
  local copies, waits for them, and re-layouts  1.19 us (2%)
  between operations  0.68 us (1%)
    all_to_all x1, waiting for transfers between devices, local(): both = lax.all_to_all(jnp.stack([own, own]), 'op', 0, 0, tiled=False)  25.5 us
    all_to_all x1, starting transfers between devices, local(): both = lax.all_to_all(jnp.stack([own, own]), 'op', 0, 0, tiled=False)  7.56 us
    pallas_call x1, Pallas kernels, local(): pl.pallas_call(inner_kernel, grid_spec=scalars(num_scalar_prefetch=2, gri...  6.15 us
    pallas_call x1, Pallas kernels, local(): pl.pallas_call(final_kernel, grid_spec=scalars(num_scalar_prefetch=1, gri...  5.88 us
    reduce_sum x1, other arithmetic, local(): jnp.sum(order_field * order_field, axis=0)  2.85 us
    pallas_call x1, Pallas kernels, local(): pl.pallas_call(edge_kernel, grid_spec=scalars(num_scalar_prefetch=1, grid...  2.75 us
    concatenate x1, other arithmetic, local(): edges = jnp.concatenate([pair[:, :, :1], pair[:, :, -1:]], axis=2)  1.28 us
    another operation x2, other arithmetic, local(): both = lax.all_to_all(jnp.stack([own, own]), 'op', 0, 0, tiled=False)  1.2 us
  transfers between devices with their start and end apart: 3, of which 1 were waited for; matrix products, arithmetic and copies ran while one was open for 5% of the time, Pallas kernels for 21%

profile of v14, /device:TPU:62, one launch (start us, length us, event | category | flops | bytes accessed | tf_op | source)
XLA Modules:
  0.0 56.8 jit_solution(16381438426463987279)
XLA Ops:
  0.6 0.7 %broadcast_multiply_fusion = f32[8]{0:T(128)S(1)} fusion(f32[8]{0:T(128)} %rate_ref.5), kind=kLoop, calls=%fused_computation.11 | loop fusion | flops 8 | bytes 64 | tf_op jit(solution)/shard_map/mul | solution.py:99
  1.3 2.9 %multiply_reduce_fusion.1 = (f32[8,64,128]{2,1,0:T(8,128)S(1)}, f32[8,64,128]{2,1,0:T(8,128)S(1)}) fusion(f32[8,8,64,128]{3,2,1,0:T(8,128)} %order_ref.2, f32[8,8,64,128]{3,2,1,0:T(8,128)} %adjoint_ref.2, f32[8]{0:T(128)S(1)} %broadcast_multiply_fusion), kind=kLoop, calls=%fused_computation.1 | loop fusion | flops 2490368 | bytes 4718624 | tf_op jit(solution)/shard_map/reduce_sum | solution.py:100
  4.1 0.1 fusion.1
  4.3 0.0 copy-start
  4.3 1.1 %pad_maximum_fusion = f32[2,2,8,64,128]{4,3,2,1,0:T(8,128)} fusion(f32[1,2,8,64,128]{4,3,2,1,0:T(8,128)S(1)} %get-tuple-element.22), kind=kLoop, calls=%fused_computation.7 | loop fusion | flops 262144 | bytes 1572864 | tf_op jit(solution)/shard_map/stack | solution.py:101
  5.4 7.6 %all-to-all-start = ((f32[2,2,8,64,128]{4,3,2,1,0:T(8,128)}), f32[2,2,8,64,128]{4,3,2,1,0:T(8,128)}, u32[]{:S(2)}, u32[]{:S(2)}) async-start(f32[2,2,8,64,128]{4,3,2,1,0:T(8,128)} %pad_maximum_fusion), calls=%async_computation | async-start | bytes 2097152 | tf_op jit(solution)/shard_map/all_to_all | solution.py:101
  12.9 0.0 copy-done
  12.9 1.3 %fusion = f32[2,8,2,64,128]{4,3,2,1,0:T(8,128)S(1)} fusion(f32[1,8,8,64,128]{4,3,2,1,0:T(8,128)S(1)} %bitcast.8, f32[1,8,8,64,128]{4,3,2,1,0:T(8,128)} %bitcast.9), kind=kLoop, calls=%fused_computation.3 | loop fusion | flops 2359296 | bytes 5242880 | tf_op jit(solution)/shard_map/concatenate | solution.py:104
  14.2 0.1 fusion.2
  14.3 0.1 collective-permute-start.1
  14.4 0.5 collective-permute-start
  14.9 0.5 iota_add_fusion.index_ref
  15.4 6.2 %shard_map.59 = (f32[8,8,64,128]{3,2,1,0:T(8,128)}, f32[8,8,64,128]{3,2,1,0:T(8,128)}) custom-call(f32[8]{0:T(128)} %rate_ref.5, s32[8]{0:T(128)} %iota_add_fusion.index_ref, s32[8,128]{1,0:T(8,128)} %labels_ref.1, f32[8,8,64,128]{3,2,1,0:T(8,128)} %order_ref.2, f32[8,8,64,128]{3,2,1,0:T(8,128)} %adjoint_ref.2), custom_call_target="tpu_custom_call" | custom-call | tf_op jit(solution)/shard_map/pallas_call | solution.py:112
  21.6 25.5 %all-to-all-done = f32[2,2,8,64,128]{4,3,2,1,0:T(8,128)} async-done(((f32[2,2,8,64,128]{4,3,2,1,0:T(8,128)}), f32[2,2,8,64,128]{4,3,2,1,0:T(8,128)}, u32[]{:S(2)}, u32[]{:S(2)}) %all-to-all-start) | async-done | bytes 1048608 | tf_op jit(solution)/shard_map/all_to_all | solution.py:101
  47.1 1.1 %dynamic-slice_bitcast_fusion.other_ref = f32[2,8,64,128]{3,2,1,0:T(8,128)S(1)} fusion(f32[2,2,8,64,128]{4,3,2,1,0:T(8,128)} %all-to-all-done, s32[]{:T(128)S(6)} %select_n.3), kind=kLoop, calls=%fused_computation.9 | loop fusion | bytes 1048580 | tf_op jit(solution)/shard_map/squeeze | solution.py:102
  48.2 5.9 %shard_map.60 = (f32[8,8,64,128]{3,2,1,0:T(8,128)}, f32[8,8,64,128]{3,2,1,0:T(8,128)}) custom-call(f32[8]{0:T(128)} %rate_ref.5, f32[8,8,64,128]{3,2,1,0:T(8,128)} %order_ref.2, f32[8,8,64,128]{3,2,1,0:T(8,128)} %adjoint_ref.2, f32[2,8,64,128]{3,2,1,0:T(8,128)S(1)} %get-tuple-element.11.own_ref, f32[2,8,64,128]{3,2,1,0:T(8,128)S(1)} %dynamic-slice_bitcast_fusion.other_ref, ...), custom_call_target="tpu_custom_call" | custom-call | tf_op jit(solution)/shard_map/pallas_call | solution.py:118
  54.0 0.0 collective-permute-done.1.above_ref
  54.0 0.0 collective-permute-done.below_ref
  54.1 2.8 %shard_map.61 = (f32[8,8,64,128]{3,2,1,0:T(8,128)}, f32[8,8,64,128]{3,2,1,0:T(8,128)}) custom-call(f32[8]{0:T(128)} %rate_ref.5, f32[2,8,1,64,128]{4,3,2,1,0:T(8,128)S(1)} %collective-permute-done.below_ref, f32[2,8,1,64,128]{4,3,2,1,0:T(8,128)S(1)} %collective-permute-done.1.above_ref, ...), custom_call_target="tpu_custom_call", output_to_operand_aliasing={{0}: (3, {}), {1}: (4, {})} | custom-call | tf_op jit(solution)/shard_map/pallas_call | solution.py:125
Async XLA Ops:
  4.3 8.7 %copy-start = (f32[8,8,64,128]{3,2,1,0:T(8,128)S(1)}, f32[8,8,64,128]{3,2,1,0:T(8,128)}, u32[]{:S(2)}) copy-start(f32[8,8,64,128]{3,2,1,0:T(8,128)} %adjoint_ref.2) | copy-start | bytes 6291460
  5.4 41.7 %all-to-all-start = ((f32[2,2,8,64,128]{4,3,2,1,0:T(8,128)}), f32[2,2,8,64,128]{4,3,2,1,0:T(8,128)}, u32[]{:S(2)}, u32[]{:S(2)}) async-start(f32[2,2,8,64,128]{4,3,2,1,0:T(8,128)} %pad_maximum_fusion), calls=%async_computation | async-start | bytes 2097152 | tf_op jit(solution)/shard_map/all_to_all | solution.py:101
  14.3 39.7 %collective-permute-start.1 = (f32[2,8,1,64,128]{4,3,2,1,0:T(8,128)S(1)}, f32[2,8,1,64,128]{4,3,2,1,0:T(8,128)S(1)}, u32[]{:S(2)}, u32[]{:S(2)}) collective-permute-start(f32[2,8,1,64,128]{4,3,2,1,0:T(8,128)S(1)} %get-tuple-element.20), channel_id=1, source_target_pairs={{0,254},{2,0},{4,2},{6,4},{8,6},{10,8},{12,10},{14,12},{16,14},{18... | collective-permute-start | bytes 1572872 | tf_op jit(solution)/shard_map/ppermute | solution.py:11
  14.4 39.6 %collective-permute-start = (f32[2,8,1,64,128]{4,3,2,1,0:T(8,128)S(1)}, f32[2,8,1,64,128]{4,3,2,1,0:T(8,128)S(1)}, u32[]{:S(2)}, u32[]{:S(2)}) collective-permute-start(f32[2,8,1,64,128]{4,3,2,1,0:T(8,128)S(1)} %get-tuple-element.21), channel_id=1, source_target_pairs={{0,2},{2,4},{4,6},{6,8},{8,10},{10,12},{12,14},{14,16},{16,18},{18... | collective-permute-start | bytes 1572872 | tf_op jit(solution)/shard_map/ppermute | solution.py:11

commit v15 on v13

--- a/solution.py
+++ b/solution.py
@@ -66,8 +66,8 @@
         final_one(q, p, rate_ref, order_ref, adjoint_ref, own_ref, other_ref,
                   inner_order_ref, inner_adjoint_ref, order_next_ref, adjoint_order_ref)
         for s, r in enumerate((0, rows - 1)):
-            edge_ref[0, s, p] = order_next_ref[q, r]
-            edge_ref[1, s, p] = adjoint_order_ref[q, r]
+            edge_ref[0, s, q] = order_next_ref[q, r]
+            edge_ref[1, s, q] = adjoint_order_ref[q, r]
 
 
 def final_one(q, p, rate_ref, order_ref, adjoint_ref, own_ref, other_ref, inner_order_ref, inner_adjoint_ref,
@@ -84,9 +84,12 @@
         adjoint_order_ref[q, j] = adj - ((inner_adjoint_ref[q, j] + w * squares) + o * coupled)
 
 
-def edge_kernel(rate_ref, below_ref, above_ref, edge_ref, order_next_in, adjoint_order_in, order_next_ref, adjoint_order_ref,
-                rows_buf, store_sem):
+def edge_kernel(rate_ref, below_ref, above_ref, edge_hbm, order_next_in, adjoint_order_in, order_next_ref, adjoint_order_ref,
+                edge_ref, rows_buf, load_sem, store_sem):
     count, rows = order_next_in.shape[:2]
+    load = pltpu.make_async_copy(edge_hbm, edge_ref, load_sem)
+    load.start()
+    load.wait()
     for s, halo in enumerate((below_ref, above_ref)):
         for p in range(count):
             rate = 0.1 * rate_ref[p]
@@ -125,28 +128,32 @@
         out_shape=[jax.ShapeDtypeStruct(order_field.shape, jnp.float32)] * 2,
     )(mobility, indices, labels, order_late, adjoint_late)
     on_chip = pl.BlockSpec(memory_space=pltpu.VMEM)
-    whole = pl.BlockSpec((2, rows, depth, width), lambda p, *_: (0, 0, 0, 0))
     order_next, adjoint_order, edge_rows = pl.pallas_call(
         final_kernel,
         grid_spec=scalars(
             num_scalar_prefetch=1,
             grid=(count // group,),
-            in_specs=[block, block, whole, whole, block, block],
-            out_specs=[block, block, on_chip],
+            in_specs=[block, block, on_chip, on_chip, block, block],
+            out_specs=[block, block, pl.BlockSpec((2, 2, group, depth, width), lambda p, *_: (0, 0, p, 0, 0))],
         ),
         out_shape=[jax.ShapeDtypeStruct(order_field.shape, jnp.float32)] * 2
-        + [pltpu.VMEM((2, 2, count, depth, width), jnp.float32)],
-    )(mobility, order_field, adjoint_next, own, other,
+        + [jax.ShapeDtypeStruct((2, 2, count, depth, width), jnp.float32)],
+    )(mobility, order_field, adjoint_next, *[pltpu.with_memory_space_constraint(x, pltpu.VMEM) for x in (own, other)],
       inner_order, inner_adjoint)
     anywhere = pl.BlockSpec(memory_space=pl.ANY)
     return pl.pallas_call(
         edge_kernel,
-        in_specs=[pl.BlockSpec(memory_space=pltpu.SMEM), on_chip, on_chip, on_chip, anywhere, anywhere],
+        in_specs=[pl.BlockSpec(memory_space=pltpu.SMEM), on_chip, on_chip, anywhere, anywhere, anywhere],
         out_specs=[anywhere, anywhere],
         out_shape=[jax.ShapeDtypeStruct(order_field.shape, jnp.float32)] * 2,
-        scratch_shapes=[pltpu.VMEM((2, 2, count, 1, depth, width), jnp.float32), pltpu.SemaphoreType.DMA((2, 2))],
+        scratch_shapes=[
+            pltpu.VMEM((2, 2, count, depth, width), jnp.float32),
+            pltpu.VMEM((2, 2, count, 1, depth, width), jnp.float32),
+            pltpu.SemaphoreType.DMA(()),
+            pltpu.SemaphoreType.DMA((2, 2)),
+        ],
         input_output_aliases={4: 0, 5: 1},
-    )(mobility, *[pltpu.with_memory_space_constraint(x, pltpu.VMEM) for x in (below, above, edge_rows)], order_next, adjoint_order)
+    )(mobility, *[pltpu.with_memory_space_constraint(x, pltpu.VMEM) for x in (below, above)], edge_rows, order_next, adjoint_order)
 
 
 def solution(mesh):

time: 47.9 us -> 48.2 us (level)
  local copies, waits for them, and re-layouts: 1.84 us -> 0.11 us
  Pallas kernels: 14.1 us -> 15.3 us
  waiting for transfers between devices: 16.5 us -> 17.3 us
    pallas_call x1, Pallas kernels: 1.77 us -> 3 us  [local(): pl.pallas_call(edge_kernel, in_specs=[pl.BlockSpec(memory_space=pltpu.SME...]
    slice x1, local copies, waits for them, and re-layouts: 1.05 us -> 0.1 us  [local(): above = shift_along(edges[:, :, :1], 'space', -1)]
    ppermute x3, waiting for transfers between devices: 16.5 us -> 17.3 us  [shift_along(): lax.ppermute(cells, axis, [(i, (i + step) % count) for i in range(count)])]
    unnamed x8 -> x4, local copies, waits for them, and re-layouts: 0.79 us -> 0.01 us
  transfers between devices with their start and end apart: 3 -> 3, of which waited for: 1 -> 1; matrix products, arithmetic and copies ran while one was open for 3% -> 1% of each run, Pallas kernels for 26% -> 26%
where the time goes in v15:
time: 48.2 us; the launch traced here: 48 us
  waiting for transfers between devices  17.3 us (36%)
  Pallas kernels  15.3 us (32%)
  starting transfers between devices  10.4 us (22%)
  other arithmetic  4.29 us (9%)
  between operations  0.67 us (1%)
    ppermute x3, waiting for transfers between devices, shift_along(): lax.ppermute(cells, axis, [(i, (i + step) % count) for i in range(count)])  17.3 us
    ppermute x3, starting transfers between devices, shift_along(): lax.ppermute(cells, axis, [(i, (i + step) % count) for i in range(count)])  10.4 us
    pallas_call x1, Pallas kernels, local(): pl.pallas_call(inner_kernel, grid_spec=scalars(num_scalar_prefetch=2, gri...  6.16 us
    pallas_call x1, Pallas kernels, local(): pl.pallas_call(final_kernel, grid_spec=scalars(num_scalar_prefetch=1, gri...  6.11 us
    reduce_sum x1, other arithmetic, local(): jnp.sum(order_field * order_field, axis=0)  3.01 us
    pallas_call x1, Pallas kernels, local(): pl.pallas_call(edge_kernel, in_specs=[pl.BlockSpec(memory_space=pltpu.SME...  3 us
  transfers between devices with their start and end apart: 3, of which 1 were waited for; matrix products, arithmetic and copies ran while one was open for 1% of the time, Pallas kernels for 26%

profile of v15, /device:TPU:64, one launch (start us, length us, event | category | flops | bytes accessed | tf_op | source)
XLA Modules:
  0.0 48.0 jit_solution(11445700565051829316)
XLA Ops:
  0.6 0.7 %broadcast_multiply_fusion = f32[8]{0:T(128)S(1)} fusion(f32[8]{0:T(128)} %rate_ref.5), kind=kLoop, calls=%fused_computation.9 | loop fusion | flops 8 | bytes 64 | tf_op jit(solution)/shard_map/mul | solution.py:113
  1.3 0.0 copy-start
  1.3 0.0 copy-start.1
  1.3 3.0 %multiply_reduce_fusion.1 = (f32[8,64,128]{2,1,0:T(8,128)S(1)}, f32[8,64,128]{2,1,0:T(8,128)S(1)}) fusion(f32[8,8,64,128]{3,2,1,0:T(8,128)} %order_ref.2, f32[8,8,64,128]{3,2,1,0:T(8,128)} %adjoint_ref.2, f32[8]{0:T(128)S(1)} %broadcast_multiply_fusion), kind=kLoop, calls=%fused_computation.1 | loop fusion | flops 2490368 | bytes 4718624 | tf_op jit(solution)/shard_map/reduce_sum | solution.py:114
  4.4 5.5 %collective-permute-start.2 = (f32[2,8,64,128]{3,2,1,0:T(8,128)S(1)}, f32[2,8,64,128]{3,2,1,0:T(8,128)S(1)}, u32[]{:S(2)}, u32[]{:S(2)}) collective-permute-start(f32[2,8,64,128]{3,2,1,0:T(8,128)S(1)} %pad_maximum_fusion.own_ref), channel_id=1, source_target_pairs={{0,1},{1,0},{2,3},{3,2},{4,5},{5,4},{6,7},{7,6},{8,9},{9,8},{10,11... | collective-permute-start | bytes 1572872 | tf_op jit(solution)/shard_map/ppermute | solution.py:11
  9.8 0.0 copy-done
  9.8 0.0 copy-done.1
  9.8 0.1 fusion
  9.9 0.1 fusion.1
  10.0 4.9 %collective-permute-start.1 = (f32[2,8,1,64,128]{4,3,2,1,0:T(8,128)S(1)}, f32[2,8,1,64,128]{4,3,2,1,0:T(8,128)S(1)}, u32[]{:S(2)}, u32[]{:S(2)}) collective-permute-start(f32[2,8,1,64,128]{4,3,2,1,0:T(8,128)S(1)} %get-tuple-element.22), channel_id=1, source_target_pairs={{0,254},{2,0},{4,2},{6,4},{8,6},{10,8},{12,10},{14,12},{16,14},{18... | collective-permute-start | bytes 1572872 | tf_op jit(solution)/shard_map/ppermute | solution.py:11
  14.9 0.0 collective-permute-start
  14.9 0.5 %iota_add_fusion.index_ref = s32[8]{0:T(128)} fusion(s32[]{:T(128)S(6)} %mul.26), kind=kLoop, calls=%fused_computation.8 | loop fusion | flops 8 | bytes 36 | tf_op jit(solution)/shard_map/add | solution.py:111
  15.4 6.2 %shard_map.59 = (f32[8,8,64,128]{3,2,1,0:T(8,128)}, f32[8,8,64,128]{3,2,1,0:T(8,128)}) custom-call(f32[8]{0:T(128)} %rate_ref.5, s32[8]{0:T(128)} %iota_add_fusion.index_ref, s32[8,128]{1,0:T(8,128)} %labels_ref.1, f32[8,8,64,128]{3,2,1,0:T(8,128)} %order_ref.2, f32[8,8,64,128]{3,2,1,0:T(8,128)} %adjoint_ref.2), custom_call_target="tpu_custom_call" | custom-call | tf_op jit(solution)/shard_map/pallas_call | solution.py:125
  21.6 17.3 %collective-permute-done.2.other_ref = f32[2,8,64,128]{3,2,1,0:T(8,128)S(1)} collective-permute-done((f32[2,8,64,128]{3,2,1,0:T(8,128)S(1)}, f32[2,8,64,128]{3,2,1,0:T(8,128)S(1)}, u32[]{:S(2)}, u32[]{:S(2)}) %collective-permute-start.2) | collective-permute-done | bytes 524320 | tf_op jit(solution)/shard_map/ppermute | solution.py:11
  38.9 6.1 %shard_map.60 = (f32[8,8,64,128]{3,2,1,0:T(8,128)}, f32[8,8,64,128]{3,2,1,0:T(8,128)}, f32[2,2,8,64,128]{4,3,2,1,0:T(8,128)}) custom-call(f32[8]{0:T(128)} %rate_ref.5, f32[8,8,64,128]{3,2,1,0:T(8,128)} %order_ref.2, f32[8,8,64,128]{3,2,1,0:T(8,128)} %adjoint_ref.2, f32[2,8,64,128]{3,2,1,0:T(8,128)S(1)} %pad_maximum_fusion.own_ref, ...), custom_call_target="tpu_custom_call" | custom-call | tf_op jit(solution)/shard_map/pallas_call | solution.py:131
  45.0 0.0 collective-permute-done.1.above_ref
  45.0 0.0 collective-permute-done.below_ref
  45.0 3.0 %shard_map.61 = (f32[8,8,64,128]{3,2,1,0:T(8,128)}, f32[8,8,64,128]{3,2,1,0:T(8,128)}) custom-call(f32[8]{0:T(128)} %rate_ref.5, f32[2,8,1,64,128]{4,3,2,1,0:T(8,128)S(1)} %collective-permute-done.below_ref, f32[2,8,1,64,128]{4,3,2,1,0:T(8,128)S(1)} %collective-permute-done.1.above_ref, ...), custom_call_target="tpu_custom_call", output_to_operand_aliasing={{0}: (4, {}), {1}: (5, {})} | custom-call | tf_op jit(solution)/shard_map/pallas_call | solution.py:144
  (1 shorter events, 0.0 us)
Async XLA Ops:
  1.3 8.5 %copy-start = (f32[8,8,64,128]{3,2,1,0:T(8,128)S(1)}, f32[8,8,64,128]{3,2,1,0:T(8,128)}, u32[]{:S(2)}) copy-start(f32[8,8,64,128]{3,2,1,0:T(8,128)} %adjoint_ref.2) | copy-start | bytes 6291460
  1.3 8.5 %copy-start.1 = (f32[8,8,64,128]{3,2,1,0:T(8,128)S(1)}, f32[8,8,64,128]{3,2,1,0:T(8,128)}, u32[]{:S(2)}) copy-start(f32[8,8,64,128]{3,2,1,0:T(8,128)} %order_ref.2) | copy-start | bytes 6291460
  4.4 34.6 %collective-permute-start.2 = (f32[2,8,64,128]{3,2,1,0:T(8,128)S(1)}, f32[2,8,64,128]{3,2,1,0:T(8,128)S(1)}, u32[]{:S(2)}, u32[]{:S(2)}) collective-permute-start(f32[2,8,64,128]{3,2,1,0:T(8,128)S(1)} %pad_maximum_fusion.own_ref), channel_id=1, source_target_pairs={{0,1},{1,0},{2,3},{3,2},{4,5},{5,4},{6,7},{7,6},{8,9},{9,8},{10,11... | collective-permute-start | bytes 1572872 | tf_op jit(solution)/shard_map/ppermute | solution.py:11
  10.0 35.0 %collective-permute-start.1 = (f32[2,8,1,64,128]{4,3,2,1,0:T(8,128)S(1)}, f32[2,8,1,64,128]{4,3,2,1,0:T(8,128)S(1)}, u32[]{:S(2)}, u32[]{:S(2)}) collective-permute-start(f32[2,8,1,64,128]{4,3,2,1,0:T(8,128)S(1)} %get-tuple-element.22), channel_id=1, source_target_pairs={{0,254},{2,0},{4,2},{6,4},{8,6},{10,8},{12,10},{14,12},{16,14},{18... | collective-permute-start | bytes 1572872 | tf_op jit(solution)/shard_map/ppermute | solution.py:11
  14.9 30.1 %collective-permute-start = (f32[2,8,1,64,128]{4,3,2,1,0:T(8,128)S(1)}, f32[2,8,1,64,128]{4,3,2,1,0:T(8,128)S(1)}, u32[]{:S(2)}, u32[]{:S(2)}) collective-permute-start(f32[2,8,1,64,128]{4,3,2,1,0:T(8,128)S(1)} %get-tuple-element.23), channel_id=1, source_target_pairs={{0,2},{2,4},{4,6},{6,8},{8,10},{10,12},{12,14},{14,16},{16,18},{18... | collective-permute-start | bytes 1572872 | tf_op jit(solution)/shard_map/ppermute | solution.py:11

commit v16 on v12

--- a/solution.py
+++ b/solution.py
@@ -114,9 +114,10 @@
         out_shape=[jax.ShapeDtypeStruct(order_field.shape, jnp.float32)] * 2,
     )(mobility, indices, labels, order_late, adjoint_late)
     on_chip = pl.BlockSpec(memory_space=pltpu.VMEM)
+    every = pl.BlockSpec((count, rows, depth, width), lambda p, *_: (0, 0, 0, 0))
     order_next, adjoint_order = pl.pallas_call(
         final_kernel,
-        grid_spec=scalars(num_scalar_prefetch=1, grid=(count // group,), in_specs=[block, block, on_chip, on_chip, block, block], out_specs=[block, block]),
+        grid_spec=scalars(num_scalar_prefetch=1, grid=(1,), in_specs=[every, every, on_chip, on_chip, every, every], out_specs=[every, every]),
         out_shape=[jax.ShapeDtypeStruct(order_field.shape, jnp.float32)] * 2,
     )(mobility, order_field, adjoint_next, *[pltpu.with_memory_space_constraint(x, pltpu.VMEM) for x in (own, other)],
       inner_order, inner_adjoint)

time: 47.7 us -> 48.9 us (1.025)
  Pallas kernels: 14.8 us -> 16 us
    pallas_call x1, Pallas kernels: 5.88 us -> 7.09 us  [local(): pl.pallas_call(final_kernel, grid_spec=scalars(num_scalar_prefetch=1, gri...]
  transfers between devices with their start and end apart: 3 -> 3, of which waited for: 1 -> 1; matrix products, arithmetic and copies ran while one was open for 1% -> 1% of each run, Pallas kernels for 25% -> 27%
where the time goes in v16:
time: 48.9 us; the launch traced here: 48.8 us
  waiting for transfers between devices  17.3 us (35%)
  Pallas kernels  16 us (33%)
  starting transfers between devices  10.4 us (21%)
  other arithmetic  4.29 us (9%)
  between operations  0.67 us (1%)
    ppermute x3, waiting for transfers between devices, shift_along(): lax.ppermute(cells, axis, [(i, (i + step) % count) for i in range(count)])  17.3 us
    ppermute x3, starting transfers between devices, shift_along(): lax.ppermute(cells, axis, [(i, (i + step) % count) for i in range(count)])  10.4 us
    pallas_call x1, Pallas kernels, local(): pl.pallas_call(final_kernel, grid_spec=scalars(num_scalar_prefetch=1, gri...  7.09 us
    pallas_call x1, Pallas kernels, local(): pl.pallas_call(inner_kernel, grid_spec=scalars(num_scalar_prefetch=2, gri...  6.16 us
    reduce_sum x1, other arithmetic, local(): jnp.sum(order_field * order_field, axis=0)  3.01 us
    pallas_call x1, Pallas kernels, local(): pl.pallas_call(edge_kernel, grid_spec=scalars(num_scalar_prefetch=1, grid...  2.75 us
  transfers between devices with their start and end apart: 3, of which 1 were waited for; matrix products, arithmetic and copies ran while one was open for 1% of the time, Pallas kernels for 27%

profile of v16, /device:TPU:64, one launch (start us, length us, event | category | flops | bytes accessed | tf_op | source)
XLA Modules:
  0.0 48.8 jit_solution(12995931574494315723)
XLA Ops:
  0.6 0.7 %broadcast_multiply_fusion = f32[8]{0:T(128)S(1)} fusion(f32[8]{0:T(128)} %rate_ref.5), kind=kLoop, calls=%fused_computation.9 | loop fusion | flops 8 | bytes 64 | tf_op jit(solution)/shard_map/mul | solution.py:99
  1.3 0.0 copy-start
  1.3 0.0 copy-start.1
  1.3 3.0 %multiply_reduce_fusion.1 = (f32[8,64,128]{2,1,0:T(8,128)S(1)}, f32[8,64,128]{2,1,0:T(8,128)S(1)}) fusion(f32[8,8,64,128]{3,2,1,0:T(8,128)} %order_ref.2, f32[8,8,64,128]{3,2,1,0:T(8,128)} %adjoint_ref.2, f32[8]{0:T(128)S(1)} %broadcast_multiply_fusion), kind=kLoop, calls=%fused_computation.1 | loop fusion | flops 2490368 | bytes 4718624 | tf_op jit(solution)/shard_map/reduce_sum | solution.py:100
  4.4 5.5 %collective-permute-start.2 = (f32[2,8,64,128]{3,2,1,0:T(8,128)S(1)}, f32[2,8,64,128]{3,2,1,0:T(8,128)S(1)}, u32[]{:S(2)}, u32[]{:S(2)}) collective-permute-start(f32[2,8,64,128]{3,2,1,0:T(8,128)S(1)} %pad_maximum_fusion.own_ref), channel_id=1, source_target_pairs={{0,1},{1,0},{2,3},{3,2},{4,5},{5,4},{6,7},{7,6},{8,9},{9,8},{10,11... | collective-permute-start | bytes 1572872 | tf_op jit(solution)/shard_map/ppermute | solution.py:11
  9.8 0.0 copy-done
  9.8 0.0 copy-done.1
  9.8 0.1 fusion
  9.9 0.1 fusion.1
  10.0 4.9 %collective-permute-start.1 = (f32[2,8,1,64,128]{4,3,2,1,0:T(8,128)S(1)}, f32[2,8,1,64,128]{4,3,2,1,0:T(8,128)S(1)}, u32[]{:S(2)}, u32[]{:S(2)}) collective-permute-start(f32[2,8,1,64,128]{4,3,2,1,0:T(8,128)S(1)} %get-tuple-element.20), channel_id=1, source_target_pairs={{0,254},{2,0},{4,2},{6,4},{8,6},{10,8},{12,10},{14,12},{16,14},{18... | collective-permute-start | bytes 1572872 | tf_op jit(solution)/shard_map/ppermute | solution.py:11
  14.9 0.0 collective-permute-start
  14.9 0.5 %iota_add_fusion.index_ref = s32[8]{0:T(128)} fusion(s32[]{:T(128)S(6)} %mul.26), kind=kLoop, calls=%fused_computation.8 | loop fusion | flops 8 | bytes 36 | tf_op jit(solution)/shard_map/add | solution.py:97
  15.4 6.2 %shard_map.59 = (f32[8,8,64,128]{3,2,1,0:T(8,128)}, f32[8,8,64,128]{3,2,1,0:T(8,128)}) custom-call(f32[8]{0:T(128)} %rate_ref.5, s32[8]{0:T(128)} %iota_add_fusion.index_ref, s32[8,128]{1,0:T(8,128)} %labels_ref.1, f32[8,8,64,128]{3,2,1,0:T(8,128)} %order_ref.2, f32[8,8,64,128]{3,2,1,0:T(8,128)} %adjoint_ref.2), custom_call_target="tpu_custom_call" | custom-call | tf_op jit(solution)/shard_map/pallas_call | solution.py:111
  21.6 17.3 %collective-permute-done.2.other_ref = f32[2,8,64,128]{3,2,1,0:T(8,128)S(1)} collective-permute-done((f32[2,8,64,128]{3,2,1,0:T(8,128)S(1)}, f32[2,8,64,128]{3,2,1,0:T(8,128)S(1)}, u32[]{:S(2)}, u32[]{:S(2)}) %collective-permute-start.2) | collective-permute-done | bytes 524320 | tf_op jit(solution)/shard_map/ppermute | solution.py:11
  38.9 7.1 %shard_map.60 = (f32[8,8,64,128]{3,2,1,0:T(8,128)}, f32[8,8,64,128]{3,2,1,0:T(8,128)}) custom-call(f32[8]{0:T(128)} %rate_ref.5, f32[8,8,64,128]{3,2,1,0:T(8,128)} %order_ref.2, f32[8,8,64,128]{3,2,1,0:T(8,128)} %adjoint_ref.2, f32[2,8,64,128]{3,2,1,0:T(8,128)S(1)} %pad_maximum_fusion.own_ref, f32[2,8,64,128]{3,2,1,0:T(8,128)S(1)} %collective-permute-done.2.other_ref, ...), custom_call_target="tpu_custom_call" | custom-call | tf_op jit(solution)/shard_map/pallas_call | solution.py:118
  46.0 0.0 collective-permute-done.1.above_ref
  46.0 0.0 collective-permute-done.below_ref
  46.0 2.8 %shard_map.61 = (f32[8,8,64,128]{3,2,1,0:T(8,128)}, f32[8,8,64,128]{3,2,1,0:T(8,128)}) custom-call(f32[8]{0:T(128)} %rate_ref.5, f32[2,8,1,64,128]{4,3,2,1,0:T(8,128)S(1)} %collective-permute-done.below_ref, f32[2,8,1,64,128]{4,3,2,1,0:T(8,128)S(1)} %collective-permute-done.1.above_ref, ...), custom_call_target="tpu_custom_call", output_to_operand_aliasing={{0}: (3, {}), {1}: (4, {})} | custom-call | tf_op jit(solution)/shard_map/pallas_call | solution.py:125
  (1 shorter events, 0.0 us)
Async XLA Ops:
  1.3 8.5 %copy-start = (f32[8,8,64,128]{3,2,1,0:T(8,128)S(1)}, f32[8,8,64,128]{3,2,1,0:T(8,128)}, u32[]{:S(2)}) copy-start(f32[8,8,64,128]{3,2,1,0:T(8,128)} %adjoint_ref.2) | copy-start | bytes 6291460
  1.3 8.5 %copy-start.1 = (f32[8,8,64,128]{3,2,1,0:T(8,128)S(1)}, f32[8,8,64,128]{3,2,1,0:T(8,128)}, u32[]{:S(2)}) copy-start(f32[8,8,64,128]{3,2,1,0:T(8,128)} %order_ref.2) | copy-start | bytes 6291460
  4.4 34.6 %collective-permute-start.2 = (f32[2,8,64,128]{3,2,1,0:T(8,128)S(1)}, f32[2,8,64,128]{3,2,1,0:T(8,128)S(1)}, u32[]{:S(2)}, u32[]{:S(2)}) collective-permute-start(f32[2,8,64,128]{3,2,1,0:T(8,128)S(1)} %pad_maximum_fusion.own_ref), channel_id=1, source_target_pairs={{0,1},{1,0},{2,3},{3,2},{4,5},{5,4},{6,7},{7,6},{8,9},{9,8},{10,11... | collective-permute-start | bytes 1572872 | tf_op jit(solution)/shard_map/ppermute | solution.py:11
  10.0 36.0 %collective-permute-start.1 = (f32[2,8,1,64,128]{4,3,2,1,0:T(8,128)S(1)}, f32[2,8,1,64,128]{4,3,2,1,0:T(8,128)S(1)}, u32[]{:S(2)}, u32[]{:S(2)}) collective-permute-start(f32[2,8,1,64,128]{4,3,2,1,0:T(8,128)S(1)} %get-tuple-element.20), channel_id=1, source_target_pairs={{0,254},{2,0},{4,2},{6,4},{8,6},{10,8},{12,10},{14,12},{16,14},{18... | collective-permute-start | bytes 1572872 | tf_op jit(solution)/shard_map/ppermute | solution.py:11
  14.9 31.1 %collective-permute-start = (f32[2,8,1,64,128]{4,3,2,1,0:T(8,128)S(1)}, f32[2,8,1,64,128]{4,3,2,1,0:T(8,128)S(1)}, u32[]{:S(2)}, u32[]{:S(2)}) collective-permute-start(f32[2,8,1,64,128]{4,3,2,1,0:T(8,128)S(1)} %get-tuple-element.21), channel_id=1, source_target_pairs={{0,2},{2,4},{4,6},{6,8},{8,10},{10,12},{12,14},{14,16},{16,18},{18... | collective-permute-start | bytes 1572872 | tf_op jit(solution)/shard_map/ppermute | solution.py:11

commit v17 on v12

--- a/solution.py
+++ b/solution.py
@@ -80,13 +80,17 @@
         adjoint_order_ref[q, j] = adj - ((inner_adjoint_ref[q, j] + w * squares) + o * coupled)
 
 
-def edge_kernel(rate_ref, below_ref, above_ref, order_next_in, adjoint_order_in, order_next_ref, adjoint_order_ref):
+def edge_kernel(rate_ref, flag_ref, cross_ref, below_ref, above_ref, order_next_in, adjoint_order_in,
+                order_next_ref, adjoint_order_ref):
     side = pl.program_id(0)
     count = order_next_in.shape[0]
+    crossed = jnp.where(side == 0, flag_ref[0], flag_ref[1]) != 0
     for p in range(count):
         rate = 0.1 * rate_ref[p]
         order_row = jnp.where(side == 0, below_ref[0, p, 0], above_ref[0, p, 0])
         adjoint_row = jnp.where(side == 0, below_ref[1, p, 0], above_ref[1, p, 0])
+        order_row = jnp.where(crossed, cross_ref[0, p, 0], order_row)
+        adjoint_row = jnp.where(crossed, cross_ref[1, p, 0], adjoint_row)
         order_next_ref[p, 0] = order_next_in[p, 0] + (0.5 * rate) * order_row
         adjoint_order_ref[p, 0] = adjoint_order_in[p, 0] + 0.5 * (rate * adjoint_row)
 
@@ -95,15 +99,27 @@
     count, rows, depth, width = order_field.shape
     first = lax.axis_index("op") * count
     indices = first + jnp.arange(count, dtype=jnp.int32)
+    pair = jnp.stack([order_field, adjoint_next])
+    head = pair[:, :, :1]
+    tail = pair[:, :, -1:]
+    tiles = lax.axis_size("space")
+    span = 32 if tiles % 32 == 0 else tiles
+    where = lax.axis_index("space")
+    opening = where % span == 0
+    last = (where + 1) % span == 0
+    crossing = [(i, (i + 1) % tiles) for i in range(tiles) if (i + 1) % span == 0]
+    crossing += [(i, (i - 1) % tiles) for i in range(tiles) if i % span == 0]
+    outgoing, order_sums, adjoint_sums = lax.optimization_barrier((jnp.where(last, tail, head), order_field, adjoint_next))
+    cross = lax.ppermute(outgoing, "space", crossing)
     rates = mobility[:, None, None, None]
-    weighted = 0.1 * rates * adjoint_next
-    own = jnp.stack([jnp.sum(order_field * order_field, axis=0), jnp.sum(order_field * weighted, axis=0)])
+    weighted = 0.1 * rates * adjoint_sums
+    own = jnp.stack([jnp.sum(order_sums * order_sums, axis=0), jnp.sum(order_sums * weighted, axis=0)])
     other = shift_along(own, "op", 1)
-    pair = jnp.stack([order_field, adjoint_next])
-    edges = jnp.concatenate([pair[:, :, :1], pair[:, :, -1:]], axis=2)
+    edges = jnp.concatenate([head, tail], axis=2)
     edges, own, order_late, adjoint_late = lax.optimization_barrier((edges, own, order_field, adjoint_next))
-    below = shift_along(edges[:, :, 1:], "space", 1)
-    above = shift_along(edges[:, :, :1], "space", -1)
+    below = lax.ppermute(edges[:, :, 1:], "space", [(i, i + 1) for i in range(tiles - 1) if (i + 1) % span != 0])
+    above = lax.ppermute(edges[:, :, :1], "space", [(i, i - 1) for i in range(1, tiles) if i % span != 0])
+    flags = jnp.stack([opening, last]).astype(jnp.int32)
     scalars = pltpu.PrefetchScalarGridSpec
     group = 4
     block = pl.BlockSpec((group, rows, depth, width), lambda p, *_: (p, 0, 0, 0))
@@ -123,10 +139,10 @@
     row = pl.BlockSpec((count, 1, depth, width), lambda s, *_: (0, s * (rows - 1), 0, 0))
     return pl.pallas_call(
         edge_kernel,
-        grid_spec=scalars(num_scalar_prefetch=1, grid=(2,), in_specs=[on_chip, on_chip, row, row], out_specs=[row, row]),
+        grid_spec=scalars(num_scalar_prefetch=2, grid=(2,), in_specs=[on_chip, on_chip, on_chip, row, row], out_specs=[row, row]),
         out_shape=[jax.ShapeDtypeStruct(order_field.shape, jnp.float32)] * 2,
-        input_output_aliases={3: 0, 4: 1},
-    )(mobility, *[pltpu.with_memory_space_constraint(x, pltpu.VMEM) for x in (below, above)], order_next, adjoint_order)
+        input_output_aliases={5: 0, 6: 1},
+    )(mobility, flags, *[pltpu.with_memory_space_constraint(x, pltpu.VMEM) for x in (cross, below, above)], order_next, adjoint_order)
 
 
 def solution(mesh):

time: 47.7 us -> 47.9 us (level)
  waiting for transfers between devices: 17.3 us -> 9.58 us
  starting transfers between devices: 10.4 us -> 16.5 us
  local copies, waits for them, and re-layouts: 0.11 us -> 2.14 us
    ppermute x0 -> x3, starting transfers between devices: none -> 11.1 us  [the longest x1 6.71 us: local(): cross = lax.ppermute(outgoing, 'space', crossing)]
    ppermute x3 -> x1, waiting for transfers between devices: 17.3 us -> 9.57 us  [shift_along(): lax.ppermute(cells, axis, [(i, (i + step) % count) for i in range(count)])]
    ppermute x3 -> x1, starting transfers between devices: 10.4 us -> 5.48 us  [shift_along(): lax.ppermute(cells, axis, [(i, (i + step) % count) for i in range(count)])]
    reduce_sum x1, other arithmetic: 3.01 us -> 0.59 us  [local(): jnp.sum(order_sums * order_sums, axis=0)]
    select_n x0 -> x1, other arithmetic: none -> 1.48 us  [local(): jnp.where(last, tail, head)]
    unnamed x4, local copies, waits for them, and re-layouts: 0.01 us -> 1.05 us
    slice x1, local copies, waits for them, and re-layouts: 0.1 us -> 1.09 us  [local(): edges[:, :, :1]]
    convert_element_type x0 -> x1, other arithmetic: none -> 0.59 us  [local(): flags = jnp.stack([opening, last]).astype(jnp.int32)]
  transfers between devices with their start and end apart: 3 -> 4, of which waited for: 1 -> 1; matrix products, arithmetic and copies ran while one was open for 1% -> 5% of each run, Pallas kernels for 25% -> 25%
where the time goes in v17:
time: 47.9 us; the launch traced here: 47.7 us
  starting transfers between devices  16.5 us (34%)
  Pallas kernels  14.8 us (31%)
  waiting for transfers between devices  9.58 us (20%)
  other arithmetic  3.95 us (8%)
  local copies, waits for them, and re-layouts  2.14 us (4%)
  between operations  0.74 us (2%)
    ppermute x1, waiting for transfers between devices, shift_along(): lax.ppermute(cells, axis, [(i, (i + step) % count) for i in range(count)])  9.57 us
    ppermute x1, starting transfers between devices, local(): cross = lax.ppermute(outgoing, 'space', crossing)  6.71 us
    pallas_call x1, Pallas kernels, local(): pl.pallas_call(inner_kernel, grid_spec=scalars(num_scalar_prefetch=2, gri...  6.15 us
    pallas_call x1, Pallas kernels, local(): pl.pallas_call(final_kernel, grid_spec=scalars(num_scalar_prefetch=1, gri...  5.88 us
    ppermute x1, starting transfers between devices, shift_along(): lax.ppermute(cells, axis, [(i, (i + step) % count) for i in range(count)])  5.48 us
    ppermute x1, starting transfers between devices, local(): lax.ppermute(edges[:, :, 1:], 'space', [(i, i + 1) for i in range(tiles -...  3.06 us
    pallas_call x1, Pallas kernels, local(): pl.pallas_call(edge_kernel, grid_spec=scalars(num_scalar_prefetch=2, grid...  2.78 us
    select_n x1, other arithmetic, local(): jnp.where(last, tail, head)  1.48 us
  transfers between devices with their start and end apart: 4, of which 1 were waited for; matrix products, arithmetic and copies ran while one was open for 5% of the time, Pallas kernels for 25%

profile of v17, /device:TPU:64, one launch (start us, length us, event | category | flops | bytes accessed | tf_op | source)
XLA Modules:
  0.0 47.7 jit_solution(4095527563993924614)
XLA Ops:
  0.6 0.7 %broadcast_multiply_fusion = f32[8]{0:T(128)S(1)} fusion(f32[8]{0:T(128)} %rate_ref.5), kind=kLoop, calls=%fused_computation.9 | loop fusion | flops 8 | bytes 64 | tf_op jit(solution)/shard_map/mul | solution.py:115
  1.3 0.0 copy-start
  1.3 0.0 copy-start.1
  1.3 1.5 %broadcast_select_fusion = (f32[2,8,1,64,128]{4,3,2,1,0:T(8,128)S(1)}, f32[2,8,1,64,128]{4,3,2,1,0:T(8,128)S(1)}, f32[2,8,1,64,128]{4,3,2,1,0:T(8,128)S(1)}) fusion(pred[]{:T(512)} %eq.10, f32[1,8,8,64,128]{4,3,2,1,0:T(8,128)} %bitcast.6, f32[1,8,8,64,128]{4,3,2,1,0:T(8,128)} %bitcast.7), kind=kLoop, calls=%fused_computation.6 | loop fusion | flops 393216 | bytes 5767169 | tf_op jit(solution)/shard_map/jit(_where)/select_n | solution.py:112
  2.8 0.4 copy-done
  3.2 0.6 %copy-done.1 = f32[8,8,64,128]{3,2,1,0:T(8,128)S(1)} copy-done((f32[8,8,64,128]{3,2,1,0:T(8,128)S(1)}, f32[8,8,64,128]{3,2,1,0:T(8,128)}, u32[]{:S(2)}) %copy-start.1) | copy-done | bytes 2097176
  3.8 0.6 %multiply_reduce_fusion.1 = (f32[8,64,128]{2,1,0:T(8,128)S(1)}, f32[8,64,128]{2,1,0:T(8,128)S(1)}) fusion(f32[8,8,64,128]{3,2,1,0:T(8,128)S(1)} %copy-done.1, f32[8,8,64,128]{3,2,1,0:T(8,128)S(1)} %copy-done, f32[8]{0:T(128)S(1)} %broadcast_multiply_fusion), kind=kLoop, calls=%fused_computation.1 | loop fusion | flops 2490368 | bytes 4718624 | tf_op jit(solution)/shard_map/reduce_sum | solution.py:116
  4.5 5.5 %collective-permute-start.3 = (f32[2,8,64,128]{3,2,1,0:T(8,128)S(1)}, f32[2,8,64,128]{3,2,1,0:T(8,128)S(1)}, u32[]{:S(2)}, u32[]{:S(2)}) collective-permute-start(f32[2,8,64,128]{3,2,1,0:T(8,128)S(1)} %pad_maximum_fusion.3.own_ref), channel_id=1, source_target_pairs={{0,1},{1,0},{2,3},{3,2},{4,5},{5,4},{6,7},{7,6},{8,9},{9,8},{10,11... | collective-permute-start | bytes 1572872 | tf_op jit(solution)/shard_map/ppermute | solution.py:11
  10.0 6.7 %collective-permute-start = (f32[2,8,1,64,128]{4,3,2,1,0:T(8,128)S(1)}, f32[2,8,1,64,128]{4,3,2,1,0:T(8,128)S(1)}, u32[]{:S(2)}, u32[]{:S(2)}) collective-permute-start(f32[2,8,1,64,128]{4,3,2,1,0:T(8,128)S(1)} %get-tuple-element.13), channel_id=1, source_target_pairs={{62,64},{126,128},{190,192},{254,0},{0,254},{64,62},{128,126},{192... | collective-permute-start | bytes 1572872 | tf_op jit(solution)/shard_map/ppermute | solution.py:113
  16.7 0.1 pad_maximum_fusion
  16.8 1.1 %fusion = (f32[2,8,1,64,128]{4,3,2,1,0:T(8,128)}, f32[2,8,1,64,128]{4,3,2,1,0:T(8,128)}) fusion(f32[2,8,2,64,128]{4,3,2,1,0:T(8,128)S(1)} %pad_maximum_fusion), kind=kLoop, calls=%fused_computation.10 | loop fusion | bytes 2097152 | tf_op jit(solution)/shard_map/slice | solution.py:121
  17.9 1.3 %collective-permute-start.2 = (f32[2,8,1,64,128]{4,3,2,1,0:T(8,128)}, f32[2,8,1,64,128]{4,3,2,1,0:T(8,128)S(1)}, u32[]{:S(2)}, u32[]{:S(2)}) collective-permute-start(f32[2,8,1,64,128]{4,3,2,1,0:T(8,128)} %get-tuple-element.29), channel_id=1, source_target_pairs={{2,0},{4,2},{6,4},{8,6},{10,8},{12,10},{14,12},{16,14},{18,16},{20... | collective-permute-start | bytes 1572872 | tf_op jit(solution)/shard_map/ppermute | solution.py:121
  19.1 3.1 %collective-permute-start.1 = (f32[2,8,1,64,128]{4,3,2,1,0:T(8,128)}, f32[2,8,1,64,128]{4,3,2,1,0:T(8,128)S(1)}, u32[]{:S(2)}, u32[]{:S(2)}) collective-permute-start(f32[2,8,1,64,128]{4,3,2,1,0:T(8,128)} %get-tuple-element.30), channel_id=1, source_target_pairs={{0,2},{2,4},{4,6},{6,8},{8,10},{10,12},{12,14},{14,16},{16,18},{18... | collective-permute-start | bytes 1572872 | tf_op jit(solution)/shard_map/ppermute | solution.py:120
  22.2 0.5 %iota_add_fusion.index_ref = s32[8]{0:T(128)} fusion(s32[]{:T(128)S(6)} %mul.26), kind=kLoop, calls=%fused_computation.8 | loop fusion | flops 8 | bytes 36 | tf_op jit(solution)/shard_map/add | solution.py:101
  22.7 6.1 %shard_map.59 = (f32[8,8,64,128]{3,2,1,0:T(8,128)}, f32[8,8,64,128]{3,2,1,0:T(8,128)}) custom-call(f32[8]{0:T(128)} %rate_ref.5, s32[8]{0:T(128)} %iota_add_fusion.index_ref, s32[8,128]{1,0:T(8,128)} %labels_ref.1, f32[8,8,64,128]{3,2,1,0:T(8,128)} %order_ref.2, f32[8,8,64,128]{3,2,1,0:T(8,128)} %adjoint_ref.2), custom_call_target="tpu_custom_call" | custom-call | tf_op jit(solution)/shard_map/pallas_call | solution.py:127
  28.9 0.6 %add_convert_fusion.flag_ref = s32[2]{0:T(128)} fusion(pred[1]{0:T(512)(128)(4,1)} %bitcast.1, pred[1]{0:T(512)(128)(4,1)} %bitcast), kind=kLoop, calls=%fused_computation.7 | loop fusion | flops 4 | bytes 10 | tf_op jit(solution)/shard_map/convert_element_type | solution.py:122
  29.5 9.6 %collective-permute-done.3.other_ref = f32[2,8,64,128]{3,2,1,0:T(8,128)S(1)} collective-permute-done((f32[2,8,64,128]{3,2,1,0:T(8,128)S(1)}, f32[2,8,64,128]{3,2,1,0:T(8,128)S(1)}, u32[]{:S(2)}, u32[]{:S(2)}) %collective-permute-start.3) | collective-permute-done | bytes 524320 | tf_op jit(solution)/shard_map/ppermute | solution.py:11
  39.1 5.9 %shard_map.60 = (f32[8,8,64,128]{3,2,1,0:T(8,128)}, f32[8,8,64,128]{3,2,1,0:T(8,128)}) custom-call(f32[8]{0:T(128)} %rate_ref.5, f32[8,8,64,128]{3,2,1,0:T(8,128)} %order_ref.2, f32[8,8,64,128]{3,2,1,0:T(8,128)} %adjoint_ref.2, f32[2,8,64,128]{3,2,1,0:T(8,128)S(1)} %pad_maximum_fusion.3.own_ref, f32[2,8,64,128]{3,2,1,0:T(8,128)S(1)} %collective-permute-done.3.other_ref, ...), custom_call_target="tpu_custom_call" | custom-call | tf_op jit(solution)/shard_map/pallas_call | solution.py:133
  44.9 0.0 collective-permute-done.cross_ref
  44.9 0.0 collective-permute-done.2.above_ref
  44.9 0.0 collective-permute-done.1.below_ref
  45.0 2.8 %shard_map.61 = (f32[8,8,64,128]{3,2,1,0:T(8,128)}, f32[8,8,64,128]{3,2,1,0:T(8,128)}) custom-call(f32[8]{0:T(128)} %rate_ref.5, s32[2]{0:T(128)} %add_convert_fusion.flag_ref, f32[2,8,1,64,128]{4,3,2,1,0:T(8,128)S(1)} %collective-permute-done.cross_ref, ...), custom_call_target="tpu_custom_call", output_to_operand_aliasing={{0}: (5, {}), {1}: (6, {})} | custom-call | tf_op jit(solution)/shard_map/pallas_call | solution.py:140
  (1 shorter events, 0.0 us)
Async XLA Ops:
  1.3 1.9 %copy-start = (f32[8,8,64,128]{3,2,1,0:T(8,128)S(1)}, f32[8,8,64,128]{3,2,1,0:T(8,128)}, u32[]{:S(2)}) copy-start(f32[8,8,64,128]{3,2,1,0:T(8,128)} %adjoint_ref.2) | copy-start | bytes 6291460
  1.3 2.5 %copy-start.1 = (f32[8,8,64,128]{3,2,1,0:T(8,128)S(1)}, f32[8,8,64,128]{3,2,1,0:T(8,128)}, u32[]{:S(2)}) copy-start(f32[8,8,64,128]{3,2,1,0:T(8,128)} %order_ref.2) | copy-start | bytes 6291460
  4.5 34.6 %collective-permute-start.3 = (f32[2,8,64,128]{3,2,1,0:T(8,128)S(1)}, f32[2,8,64,128]{3,2,1,0:T(8,128)S(1)}, u32[]{:S(2)}, u32[]{:S(2)}) collective-permute-start(f32[2,8,64,128]{3,2,1,0:T(8,128)S(1)} %pad_maximum_fusion.3.own_ref), channel_id=1, source_target_pairs={{0,1},{1,0},{2,3},{3,2},{4,5},{5,4},{6,7},{7,6},{8,9},{9,8},{10,11... | collective-permute-start | bytes 1572872 | tf_op jit(solution)/shard_map/ppermute | solution.py:11
  10.0 35.0 %collective-permute-start = (f32[2,8,1,64,128]{4,3,2,1,0:T(8,128)S(1)}, f32[2,8,1,64,128]{4,3,2,1,0:T(8,128)S(1)}, u32[]{:S(2)}, u32[]{:S(2)}) collective-permute-start(f32[2,8,1,64,128]{4,3,2,1,0:T(8,128)S(1)} %get-tuple-element.13), channel_id=1, source_target_pairs={{62,64},{126,128},{190,192},{254,0},{0,254},{64,62},{128,126},{192... | collective-permute-start | bytes 1572872 | tf_op jit(solution)/shard_map/ppermute | solution.py:113
  17.9 27.1 %collective-permute-start.2 = (f32[2,8,1,64,128]{4,3,2,1,0:T(8,128)}, f32[2,8,1,64,128]{4,3,2,1,0:T(8,128)S(1)}, u32[]{:S(2)}, u32[]{:S(2)}) collective-permute-start(f32[2,8,1,64,128]{4,3,2,1,0:T(8,128)} %get-tuple-element.29), channel_id=1, source_target_pairs={{2,0},{4,2},{6,4},{8,6},{10,8},{12,10},{14,12},{16,14},{18,16},{20... | collective-permute-start | bytes 1572872 | tf_op jit(solution)/shard_map/ppermute | solution.py:121
  19.1 25.8 %collective-permute-start.1 = (f32[2,8,1,64,128]{4,3,2,1,0:T(8,128)}, f32[2,8,1,64,128]{4,3,2,1,0:T(8,128)S(1)}, u32[]{:S(2)}, u32[]{:S(2)}) collective-permute-start(f32[2,8,1,64,128]{4,3,2,1,0:T(8,128)} %get-tuple-element.30), channel_id=1, source_target_pairs={{0,2},{2,4},{4,6},{6,8},{8,10},{10,12},{12,14},{14,16},{16,18},{18... | collective-permute-start | bytes 1572872 | tf_op jit(solution)/shard_map/ppermute | solution.py:120

commit v18 on v13

--- a/solution.py
+++ b/solution.py
@@ -66,8 +66,7 @@
         final_one(q, p, rate_ref, order_ref, adjoint_ref, own_ref, other_ref,
                   inner_order_ref, inner_adjoint_ref, order_next_ref, adjoint_order_ref)
         for s, r in enumerate((0, rows - 1)):
-            edge_ref[0, s, p] = order_next_ref[q, r]
-            edge_ref[1, s, p] = adjoint_order_ref[q, r]
+            edge_ref[s, p] = adjoint_order_ref[q, r]
 
 
 def final_one(q, p, rate_ref, order_ref, adjoint_ref, own_ref, other_ref, inner_order_ref, inner_adjoint_ref,
@@ -85,13 +84,21 @@
 
 
 def edge_kernel(rate_ref, below_ref, above_ref, edge_ref, order_next_in, adjoint_order_in, order_next_ref, adjoint_order_ref,
-                rows_buf, store_sem):
+                rows_buf, load_sem, store_sem):
     count, rows = order_next_in.shape[:2]
+    loads = [
+        pltpu.make_async_copy(order_next_in.at[:, pl.ds(r, 1)], rows_buf.at[0, s], load_sem.at[s])
+        for s, r in enumerate((0, rows - 1))
+    ]
+    for copy in loads:
+        copy.start()
+    for copy in loads:
+        copy.wait()
     for s, halo in enumerate((below_ref, above_ref)):
         for p in range(count):
             rate = 0.1 * rate_ref[p]
-            rows_buf[0, s, p, 0] = edge_ref[0, s, p] + (0.5 * rate) * halo[0, p, 0]
-            rows_buf[1, s, p, 0] = edge_ref[1, s, p] + 0.5 * (rate * halo[1, p, 0])
+            rows_buf[0, s, p, 0] = rows_buf[0, s, p, 0] + (0.5 * rate) * halo[0, p, 0]
+            rows_buf[1, s, p, 0] = edge_ref[s, p] + 0.5 * (rate * halo[1, p, 0])
     stores = []
     for a, target in enumerate((order_next_ref, adjoint_order_ref)):
         for s, r in enumerate((0, rows - 1)):
@@ -125,18 +132,17 @@
         out_shape=[jax.ShapeDtypeStruct(order_field.shape, jnp.float32)] * 2,
     )(mobility, indices, labels, order_late, adjoint_late)
     on_chip = pl.BlockSpec(memory_space=pltpu.VMEM)
-    whole = pl.BlockSpec((2, rows, depth, width), lambda p, *_: (0, 0, 0, 0))
     order_next, adjoint_order, edge_rows = pl.pallas_call(
         final_kernel,
         grid_spec=scalars(
             num_scalar_prefetch=1,
             grid=(count // group,),
-            in_specs=[block, block, whole, whole, block, block],
+            in_specs=[block, block, on_chip, on_chip, block, block],
             out_specs=[block, block, on_chip],
         ),
         out_shape=[jax.ShapeDtypeStruct(order_field.shape, jnp.float32)] * 2
-        + [pltpu.VMEM((2, 2, count, depth, width), jnp.float32)],
-    )(mobility, order_field, adjoint_next, own, other,
+        + [pltpu.VMEM((2, count, depth, width), jnp.float32)],
+    )(mobility, order_field, adjoint_next, *[pltpu.with_memory_space_constraint(x, pltpu.VMEM) for x in (own, other)],
       inner_order, inner_adjoint)
     anywhere = pl.BlockSpec(memory_space=pl.ANY)
     return pl.pallas_call(
@@ -144,7 +150,11 @@
         in_specs=[pl.BlockSpec(memory_space=pltpu.SMEM), on_chip, on_chip, on_chip, anywhere, anywhere],
         out_specs=[anywhere, anywhere],
         out_shape=[jax.ShapeDtypeStruct(order_field.shape, jnp.float32)] * 2,
-        scratch_shapes=[pltpu.VMEM((2, 2, count, 1, depth, width), jnp.float32), pltpu.SemaphoreType.DMA((2, 2))],
+        scratch_shapes=[
+            pltpu.VMEM((2, 2, count, 1, depth, width), jnp.float32),
+            pltpu.SemaphoreType.DMA((2,)),
+            pltpu.SemaphoreType.DMA((2, 2)),
+        ],
         input_output_aliases={4: 0, 5: 1},
     )(mobility, *[pltpu.with_memory_space_constraint(x, pltpu.VMEM) for x in (below, above, edge_rows)], order_next, adjoint_order)
 

time: 47.9 us -> 47.8 us (level)
  Pallas kernels: 14.1 us -> 14.9 us
  local copies, waits for them, and re-layouts: 1.84 us -> 1.05 us
    pallas_call x1, Pallas kernels: 1.77 us -> 2.82 us  [local(): pl.pallas_call(edge_kernel, in_specs=[pl.BlockSpec(memory_space=pltpu.SME...]
    unnamed x8 -> x4, local copies, waits for them, and re-layouts: 0.79 us -> 0.01 us
  transfers between devices with their start and end apart: 3 -> 3, of which waited for: 1 -> 1; matrix products, arithmetic and copies ran while one was open for 3% -> 3% of each run, Pallas kernels for 26% -> 25%
where the time goes in v18:
time: 47.8 us; the launch traced here: 47.7 us
  waiting for transfers between devices  16.5 us (35%)
  Pallas kernels  14.9 us (31%)
  starting transfers between devices  10.3 us (22%)
  other arithmetic  4.29 us (9%)
  local copies, waits for them, and re-layouts  1.05 us (2%)
  between operations  0.66 us (1%)
    ppermute x3, waiting for transfers between devices, shift_along(): lax.ppermute(cells, axis, [(i, (i + step) % count) for i in range(count)])  16.5 us
    ppermute x3, starting transfers between devices, shift_along(): lax.ppermute(cells, axis, [(i, (i + step) % count) for i in range(count)])  10.3 us
    pallas_call x1, Pallas kernels, local(): pl.pallas_call(inner_kernel, grid_spec=scalars(num_scalar_prefetch=2, gri...  6.16 us
    pallas_call x1, Pallas kernels, local(): pl.pallas_call(final_kernel, grid_spec=scalars(num_scalar_prefetch=1, gri...  5.92 us
    reduce_sum x1, other arithmetic, local(): jnp.sum(order_field * order_field, axis=0)  3.01 us
    pallas_call x1, Pallas kernels, local(): pl.pallas_call(edge_kernel, in_specs=[pl.BlockSpec(memory_space=pltpu.SME...  2.82 us
    slice x1, local copies, waits for them, and re-layouts, local(): above = shift_along(edges[:, :, :1], 'space', -1)  1.05 us
  transfers between devices with their start and end apart: 3, of which 1 were waited for; matrix products, arithmetic and copies ran while one was open for 3% of the time, Pallas kernels for 25%

profile of v18, /device:TPU:64, one launch (start us, length us, event | category | flops | bytes accessed | tf_op | source)
XLA Modules:
  0.0 47.7 jit_solution(5015034611856054813)
XLA Ops:
  0.6 0.7 %broadcast_multiply_fusion = f32[8]{0:T(128)S(1)} fusion(f32[8]{0:T(128)} %rate_ref.5), kind=kLoop, calls=%fused_computation.9 | loop fusion | flops 8 | bytes 64 | tf_op jit(solution)/shard_map/mul | solution.py:117
  1.3 0.0 copy-start
  1.3 0.0 copy-start.1
  1.3 3.0 %multiply_reduce_fusion.1 = (f32[8,64,128]{2,1,0:T(8,128)S(1)}, f32[8,64,128]{2,1,0:T(8,128)S(1)}) fusion(f32[8,8,64,128]{3,2,1,0:T(8,128)} %order_ref.2, f32[8,8,64,128]{3,2,1,0:T(8,128)} %adjoint_ref.2, f32[8]{0:T(128)S(1)} %broadcast_multiply_fusion), kind=kLoop, calls=%fused_computation.1 | loop fusion | flops 2490368 | bytes 4718624 | tf_op jit(solution)/shard_map/reduce_sum | solution.py:118
  4.4 5.5 %collective-permute-start.2 = (f32[2,8,64,128]{3,2,1,0:T(8,128)S(1)}, f32[2,8,64,128]{3,2,1,0:T(8,128)S(1)}, u32[]{:S(2)}, u32[]{:S(2)}) collective-permute-start(f32[2,8,64,128]{3,2,1,0:T(8,128)S(1)} %pad_maximum_fusion.own_ref), channel_id=1, source_target_pairs={{0,1},{1,0},{2,3},{3,2},{4,5},{5,4},{6,7},{7,6},{8,9},{9,8},{10,11... | collective-permute-start | bytes 1572872 | tf_op jit(solution)/shard_map/ppermute | solution.py:11
  9.8 0.0 copy-done
  9.8 0.0 copy-done.1
  9.8 0.1 fusion
  9.9 1.0 %fusion.1 = (f32[2,8,1,64,128]{4,3,2,1,0:T(8,128)}, f32[2,8,1,64,128]{4,3,2,1,0:T(8,128)}) fusion(f32[2,8,2,64,128]{4,3,2,1,0:T(8,128)S(1)} %fusion), kind=kLoop, calls=%fused_computation.10 | loop fusion | bytes 2097152 | tf_op jit(solution)/shard_map/slice | solution.py:124
  11.0 4.8 %collective-permute-start.1 = (f32[2,8,1,64,128]{4,3,2,1,0:T(8,128)}, f32[2,8,1,64,128]{4,3,2,1,0:T(8,128)S(1)}, u32[]{:S(2)}, u32[]{:S(2)}) collective-permute-start(f32[2,8,1,64,128]{4,3,2,1,0:T(8,128)} %get-tuple-element.22), channel_id=1, source_target_pairs={{0,254},{2,0},{4,2},{6,4},{8,6},{10,8},{12,10},{14,12},{16,14},{18... | collective-permute-start | bytes 1572872 | tf_op jit(solution)/shard_map/ppermute | solution.py:11
  15.8 0.0 collective-permute-start
  15.8 0.5 %iota_add_fusion.index_ref = s32[8]{0:T(128)} fusion(s32[]{:T(128)S(6)} %mul.26), kind=kLoop, calls=%fused_computation.8 | loop fusion | flops 8 | bytes 36 | tf_op jit(solution)/shard_map/add | solution.py:115
  16.3 6.2 %shard_map.59 = (f32[8,8,64,128]{3,2,1,0:T(8,128)}, f32[8,8,64,128]{3,2,1,0:T(8,128)}) custom-call(f32[8]{0:T(128)} %rate_ref.5, s32[8]{0:T(128)} %iota_add_fusion.index_ref, s32[8,128]{1,0:T(8,128)} %labels_ref.1, f32[8,8,64,128]{3,2,1,0:T(8,128)} %order_ref.2, f32[8,8,64,128]{3,2,1,0:T(8,128)} %adjoint_ref.2), custom_call_target="tpu_custom_call" | custom-call | tf_op jit(solution)/shard_map/pallas_call | solution.py:129
  22.4 16.5 %collective-permute-done.2.other_ref = f32[2,8,64,128]{3,2,1,0:T(8,128)S(1)} collective-permute-done((f32[2,8,64,128]{3,2,1,0:T(8,128)S(1)}, f32[2,8,64,128]{3,2,1,0:T(8,128)S(1)}, u32[]{:S(2)}, u32[]{:S(2)}) %collective-permute-start.2) | collective-permute-done | bytes 524320 | tf_op jit(solution)/shard_map/ppermute | solution.py:11
  38.9 5.9 %shard_map.60 = (f32[8,8,64,128]{3,2,1,0:T(8,128)}, f32[8,8,64,128]{3,2,1,0:T(8,128)}, f32[2,8,64,128]{3,2,1,0:T(8,128)S(1)}) custom-call(f32[8]{0:T(128)} %rate_ref.5, f32[8,8,64,128]{3,2,1,0:T(8,128)} %order_ref.2, f32[8,8,64,128]{3,2,1,0:T(8,128)} %adjoint_ref.2, f32[2,8,64,128]{3,2,1,0:T(8,128)S(1)} %pad_maximum_fusion.own_ref, ...), custom_call_target="tpu_custom_call" | custom-call | tf_op jit(solution)/shard_map/pallas_call | solution.py:135
  44.9 0.0 collective-permute-done.1.above_ref
  44.9 0.0 collective-permute-done.below_ref
  44.9 2.8 %shard_map.61 = (f32[8,8,64,128]{3,2,1,0:T(8,128)}, f32[8,8,64,128]{3,2,1,0:T(8,128)}) custom-call(f32[8]{0:T(128)} %rate_ref.5, f32[2,8,1,64,128]{4,3,2,1,0:T(8,128)S(1)} %collective-permute-done.below_ref, f32[2,8,1,64,128]{4,3,2,1,0:T(8,128)S(1)} %collective-permute-done.1.above_ref, ...), custom_call_target="tpu_custom_call", output_to_operand_aliasing={{0}: (4, {}), {1}: (5, {})} | custom-call | tf_op jit(solution)/shard_map/pallas_call | solution.py:148
  (1 shorter events, 0.0 us)
Async XLA Ops:
  1.3 8.5 %copy-start = (f32[8,8,64,128]{3,2,1,0:T(8,128)S(1)}, f32[8,8,64,128]{3,2,1,0:T(8,128)}, u32[]{:S(2)}) copy-start(f32[8,8,64,128]{3,2,1,0:T(8,128)} %adjoint_ref.2) | copy-start | bytes 6291460
  1.3 8.5 %copy-start.1 = (f32[8,8,64,128]{3,2,1,0:T(8,128)S(1)}, f32[8,8,64,128]{3,2,1,0:T(8,128)}, u32[]{:S(2)}) copy-start(f32[8,8,64,128]{3,2,1,0:T(8,128)} %order_ref.2) | copy-start | bytes 6291460
  4.4 34.6 %collective-permute-start.2 = (f32[2,8,64,128]{3,2,1,0:T(8,128)S(1)}, f32[2,8,64,128]{3,2,1,0:T(8,128)S(1)}, u32[]{:S(2)}, u32[]{:S(2)}) collective-permute-start(f32[2,8,64,128]{3,2,1,0:T(8,128)S(1)} %pad_maximum_fusion.own_ref), channel_id=1, source_target_pairs={{0,1},{1,0},{2,3},{3,2},{4,5},{5,4},{6,7},{7,6},{8,9},{9,8},{10,11... | collective-permute-start | bytes 1572872 | tf_op jit(solution)/shard_map/ppermute | solution.py:11
  11.0 33.9 %collective-permute-start.1 = (f32[2,8,1,64,128]{4,3,2,1,0:T(8,128)}, f32[2,8,1,64,128]{4,3,2,1,0:T(8,128)S(1)}, u32[]{:S(2)}, u32[]{:S(2)}) collective-permute-start(f32[2,8,1,64,128]{4,3,2,1,0:T(8,128)} %get-tuple-element.22), channel_id=1, source_target_pairs={{0,254},{2,0},{4,2},{6,4},{8,6},{10,8},{12,10},{14,12},{16,14},{18... | collective-permute-start | bytes 1572872 | tf_op jit(solution)/shard_map/ppermute | solution.py:11
  15.8 29.1 %collective-permute-start = (f32[2,8,1,64,128]{4,3,2,1,0:T(8,128)}, f32[2,8,1,64,128]{4,3,2,1,0:T(8,128)S(1)}, u32[]{:S(2)}, u32[]{:S(2)}) collective-permute-start(f32[2,8,1,64,128]{4,3,2,1,0:T(8,128)} %get-tuple-element.23), channel_id=1, source_target_pairs={{0,2},{2,4},{4,6},{6,8},{8,10},{10,12},{12,14},{14,16},{16,18},{18... | collective-permute-start | bytes 1572872 | tf_op jit(solution)/shard_map/ppermute | solution.py:11

commit v19 on v12

--- a/solution.py
+++ b/solution.py
@@ -95,9 +95,13 @@
     count, rows, depth, width = order_field.shape
     first = lax.axis_index("op") * count
     indices = first + jnp.arange(count, dtype=jnp.int32)
-    rates = mobility[:, None, None, None]
-    weighted = 0.1 * rates * adjoint_next
-    own = jnp.stack([jnp.sum(order_field * order_field, axis=0), jnp.sum(order_field * weighted, axis=0)])
+    scale = 0.1 * mobility
+    squares = order_field[0] * order_field[0]
+    coupled = order_field[0] * (scale[0] * adjoint_next[0])
+    for p in range(1, count):
+        squares = squares + order_field[p] * order_field[p]
+        coupled = coupled + order_field[p] * (scale[p] * adjoint_next[p])
+    own = jnp.stack([squares, coupled])
     other = shift_along(own, "op", 1)
     pair = jnp.stack([order_field, adjoint_next])
     edges = jnp.concatenate([pair[:, :, :1], pair[:, :, -1:]], axis=2)

time: 47.7 us -> 54.5 us (1.14)
  other arithmetic: 4.29 us -> 10.3 us
  local copies, waits for them, and re-layouts: 0.11 us -> 0.79 us
    add x0 -> x2, other arithmetic: none -> 8.85 us  [the longest x1 7.17 us: local(): coupled = coupled + order_field[p] * (scale[p] * adjoint_next[p])]
    reduce_sum x1 -> x0, other arithmetic: 3.01 us -> none  [local(): jnp.sum(order_field * order_field, axis=0)]
    slice x0 -> x1, local copies, waits for them, and re-layouts: none -> 0.67 us  [local(): coupled = order_field[0] * (scale[0] * adjoint_next[0])]
  transfers between devices with their start and end apart: 3 -> 3, of which waited for: 1 -> 1; matrix products, arithmetic and copies ran while one was open for 1% -> 1% of each run, Pallas kernels for 25% -> 22%
where the time goes in v19:
time: 54.5 us; the launch traced here: 54.3 us
  waiting for transfers between devices  17.3 us (32%)
  Pallas kernels  14.8 us (27%)
  starting transfers between devices  10.4 us (19%)
  other arithmetic  10.3 us (19%)
  local copies, waits for them, and re-layouts  0.79 us (1%)
  between operations  0.69 us (1%)
    ppermute x3, waiting for transfers between devices, shift_along(): lax.ppermute(cells, axis, [(i, (i + step) % count) for i in range(count)])  17.3 us
    ppermute x3, starting transfers between devices, shift_along(): lax.ppermute(cells, axis, [(i, (i + step) % count) for i in range(count)])  10.4 us
    add x1, other arithmetic, local(): coupled = coupled + order_field[p] * (scale[p] * adjoint_next[p])  7.17 us
    pallas_call x1, Pallas kernels, local(): pl.pallas_call(inner_kernel, grid_spec=scalars(num_scalar_prefetch=2, gri...  6.16 us
    pallas_call x1, Pallas kernels, local(): pl.pallas_call(final_kernel, grid_spec=scalars(num_scalar_prefetch=1, gri...  5.88 us
    pallas_call x1, Pallas kernels, local(): pl.pallas_call(edge_kernel, grid_spec=scalars(num_scalar_prefetch=1, grid...  2.75 us
    add x1, other arithmetic, local(): squares = squares + order_field[p] * order_field[p]  1.68 us
  transfers between devices with their start and end apart: 3, of which 1 were waited for; matrix products, arithmetic and copies ran while one was open for 1% of the time, Pallas kernels for 22%

profile of v19, /device:TPU:64, one launch (start us, length us, event | category | flops | bytes accessed | tf_op | source)
XLA Modules:
  0.0 54.3 jit_solution(2236878139204633533)
XLA Ops:
  0.6 0.0 copy-start
  0.6 0.8 %broadcast_multiply_fusion = f32[8]{0:T(128)S(1)} fusion(f32[8]{0:T(128)} %rate_ref.5), kind=kLoop, calls=%fused_computation.9 | loop fusion | flops 8 | bytes 64 | tf_op jit(solution)/shard_map/mul | solution.py:98
  1.4 0.7 %fusion.2 = (f32[1]{0:T(128)}, f32[1]{0:T(128)}, f32[1]{0:T(128)}, f32[1]{0:T(128)}, f32[1]{0:T(128)}, /*index=5*/f32[1]{0:T(128)}, f32[1]{0:T(128)}, f32[1]{0:T(128)}) fusion(f32[8]{0:T(128)S(1)} %broadcast_multiply_fusion), kind=kLoop, calls=%fused_computation.11 | loop fusion | bytes 64 | tf_op jit(solution)/shard_map/slice | solution.py:100
  2.1 1.7 %multiply_add_fusion.1 = f32[1,8,64,128]{3,2,1,0:T(8,128)S(1)} fusion(f32[8,8,64,128]{3,2,1,0:T(8,128)} %order_ref.2), kind=kLoop, calls=%fused_computation.7 | loop fusion | flops 983040 | bytes 2359296 | tf_op jit(solution)/shard_map/add | solution.py:102
  3.8 0.0 copy-done
  3.8 0.0 copy-start.1
  3.8 7.2 %multiply_add_fusion = f32[1,8,64,128]{3,2,1,0:T(8,128)S(1)} fusion(f32[8,8,64,128]{3,2,1,0:T(8,128)} %adjoint_ref.2, f32[8,8,64,128]{3,2,1,0:T(8,128)S(1)} %copy-done, f32[]{:T(128)} %bitcast.9, f32[]{:T(128)} %bitcast.8, f32[]{:T(128)} %bitcast.7, f32[]{:T(128)} %bitcast.6, f32[]{:T(128)} %bitcast.5, f32[]{:T(128)} %bitcast.4, f32[]{:T(128)} %bitcast.3, ...), kind=kLoop, calls=%fused_computation.6 | loop fusion | flops 1507328 | bytes 4456480 | tf_op jit(solution)/shard_map/add | solution.py:103
  11.0 5.5 %collective-permute-start.2 = (f32[2,8,64,128]{3,2,1,0:T(8,128)S(1)}, f32[2,8,64,128]{3,2,1,0:T(8,128)S(1)}, u32[]{:S(2)}, u32[]{:S(2)}) collective-permute-start(f32[2,8,64,128]{3,2,1,0:T(8,128)S(1)} %pad_maximum_fusion.own_ref), channel_id=1, source_target_pairs={{0,1},{1,0},{2,3},{3,2},{4,5},{5,4},{6,7},{7,6},{8,9},{9,8},{10,11... | collective-permute-start | bytes 1572872 | tf_op jit(solution)/shard_map/ppermute | solution.py:11
  16.5 0.0 copy-done.1
  16.5 0.1 fusion
  16.6 0.1 fusion.1
  16.7 4.9 %collective-permute-start.1 = (f32[2,8,1,64,128]{4,3,2,1,0:T(8,128)S(1)}, f32[2,8,1,64,128]{4,3,2,1,0:T(8,128)S(1)}, u32[]{:S(2)}, u32[]{:S(2)}) collective-permute-start(f32[2,8,1,64,128]{4,3,2,1,0:T(8,128)S(1)} %get-tuple-element.18), channel_id=1, source_target_pairs={{0,254},{2,0},{4,2},{6,4},{8,6},{10,8},{12,10},{14,12},{16,14},{18... | collective-permute-start | bytes 1572872 | tf_op jit(solution)/shard_map/ppermute | solution.py:11
  21.6 0.0 collective-permute-start
  21.6 0.5 iota_add_fusion.index_ref
  22.2 6.2 %shard_map.59 = (f32[8,8,64,128]{3,2,1,0:T(8,128)}, f32[8,8,64,128]{3,2,1,0:T(8,128)}) custom-call(f32[8]{0:T(128)} %rate_ref.5, s32[8]{0:T(128)} %iota_add_fusion.index_ref, s32[8,128]{1,0:T(8,128)} %labels_ref.1, f32[8,8,64,128]{3,2,1,0:T(8,128)} %order_ref.2, f32[8,8,64,128]{3,2,1,0:T(8,128)} %adjoint_ref.2), custom_call_target="tpu_custom_call" | custom-call | tf_op jit(solution)/shard_map/pallas_call | solution.py:115
  28.3 17.3 %collective-permute-done.2.other_ref = f32[2,8,64,128]{3,2,1,0:T(8,128)S(1)} collective-permute-done((f32[2,8,64,128]{3,2,1,0:T(8,128)S(1)}, f32[2,8,64,128]{3,2,1,0:T(8,128)S(1)}, u32[]{:S(2)}, u32[]{:S(2)}) %collective-permute-start.2) | collective-permute-done | bytes 524320 | tf_op jit(solution)/shard_map/ppermute | solution.py:11
  45.6 5.9 %shard_map.60 = (f32[8,8,64,128]{3,2,1,0:T(8,128)}, f32[8,8,64,128]{3,2,1,0:T(8,128)}) custom-call(f32[8]{0:T(128)} %rate_ref.5, f32[8,8,64,128]{3,2,1,0:T(8,128)} %order_ref.2, f32[8,8,64,128]{3,2,1,0:T(8,128)} %adjoint_ref.2, f32[2,8,64,128]{3,2,1,0:T(8,128)S(1)} %pad_maximum_fusion.own_ref, f32[2,8,64,128]{3,2,1,0:T(8,128)S(1)} %collective-permute-done.2.other_ref, ...), custom_call_target="tpu_custom_call" | custom-call | tf_op jit(solution)/shard_map/pallas_call | solution.py:121
  51.5 0.0 collective-permute-done.1.above_ref
  51.5 0.0 collective-permute-done.below_ref
  51.5 2.8 %shard_map.61 = (f32[8,8,64,128]{3,2,1,0:T(8,128)}, f32[8,8,64,128]{3,2,1,0:T(8,128)}) custom-call(f32[8]{0:T(128)} %rate_ref.5, f32[2,8,1,64,128]{4,3,2,1,0:T(8,128)S(1)} %collective-permute-done.below_ref, f32[2,8,1,64,128]{4,3,2,1,0:T(8,128)S(1)} %collective-permute-done.1.above_ref, ...), custom_call_target="tpu_custom_call", output_to_operand_aliasing={{0}: (3, {}), {1}: (4, {})} | custom-call | tf_op jit(solution)/shard_map/pallas_call | solution.py:128
  (1 shorter events, 0.0 us)
Async XLA Ops:
  0.6 3.2 %copy-start = (f32[8,8,64,128]{3,2,1,0:T(8,128)S(1)}, f32[8,8,64,128]{3,2,1,0:T(8,128)}, u32[]{:S(2)}) copy-start(f32[8,8,64,128]{3,2,1,0:T(8,128)} %order_ref.2) | copy-start | bytes 6291460
  3.8 12.7 %copy-start.1 = (f32[8,8,64,128]{3,2,1,0:T(8,128)S(1)}, f32[8,8,64,128]{3,2,1,0:T(8,128)}, u32[]{:S(2)}) copy-start(f32[8,8,64,128]{3,2,1,0:T(8,128)} %adjoint_ref.2) | copy-start | bytes 6291460
  11.0 34.6 %collective-permute-start.2 = (f32[2,8,64,128]{3,2,1,0:T(8,128)S(1)}, f32[2,8,64,128]{3,2,1,0:T(8,128)S(1)}, u32[]{:S(2)}, u32[]{:S(2)}) collective-permute-start(f32[2,8,64,128]{3,2,1,0:T(8,128)S(1)} %pad_maximum_fusion.own_ref), channel_id=1, source_target_pairs={{0,1},{1,0},{2,3},{3,2},{4,5},{5,4},{6,7},{7,6},{8,9},{9,8},{10,11... | collective-permute-start | bytes 1572872 | tf_op jit(solution)/shard_map/ppermute | solution.py:11
  16.7 34.7 %collective-permute-start.1 = (f32[2,8,1,64,128]{4,3,2,1,0:T(8,128)S(1)}, f32[2,8,1,64,128]{4,3,2,1,0:T(8,128)S(1)}, u32[]{:S(2)}, u32[]{:S(2)}) collective-permute-start(f32[2,8,1,64,128]{4,3,2,1,0:T(8,128)S(1)} %get-tuple-element.18), channel_id=1, source_target_pairs={{0,254},{2,0},{4,2},{6,4},{8,6},{10,8},{12,10},{14,12},{16,14},{18... | collective-permute-start | bytes 1572872 | tf_op jit(solution)/shard_map/ppermute | solution.py:11
  21.6 29.9 %collective-permute-start = (f32[2,8,1,64,128]{4,3,2,1,0:T(8,128)S(1)}, f32[2,8,1,64,128]{4,3,2,1,0:T(8,128)S(1)}, u32[]{:S(2)}, u32[]{:S(2)}) collective-permute-start(f32[2,8,1,64,128]{4,3,2,1,0:T(8,128)S(1)} %get-tuple-element.19), channel_id=1, source_target_pairs={{0,2},{2,4},{4,6},{6,8},{8,10},{10,12},{12,14},{14,16},{16,18},{18... | collective-permute-start | bytes 1572872 | tf_op jit(solution)/shard_map/ppermute | solution.py:11

commit v20 on v12

--- a/solution.py
+++ b/solution.py
@@ -25,11 +25,11 @@
     return laplace
 
 
-def inner_kernel(rate_ref, index_ref, labels_ref, order_ref, adjoint_ref, inner_order_ref, inner_adjoint_ref):
+def inner_kernel(rate_ref, index_ref, labels_ref, order_ref, adjoint_ref, inner_ref):
     group = order_ref.shape[0]
     for q in range(group):
         inner_one(q, pl.program_id(0) * group + q, rate_ref, index_ref, labels_ref, order_ref, adjoint_ref,
-                  inner_order_ref, inner_adjoint_ref)
+                  inner_ref.at[:, 0], inner_ref.at[:, 1])
 
 
 def inner_one(q, p, rate_ref, index_ref, labels_ref, order_ref, adjoint_ref, inner_order_ref, inner_adjoint_ref):
@@ -58,12 +58,11 @@
         prev, cur = cur, nxt
 
 
-def final_kernel(rate_ref, order_ref, adjoint_ref, own_ref, other_ref, inner_order_ref, inner_adjoint_ref,
-                 order_next_ref, adjoint_order_ref):
+def final_kernel(rate_ref, order_ref, adjoint_ref, own_ref, other_ref, inner_ref, order_next_ref, adjoint_order_ref):
     group, rows = order_ref.shape[:2]
     for q in range(group):
         final_one(q, pl.program_id(0) * group + q, rate_ref, order_ref, adjoint_ref, own_ref, other_ref,
-                  inner_order_ref, inner_adjoint_ref, order_next_ref, adjoint_order_ref)
+                  inner_ref.at[:, 0], inner_ref.at[:, 1], order_next_ref, adjoint_order_ref)
 
 
 def final_one(q, p, rate_ref, order_ref, adjoint_ref, own_ref, other_ref, inner_order_ref, inner_adjoint_ref,
@@ -108,18 +107,18 @@
     group = 4
     block = pl.BlockSpec((group, rows, depth, width), lambda p, *_: (p, 0, 0, 0))
     plane = pl.BlockSpec((rows, width), lambda p, *_: (0, 0))
-    inner_order, inner_adjoint = pl.pallas_call(
+    both = pl.BlockSpec((group, 2, rows, depth, width), lambda p, *_: (p, 0, 0, 0, 0))
+    inner = pl.pallas_call(
         inner_kernel,
-        grid_spec=scalars(num_scalar_prefetch=2, grid=(count // group,), in_specs=[plane, block, block], out_specs=[block, block]),
-        out_shape=[jax.ShapeDtypeStruct(order_field.shape, jnp.float32)] * 2,
+        grid_spec=scalars(num_scalar_prefetch=2, grid=(count // group,), in_specs=[plane, block, block], out_specs=both),
+        out_shape=jax.ShapeDtypeStruct((count, 2, rows, depth, width), jnp.float32),
     )(mobility, indices, labels, order_late, adjoint_late)
     on_chip = pl.BlockSpec(memory_space=pltpu.VMEM)
     order_next, adjoint_order = pl.pallas_call(
         final_kernel,
-        grid_spec=scalars(num_scalar_prefetch=1, grid=(count // group,), in_specs=[block, block, on_chip, on_chip, block, block], out_specs=[block, block]),
+        grid_spec=scalars(num_scalar_prefetch=1, grid=(count // group,), in_specs=[block, block, on_chip, on_chip, both], out_specs=[block, block]),
         out_shape=[jax.ShapeDtypeStruct(order_field.shape, jnp.float32)] * 2,
-    )(mobility, order_field, adjoint_next, *[pltpu.with_memory_space_constraint(x, pltpu.VMEM) for x in (own, other)],
-      inner_order, inner_adjoint)
+    )(mobility, order_field, adjoint_next, *[pltpu.with_memory_space_constraint(x, pltpu.VMEM) for x in (own, other)], inner)
     row = pl.BlockSpec((count, 1, depth, width), lambda s, *_: (0, s * (rows - 1), 0, 0))
     return pl.pallas_call(
         edge_kernel,

time: 47.7 us -> 47.8 us (level)
  no operation moved by 1% of the time
where the time goes in v20:
time: 47.8 us; the launch traced here: 47.6 us
  waiting for transfers between devices  17.3 us (36%)
  Pallas kernels  14.9 us (31%)
  starting transfers between devices  10.4 us (22%)
  other arithmetic  4.29 us (9%)
  between operations  0.67 us (1%)
    ppermute x3, waiting for transfers between devices, shift_along(): lax.ppermute(cells, axis, [(i, (i + step) % count) for i in range(count)])  17.3 us
    ppermute x3, starting transfers between devices, shift_along(): lax.ppermute(cells, axis, [(i, (i + step) % count) for i in range(count)])  10.4 us
    pallas_call x1, Pallas kernels, local(): pl.pallas_call(inner_kernel, grid_spec=scalars(num_scalar_prefetch=2, gri...  6.17 us
    pallas_call x1, Pallas kernels, local(): pl.pallas_call(final_kernel, grid_spec=scalars(num_scalar_prefetch=1, gri...  5.96 us
    reduce_sum x1, other arithmetic, local(): jnp.sum(order_field * order_field, axis=0)  3.01 us
    pallas_call x1, Pallas kernels, local(): pl.pallas_call(edge_kernel, grid_spec=scalars(num_scalar_prefetch=1, grid...  2.75 us
  transfers between devices with their start and end apart: 3, of which 1 were waited for; matrix products, arithmetic and copies ran while one was open for 1% of the time, Pallas kernels for 25%

profile of v20, /device:TPU:64, one launch (start us, length us, event | category | flops | bytes accessed | tf_op | source)
XLA Modules:
  0.0 47.6 jit_solution(1922813514027750873)
XLA Ops:
  0.6 0.7 %broadcast_multiply_fusion = f32[8]{0:T(128)S(1)} fusion(f32[8]{0:T(128)} %rate_ref.5), kind=kLoop, calls=%fused_computation.9 | loop fusion | flops 8 | bytes 64 | tf_op jit(solution)/shard_map/mul | solution.py:98
  1.3 0.0 copy-start
  1.3 0.0 copy-start.1
  1.3 3.0 %multiply_reduce_fusion.1 = (f32[8,64,128]{2,1,0:T(8,128)S(1)}, f32[8,64,128]{2,1,0:T(8,128)S(1)}) fusion(f32[8,8,64,128]{3,2,1,0:T(8,128)} %order_ref.2, f32[8,8,64,128]{3,2,1,0:T(8,128)} %adjoint_ref.2, f32[8]{0:T(128)S(1)} %broadcast_multiply_fusion), kind=kLoop, calls=%fused_computation.1 | loop fusion | flops 2490368 | bytes 4718624 | tf_op jit(solution)/shard_map/reduce_sum | solution.py:99
  4.4 5.5 %collective-permute-start.2 = (f32[2,8,64,128]{3,2,1,0:T(8,128)S(1)}, f32[2,8,64,128]{3,2,1,0:T(8,128)S(1)}, u32[]{:S(2)}, u32[]{:S(2)}) collective-permute-start(f32[2,8,64,128]{3,2,1,0:T(8,128)S(1)} %pad_maximum_fusion.own_ref), channel_id=1, source_target_pairs={{0,1},{1,0},{2,3},{3,2},{4,5},{5,4},{6,7},{7,6},{8,9},{9,8},{10,11... | collective-permute-start | bytes 1572872 | tf_op jit(solution)/shard_map/ppermute | solution.py:11
  9.8 0.0 copy-done
  9.8 0.0 copy-done.1
  9.8 0.1 fusion
  9.9 0.1 fusion.1
  10.0 4.9 %collective-permute-start.1 = (f32[2,8,1,64,128]{4,3,2,1,0:T(8,128)S(1)}, f32[2,8,1,64,128]{4,3,2,1,0:T(8,128)S(1)}, u32[]{:S(2)}, u32[]{:S(2)}) collective-permute-start(f32[2,8,1,64,128]{4,3,2,1,0:T(8,128)S(1)} %get-tuple-element.16), channel_id=1, source_target_pairs={{0,254},{2,0},{4,2},{6,4},{8,6},{10,8},{12,10},{14,12},{16,14},{18... | collective-permute-start | bytes 1572872 | tf_op jit(solution)/shard_map/ppermute | solution.py:11
  14.9 0.0 collective-permute-start
  14.9 0.5 %iota_add_fusion.index_ref = s32[8]{0:T(128)} fusion(s32[]{:T(128)S(6)} %mul.26), kind=kLoop, calls=%fused_computation.8 | loop fusion | flops 8 | bytes 36 | tf_op jit(solution)/shard_map/add | solution.py:96
  15.4 6.2 %shard_map.59.inner_ref = f32[8,2,8,64,128]{4,3,2,1,0:T(8,128)} custom-call(f32[8]{0:T(128)} %rate_ref.5, s32[8]{0:T(128)} %iota_add_fusion.index_ref, s32[8,128]{1,0:T(8,128)} %labels_ref.1, f32[8,8,64,128]{3,2,1,0:T(8,128)} %order_ref.2, f32[8,8,64,128]{3,2,1,0:T(8,128)} %adjoint_ref.2), custom_call_target="tpu_custom_call" | custom-call | tf_op jit(solution)/shard_map/pallas_call | solution.py:111
  21.6 17.3 %collective-permute-done.2.other_ref = f32[2,8,64,128]{3,2,1,0:T(8,128)S(1)} collective-permute-done((f32[2,8,64,128]{3,2,1,0:T(8,128)S(1)}, f32[2,8,64,128]{3,2,1,0:T(8,128)S(1)}, u32[]{:S(2)}, u32[]{:S(2)}) %collective-permute-start.2) | collective-permute-done | bytes 524320 | tf_op jit(solution)/shard_map/ppermute | solution.py:11
  38.9 6.0 %shard_map.60 = (f32[8,8,64,128]{3,2,1,0:T(8,128)}, f32[8,8,64,128]{3,2,1,0:T(8,128)}) custom-call(f32[8]{0:T(128)} %rate_ref.5, f32[8,8,64,128]{3,2,1,0:T(8,128)} %order_ref.2, f32[8,8,64,128]{3,2,1,0:T(8,128)} %adjoint_ref.2, f32[2,8,64,128]{3,2,1,0:T(8,128)S(1)} %pad_maximum_fusion.own_ref, f32[2,8,64,128]{3,2,1,0:T(8,128)S(1)} %collective-permute-done.2.other_ref, ...), custom_call_target="tpu_custom_call" | custom-call | tf_op jit(solution)/shard_map/pallas_call | solution.py:117
  44.9 0.0 collective-permute-done.1.above_ref
  44.9 0.0 collective-permute-done.below_ref
  44.9 2.8 %shard_map.61 = (f32[8,8,64,128]{3,2,1,0:T(8,128)}, f32[8,8,64,128]{3,2,1,0:T(8,128)}) custom-call(f32[8]{0:T(128)} %rate_ref.5, f32[2,8,1,64,128]{4,3,2,1,0:T(8,128)S(1)} %collective-permute-done.below_ref, f32[2,8,1,64,128]{4,3,2,1,0:T(8,128)S(1)} %collective-permute-done.1.above_ref, ...), custom_call_target="tpu_custom_call", output_to_operand_aliasing={{0}: (3, {}), {1}: (4, {})} | custom-call | tf_op jit(solution)/shard_map/pallas_call | solution.py:123
  (1 shorter events, 0.0 us)
Async XLA Ops:
  1.3 8.5 %copy-start = (f32[8,8,64,128]{3,2,1,0:T(8,128)S(1)}, f32[8,8,64,128]{3,2,1,0:T(8,128)}, u32[]{:S(2)}) copy-start(f32[8,8,64,128]{3,2,1,0:T(8,128)} %adjoint_ref.2) | copy-start | bytes 6291460
  1.3 8.5 %copy-start.1 = (f32[8,8,64,128]{3,2,1,0:T(8,128)S(1)}, f32[8,8,64,128]{3,2,1,0:T(8,128)}, u32[]{:S(2)}) copy-start(f32[8,8,64,128]{3,2,1,0:T(8,128)} %order_ref.2) | copy-start | bytes 6291460
  4.4 34.6 %collective-permute-start.2 = (f32[2,8,64,128]{3,2,1,0:T(8,128)S(1)}, f32[2,8,64,128]{3,2,1,0:T(8,128)S(1)}, u32[]{:S(2)}, u32[]{:S(2)}) collective-permute-start(f32[2,8,64,128]{3,2,1,0:T(8,128)S(1)} %pad_maximum_fusion.own_ref), channel_id=1, source_target_pairs={{0,1},{1,0},{2,3},{3,2},{4,5},{5,4},{6,7},{7,6},{8,9},{9,8},{10,11... | collective-permute-start | bytes 1572872 | tf_op jit(solution)/shard_map/ppermute | solution.py:11
  10.0 34.9 %collective-permute-start.1 = (f32[2,8,1,64,128]{4,3,2,1,0:T(8,128)S(1)}, f32[2,8,1,64,128]{4,3,2,1,0:T(8,128)S(1)}, u32[]{:S(2)}, u32[]{:S(2)}) collective-permute-start(f32[2,8,1,64,128]{4,3,2,1,0:T(8,128)S(1)} %get-tuple-element.16), channel_id=1, source_target_pairs={{0,254},{2,0},{4,2},{6,4},{8,6},{10,8},{12,10},{14,12},{16,14},{18... | collective-permute-start | bytes 1572872 | tf_op jit(solution)/shard_map/ppermute | solution.py:11
  14.9 30.0 %collective-permute-start = (f32[2,8,1,64,128]{4,3,2,1,0:T(8,128)S(1)}, f32[2,8,1,64,128]{4,3,2,1,0:T(8,128)S(1)}, u32[]{:S(2)}, u32[]{:S(2)}) collective-permute-start(f32[2,8,1,64,128]{4,3,2,1,0:T(8,128)S(1)} %get-tuple-element.17), channel_id=1, source_target_pairs={{0,2},{2,4},{4,6},{6,8},{8,10},{10,12},{12,14},{14,16},{16,18},{18... | collective-permute-start | bytes 1572872 | tf_op jit(solution)/shard_map/ppermute | solution.py:11

commit v21 on v12

--- a/solution.py
+++ b/solution.py
@@ -96,8 +96,7 @@
     first = lax.axis_index("op") * count
     indices = first + jnp.arange(count, dtype=jnp.int32)
     rates = mobility[:, None, None, None]
-    weighted = 0.1 * rates * adjoint_next
-    own = jnp.stack([jnp.sum(order_field * order_field, axis=0), jnp.sum(order_field * weighted, axis=0)])
+    own = jnp.stack([jnp.sum(order_field * order_field, axis=0), 0.1 * jnp.sum(order_field * (rates * adjoint_next), axis=0)])
     other = shift_along(own, "op", 1)
     pair = jnp.stack([order_field, adjoint_next])
     edges = jnp.concatenate([pair[:, :, :1], pair[:, :, -1:]], axis=2)

time: 47.7 us -> 47.1 us (0.987)
  other arithmetic: 4.29 us -> 3.67 us
    mul x1, other arithmetic: 0.66 us -> 0.03 us  [local(): 0.1 * jnp.sum(order_field * (rates * adjoint_next), axis=0)]
  transfers between devices with their start and end apart: 3 -> 3, of which waited for: 1 -> 1; matrix products, arithmetic and copies ran while one was open for 1% -> 1% of each run, Pallas kernels for 25% -> 26%
where the time goes in v21:
time: 47.1 us; the launch traced here: 47 us
  waiting for transfers between devices  17.3 us (37%)
  Pallas kernels  14.8 us (31%)
  starting transfers between devices  10.4 us (22%)
  other arithmetic  3.67 us (8%)
  between operations  0.68 us (1%)
    ppermute x3, waiting for transfers between devices, shift_along(): lax.ppermute(cells, axis, [(i, (i + step) % count) for i in range(count)])  17.3 us
    ppermute x3, starting transfers between devices, shift_along(): lax.ppermute(cells, axis, [(i, (i + step) % count) for i in range(count)])  10.4 us
    pallas_call x1, Pallas kernels, local(): pl.pallas_call(inner_kernel, grid_spec=scalars(num_scalar_prefetch=2, gri...  6.16 us
    pallas_call x1, Pallas kernels, local(): pl.pallas_call(final_kernel, grid_spec=scalars(num_scalar_prefetch=1, gri...  5.88 us
    reduce_sum x1, other arithmetic, local(): jnp.sum(order_field * order_field, axis=0)  3.02 us
    pallas_call x1, Pallas kernels, local(): pl.pallas_call(edge_kernel, grid_spec=scalars(num_scalar_prefetch=1, grid...  2.75 us
  transfers between devices with their start and end apart: 3, of which 1 were waited for; matrix products, arithmetic and copies ran while one was open for 1% of the time, Pallas kernels for 26%

profile of v21, /device:TPU:64, one launch (start us, length us, event | category | flops | bytes accessed | tf_op | source)
XLA Modules:
  0.0 47.0 jit_solution(6993119588383984746)
XLA Ops:
  0.6 0.0 copy-start
  0.6 0.0 copy-start.1
  0.7 3.0 %multiply_reduce_fusion.1 = (f32[8,64,128]{2,1,0:T(8,128)S(1)}, f32[8,64,128]{2,1,0:T(8,128)S(1)}) fusion(f32[8,8,64,128]{3,2,1,0:T(8,128)} %order_ref.2, f32[8,8,64,128]{3,2,1,0:T(8,128)} %adjoint_ref.2, f32[8]{0:T(128)} %rate_ref.5), kind=kLoop, calls=%fused_computation.1 | loop fusion | flops 2490368 | bytes 4718624 | tf_op jit(solution)/shard_map/reduce_sum | solution.py:99
  3.8 5.5 %collective-permute-start.2 = (f32[2,8,64,128]{3,2,1,0:T(8,128)S(1)}, f32[2,8,64,128]{3,2,1,0:T(8,128)S(1)}, u32[]{:S(2)}, u32[]{:S(2)}) collective-permute-start(f32[2,8,64,128]{3,2,1,0:T(8,128)S(1)} %pad_maximum_fusion.own_ref), channel_id=1, source_target_pairs={{0,1},{1,0},{2,3},{3,2},{4,5},{5,4},{6,7},{7,6},{8,9},{9,8},{10,11... | collective-permute-start | bytes 1572872 | tf_op jit(solution)/shard_map/ppermute | solution.py:11
  9.2 0.0 copy-done
  9.2 0.0 copy-done.1
  9.2 0.1 fusion
  9.3 0.1 fusion.1
  9.4 4.9 %collective-permute-start.1 = (f32[2,8,1,64,128]{4,3,2,1,0:T(8,128)S(1)}, f32[2,8,1,64,128]{4,3,2,1,0:T(8,128)S(1)}, u32[]{:S(2)}, u32[]{:S(2)}) collective-permute-start(f32[2,8,1,64,128]{4,3,2,1,0:T(8,128)S(1)} %get-tuple-element.20), channel_id=1, source_target_pairs={{0,254},{2,0},{4,2},{6,4},{8,6},{10,8},{12,10},{14,12},{16,14},{18... | collective-permute-start | bytes 1572872 | tf_op jit(solution)/shard_map/ppermute | solution.py:11
  14.3 0.0 collective-permute-start
  14.3 0.5 %iota_add_fusion.index_ref = s32[8]{0:T(128)} fusion(s32[]{:T(128)S(6)} %mul.40), kind=kLoop, calls=%fused_computation.9 | loop fusion | flops 8 | bytes 36 | tf_op jit(solution)/shard_map/add | solution.py:97
  14.8 6.2 %shard_map.59 = (f32[8,8,64,128]{3,2,1,0:T(8,128)}, f32[8,8,64,128]{3,2,1,0:T(8,128)}) custom-call(f32[8]{0:T(128)} %rate_ref.5, s32[8]{0:T(128)} %iota_add_fusion.index_ref, s32[8,128]{1,0:T(8,128)} %labels_ref.1, f32[8,8,64,128]{3,2,1,0:T(8,128)} %order_ref.2, f32[8,8,64,128]{3,2,1,0:T(8,128)} %adjoint_ref.2), custom_call_target="tpu_custom_call" | custom-call | tf_op jit(solution)/shard_map/pallas_call | solution.py:110
  21.0 17.3 %collective-permute-done.2.other_ref = f32[2,8,64,128]{3,2,1,0:T(8,128)S(1)} collective-permute-done((f32[2,8,64,128]{3,2,1,0:T(8,128)S(1)}, f32[2,8,64,128]{3,2,1,0:T(8,128)S(1)}, u32[]{:S(2)}, u32[]{:S(2)}) %collective-permute-start.2) | collective-permute-done | bytes 524320 | tf_op jit(solution)/shard_map/ppermute | solution.py:11
  38.3 5.9 %shard_map.60 = (f32[8,8,64,128]{3,2,1,0:T(8,128)}, f32[8,8,64,128]{3,2,1,0:T(8,128)}) custom-call(f32[8]{0:T(128)} %rate_ref.5, f32[8,8,64,128]{3,2,1,0:T(8,128)} %order_ref.2, f32[8,8,64,128]{3,2,1,0:T(8,128)} %adjoint_ref.2, f32[2,8,64,128]{3,2,1,0:T(8,128)S(1)} %pad_maximum_fusion.own_ref, f32[2,8,64,128]{3,2,1,0:T(8,128)S(1)} %collective-permute-done.2.other_ref, ...), custom_call_target="tpu_custom_call" | custom-call | tf_op jit(solution)/shard_map/pallas_call | solution.py:116
  44.2 0.0 collective-permute-done.1.above_ref
  44.2 0.0 collective-permute-done.below_ref
  44.2 2.8 %shard_map.61 = (f32[8,8,64,128]{3,2,1,0:T(8,128)}, f32[8,8,64,128]{3,2,1,0:T(8,128)}) custom-call(f32[8]{0:T(128)} %rate_ref.5, f32[2,8,1,64,128]{4,3,2,1,0:T(8,128)S(1)} %collective-permute-done.below_ref, f32[2,8,1,64,128]{4,3,2,1,0:T(8,128)S(1)} %collective-permute-done.1.above_ref, ...), custom_call_target="tpu_custom_call", output_to_operand_aliasing={{0}: (3, {}), {1}: (4, {})} | custom-call | tf_op jit(solution)/shard_map/pallas_call | solution.py:123
  (2 shorter events, 0.1 us)
Async XLA Ops:
  0.6 8.6 %copy-start = (f32[8,8,64,128]{3,2,1,0:T(8,128)S(1)}, f32[8,8,64,128]{3,2,1,0:T(8,128)}, u32[]{:S(2)}) copy-start(f32[8,8,64,128]{3,2,1,0:T(8,128)} %adjoint_ref.2) | copy-start | bytes 6291460
  0.6 8.6 %copy-start.1 = (f32[8,8,64,128]{3,2,1,0:T(8,128)S(1)}, f32[8,8,64,128]{3,2,1,0:T(8,128)}, u32[]{:S(2)}) copy-start(f32[8,8,64,128]{3,2,1,0:T(8,128)} %order_ref.2) | copy-start | bytes 6291460
  3.8 34.6 %collective-permute-start.2 = (f32[2,8,64,128]{3,2,1,0:T(8,128)S(1)}, f32[2,8,64,128]{3,2,1,0:T(8,128)S(1)}, u32[]{:S(2)}, u32[]{:S(2)}) collective-permute-start(f32[2,8,64,128]{3,2,1,0:T(8,128)S(1)} %pad_maximum_fusion.own_ref), channel_id=1, source_target_pairs={{0,1},{1,0},{2,3},{3,2},{4,5},{5,4},{6,7},{7,6},{8,9},{9,8},{10,11... | collective-permute-start | bytes 1572872 | tf_op jit(solution)/shard_map/ppermute | solution.py:11
  9.4 34.8 %collective-permute-start.1 = (f32[2,8,1,64,128]{4,3,2,1,0:T(8,128)S(1)}, f32[2,8,1,64,128]{4,3,2,1,0:T(8,128)S(1)}, u32[]{:S(2)}, u32[]{:S(2)}) collective-permute-start(f32[2,8,1,64,128]{4,3,2,1,0:T(8,128)S(1)} %get-tuple-element.20), channel_id=1, source_target_pairs={{0,254},{2,0},{4,2},{6,4},{8,6},{10,8},{12,10},{14,12},{16,14},{18... | collective-permute-start | bytes 1572872 | tf_op jit(solution)/shard_map/ppermute | solution.py:11
  14.3 29.9 %collective-permute-start = (f32[2,8,1,64,128]{4,3,2,1,0:T(8,128)S(1)}, f32[2,8,1,64,128]{4,3,2,1,0:T(8,128)S(1)}, u32[]{:S(2)}, u32[]{:S(2)}) collective-permute-start(f32[2,8,1,64,128]{4,3,2,1,0:T(8,128)S(1)} %get-tuple-element.21), channel_id=1, source_target_pairs={{0,2},{2,4},{4,6},{6,8},{8,10},{10,12},{12,14},{14,16},{16,18},{18... | collective-permute-start | bytes 1572872 | tf_op jit(solution)/shard_map/ppermute | solution.py:11

commit v22 on v20

--- a/solution.py
+++ b/solution.py
@@ -95,8 +95,7 @@
     first = lax.axis_index("op") * count
     indices = first + jnp.arange(count, dtype=jnp.int32)
     rates = mobility[:, None, None, None]
-    weighted = 0.1 * rates * adjoint_next
-    own = jnp.stack([jnp.sum(order_field * order_field, axis=0), jnp.sum(order_field * weighted, axis=0)])
+    own = jnp.stack([jnp.sum(order_field * order_field, axis=0), 0.1 * jnp.sum(order_field * (rates * adjoint_next), axis=0)])
     other = shift_along(own, "op", 1)
     pair = jnp.stack([order_field, adjoint_next])
     edges = jnp.concatenate([pair[:, :, :1], pair[:, :, -1:]], axis=2)

time: 47.8 us -> 47.2 us (0.987)
  other arithmetic: 4.29 us -> 3.67 us
    mul x1, other arithmetic: 0.66 us -> 0.03 us  [local(): 0.1 * jnp.sum(order_field * (rates * adjoint_next), axis=0)]
  transfers between devices with their start and end apart: 3 -> 3, of which waited for: 1 -> 1; matrix products, arithmetic and copies ran while one was open for 1% -> 1% of each run, Pallas kernels for 25% -> 26%
where the time goes in v22:
time: 47.2 us; the launch traced here: 47.1 us
  waiting for transfers between devices  17.3 us (37%)
  Pallas kernels  14.9 us (32%)
  starting transfers between devices  10.4 us (22%)
  other arithmetic  3.67 us (8%)
  between operations  0.68 us (1%)
    ppermute x3, waiting for transfers between devices, shift_along(): lax.ppermute(cells, axis, [(i, (i + step) % count) for i in range(count)])  17.3 us
    ppermute x3, starting transfers between devices, shift_along(): lax.ppermute(cells, axis, [(i, (i + step) % count) for i in range(count)])  10.4 us
    pallas_call x1, Pallas kernels, local(): pl.pallas_call(inner_kernel, grid_spec=scalars(num_scalar_prefetch=2, gri...  6.17 us
    pallas_call x1, Pallas kernels, local(): pl.pallas_call(final_kernel, grid_spec=scalars(num_scalar_prefetch=1, gri...  5.96 us
    reduce_sum x1, other arithmetic, local(): jnp.sum(order_field * order_field, axis=0)  3.02 us
    pallas_call x1, Pallas kernels, local(): pl.pallas_call(edge_kernel, grid_spec=scalars(num_scalar_prefetch=1, grid...  2.75 us
  transfers between devices with their start and end apart: 3, of which 1 were waited for; matrix products, arithmetic and copies ran while one was open for 1% of the time, Pallas kernels for 26%

profile of v22, /device:TPU:64, one launch (start us, length us, event | category | flops | bytes accessed | tf_op | source)
XLA Modules:
  0.0 47.1 jit_solution(12362736984108167881)
XLA Ops:
  0.6 0.0 copy-start
  0.6 0.0 copy-start.1
  0.7 3.0 %multiply_reduce_fusion.1 = (f32[8,64,128]{2,1,0:T(8,128)S(1)}, f32[8,64,128]{2,1,0:T(8,128)S(1)}) fusion(f32[8,8,64,128]{3,2,1,0:T(8,128)} %order_ref.2, f32[8,8,64,128]{3,2,1,0:T(8,128)} %adjoint_ref.2, f32[8]{0:T(128)} %rate_ref.5), kind=kLoop, calls=%fused_computation.1 | loop fusion | flops 2490368 | bytes 4718624 | tf_op jit(solution)/shard_map/reduce_sum | solution.py:98
  3.8 5.5 %collective-permute-start.2 = (f32[2,8,64,128]{3,2,1,0:T(8,128)S(1)}, f32[2,8,64,128]{3,2,1,0:T(8,128)S(1)}, u32[]{:S(2)}, u32[]{:S(2)}) collective-permute-start(f32[2,8,64,128]{3,2,1,0:T(8,128)S(1)} %pad_maximum_fusion.own_ref), channel_id=1, source_target_pairs={{0,1},{1,0},{2,3},{3,2},{4,5},{5,4},{6,7},{7,6},{8,9},{9,8},{10,11... | collective-permute-start | bytes 1572872 | tf_op jit(solution)/shard_map/ppermute | solution.py:11
  9.2 0.0 copy-done
  9.2 0.0 copy-done.1
  9.2 0.1 fusion
  9.3 0.1 fusion.1
  9.4 4.9 %collective-permute-start.1 = (f32[2,8,1,64,128]{4,3,2,1,0:T(8,128)S(1)}, f32[2,8,1,64,128]{4,3,2,1,0:T(8,128)S(1)}, u32[]{:S(2)}, u32[]{:S(2)}) collective-permute-start(f32[2,8,1,64,128]{4,3,2,1,0:T(8,128)S(1)} %get-tuple-element.16), channel_id=1, source_target_pairs={{0,254},{2,0},{4,2},{6,4},{8,6},{10,8},{12,10},{14,12},{16,14},{18... | collective-permute-start | bytes 1572872 | tf_op jit(solution)/shard_map/ppermute | solution.py:11
  14.3 0.0 collective-permute-start
  14.3 0.5 %iota_add_fusion.index_ref = s32[8]{0:T(128)} fusion(s32[]{:T(128)S(6)} %mul.40), kind=kLoop, calls=%fused_computation.9 | loop fusion | flops 8 | bytes 36 | tf_op jit(solution)/shard_map/add | solution.py:96
  14.8 6.2 %shard_map.59.inner_ref = f32[8,2,8,64,128]{4,3,2,1,0:T(8,128)} custom-call(f32[8]{0:T(128)} %rate_ref.5, s32[8]{0:T(128)} %iota_add_fusion.index_ref, s32[8,128]{1,0:T(8,128)} %labels_ref.1, f32[8,8,64,128]{3,2,1,0:T(8,128)} %order_ref.2, f32[8,8,64,128]{3,2,1,0:T(8,128)} %adjoint_ref.2), custom_call_target="tpu_custom_call" | custom-call | tf_op jit(solution)/shard_map/pallas_call | solution.py:110
  21.0 17.3 %collective-permute-done.2.other_ref = f32[2,8,64,128]{3,2,1,0:T(8,128)S(1)} collective-permute-done((f32[2,8,64,128]{3,2,1,0:T(8,128)S(1)}, f32[2,8,64,128]{3,2,1,0:T(8,128)S(1)}, u32[]{:S(2)}, u32[]{:S(2)}) %collective-permute-start.2) | collective-permute-done | bytes 524320 | tf_op jit(solution)/shard_map/ppermute | solution.py:11
  38.3 6.0 %shard_map.60 = (f32[8,8,64,128]{3,2,1,0:T(8,128)}, f32[8,8,64,128]{3,2,1,0:T(8,128)}) custom-call(f32[8]{0:T(128)} %rate_ref.5, f32[8,8,64,128]{3,2,1,0:T(8,128)} %order_ref.2, f32[8,8,64,128]{3,2,1,0:T(8,128)} %adjoint_ref.2, f32[2,8,64,128]{3,2,1,0:T(8,128)S(1)} %pad_maximum_fusion.own_ref, f32[2,8,64,128]{3,2,1,0:T(8,128)S(1)} %collective-permute-done.2.other_ref, ...), custom_call_target="tpu_custom_call" | custom-call | tf_op jit(solution)/shard_map/pallas_call | solution.py:116
  44.3 0.0 collective-permute-done.1.above_ref
  44.3 0.0 collective-permute-done.below_ref
  44.3 2.8 %shard_map.61 = (f32[8,8,64,128]{3,2,1,0:T(8,128)}, f32[8,8,64,128]{3,2,1,0:T(8,128)}) custom-call(f32[8]{0:T(128)} %rate_ref.5, f32[2,8,1,64,128]{4,3,2,1,0:T(8,128)S(1)} %collective-permute-done.below_ref, f32[2,8,1,64,128]{4,3,2,1,0:T(8,128)S(1)} %collective-permute-done.1.above_ref, ...), custom_call_target="tpu_custom_call", output_to_operand_aliasing={{0}: (3, {}), {1}: (4, {})} | custom-call | tf_op jit(solution)/shard_map/pallas_call | solution.py:122
  (2 shorter events, 0.1 us)
Async XLA Ops:
  0.6 8.6 %copy-start = (f32[8,8,64,128]{3,2,1,0:T(8,128)S(1)}, f32[8,8,64,128]{3,2,1,0:T(8,128)}, u32[]{:S(2)}) copy-start(f32[8,8,64,128]{3,2,1,0:T(8,128)} %adjoint_ref.2) | copy-start | bytes 6291460
  0.6 8.6 %copy-start.1 = (f32[8,8,64,128]{3,2,1,0:T(8,128)S(1)}, f32[8,8,64,128]{3,2,1,0:T(8,128)}, u32[]{:S(2)}) copy-start(f32[8,8,64,128]{3,2,1,0:T(8,128)} %order_ref.2) | copy-start | bytes 6291460
  3.8 34.6 %collective-permute-start.2 = (f32[2,8,64,128]{3,2,1,0:T(8,128)S(1)}, f32[2,8,64,128]{3,2,1,0:T(8,128)S(1)}, u32[]{:S(2)}, u32[]{:S(2)}) collective-permute-start(f32[2,8,64,128]{3,2,1,0:T(8,128)S(1)} %pad_maximum_fusion.own_ref), channel_id=1, source_target_pairs={{0,1},{1,0},{2,3},{3,2},{4,5},{5,4},{6,7},{7,6},{8,9},{9,8},{10,11... | collective-permute-start | bytes 1572872 | tf_op jit(solution)/shard_map/ppermute | solution.py:11
  9.4 34.9 %collective-permute-start.1 = (f32[2,8,1,64,128]{4,3,2,1,0:T(8,128)S(1)}, f32[2,8,1,64,128]{4,3,2,1,0:T(8,128)S(1)}, u32[]{:S(2)}, u32[]{:S(2)}) collective-permute-start(f32[2,8,1,64,128]{4,3,2,1,0:T(8,128)S(1)} %get-tuple-element.16), channel_id=1, source_target_pairs={{0,254},{2,0},{4,2},{6,4},{8,6},{10,8},{12,10},{14,12},{16,14},{18... | collective-permute-start | bytes 1572872 | tf_op jit(solution)/shard_map/ppermute | solution.py:11
  14.3 30.0 %collective-permute-start = (f32[2,8,1,64,128]{4,3,2,1,0:T(8,128)S(1)}, f32[2,8,1,64,128]{4,3,2,1,0:T(8,128)S(1)}, u32[]{:S(2)}, u32[]{:S(2)}) collective-permute-start(f32[2,8,1,64,128]{4,3,2,1,0:T(8,128)S(1)} %get-tuple-element.17), channel_id=1, source_target_pairs={{0,2},{2,4},{4,6},{6,8},{8,10},{10,12},{12,14},{14,16},{16,18},{18... | collective-permute-start | bytes 1572872 | tf_op jit(solution)/shard_map/ppermute | solution.py:11
